TPU v7x, 128 devices: a whole 4x4x4 slice. The times are simulated.
128 devices in a mesh: req: 32 (over x, y, core), tp: 4 (over z).
Axes of the slice: x: 4, y: 4, z: 4, core: 2. Of those that a mesh axis runs over, the one named last changes fastest.
Arguments:
- stream: bfloat16 [64, 64, 3584], P('req'), may hold values from -40 to 40
- queries: bfloat16 [64, 64, 3584], P('req', None, 'tp'), may hold values from -4 to 4
- key_new: bfloat16 [64, 64, 3584], P('req', None, 'tp'), may hold values from -18 to 18
- value_new: bfloat16 [64, 64, 3584], P('req', None, 'tp'), may hold values from -6 to 6
- cache_key: bfloat16 [64, 1024, 3584], P('req', None, 'tp'), may hold values from -5 to 5
- cache_value: bfloat16 [64, 1024, 3584], P('req', None, 'tp'), may hold values from -6 to 6
- cache_length: int32 [64], P('req'), may hold values from 64 to 1024, as said below
- parents: int32 [64, 64], P('req'), may hold values from -1 to 62, as said below
- accept: int32 [64, 8, 64], P('req'), may hold values from 0 to 1, as said below
- out_weight: bfloat16 [3584, 3584], P('tp'), may hold values from -0.75 to 0.75
- norm_gain: float32 [3584], replicated, may hold values from 0.1 to 1.9
- head_weight: bfloat16 [32000, 3584], P('req'), may hold values from -1 to 1
- candidate: int32 [64, 64], replicated, may hold values from 0 to 31999
- dealing: int32 [64], replicated, may hold values from 0 to 63, each once
Outputs:
- target_logprob: float32 [64, 64], P('req')
- accepted_state: bfloat16 [64, 8, 3584], P('req', None, 'tp')
Inputs may be any that keep to these rules, and one draw needn't show every extreme that they name: `cache_length`: every cache holds at least 64 live positions; in every draw some slot's cache is full. `parents`: node 0 is the root with parent -1; node t > 0 lies at depth (t - 1) // 9 + 1 and its parent lies one depth above it. `accept`: row a of a slot's matrix is one-hot on the node at depth a of the accepted path, which runs from the root down the slot's tree to some node; rows past the path's end are zero; in every draw some path ends at the deepest level.
All inputs are finite; a program needn't handle non-finite values.
Results may differ from a plain program's by a relative error of at most 0.012.
Values may be sent and summed in bfloat16 or wider, within the bound.
No kernel may reach another device: no remote copies, remote signals or barrier semaphores. Data moves between devices by JAX's collectives and lax.ppermute only.
A program may use at most 192 MiB of HBM per device.

v0:
```python
import jax
import jax.numpy as jnp
from jax import lax
from jax.sharding import PartitionSpec as P

HD = 224
ACC = 8


EPS = 1e-05
HIGH = lax.Precision.HIGHEST
block_limit = 512


def combined_all(value, axis, join):
    pieces = jax.tree.map(lambda part: lax.all_gather(part, axis), value)
    head = jax.tree.map(lambda part: part[0], pieces)
    tail = jax.tree.map(lambda part: part[1:], pieces)
    subtotal, _ = lax.scan(lambda subtotal, share: (join(subtotal, share), None), head, tail)
    return subtotal


def ancestry(parents):
    node_count = parents.shape[-1]
    node_ids = jnp.arange(node_count, dtype=jnp.int32)
    stride_map = (parents[..., :, None] == node_ids).astype(jnp.float32)
    reached = jnp.broadcast_to(jnp.eye(node_count, dtype=jnp.float32), stride_map.shape) > 0.5
    for doubling in range((ACC - 1).bit_length()):
        further = lax.optimization_barrier(
            jnp.einsum("rtk,rku->rtu", reached.astype(jnp.float32), stride_map, precision=HIGH)
        )
        reached = jnp.logical_or(reached, further > 0.5)
        stride_map = jnp.einsum("rtk,rku->rtu", stride_map, stride_map, precision=HIGH)
    return reached


def combine_stats(earlier, later):
    joint_max = jnp.maximum(earlier[0], later[0])
    joint_sum = earlier[1] * jnp.exp(earlier[0] - joint_max) + later[1] * jnp.exp(
        later[0] - joint_max
    )
    return (joint_max, joint_sum, earlier[2] + later[2])


def vocab_stats(logits, vocab_ids, wanted, along):
    row_max = jnp.max(logits, axis=along)
    row_sum = jnp.sum(jnp.exp(logits - jnp.expand_dims(row_max, along)), axis=along)
    matches = jnp.expand_dims(vocab_ids, 1 - along) == jnp.expand_dims(wanted, along)
    picked = jnp.sum(jnp.where(matches, logits, 0.0), axis=along)
    return (row_max, row_sum, picked)


def local(
    stream,
    queries,
    key_new,
    value_new,
    cache_key,
    cache_value,
    cache_length,
    parents,
    accept,
    out_weight,
    norm_gain,
    head_weight,
    candidate,
    dealing,
):
    slots, tree_size, qwidth = queries.shape
    model_width = stream.shape[2]
    heads_loc = qwidth // HD
    n_tp = lax.axis_size("tp")
    n_req = lax.axis_size("req")
    tp_id = lax.axis_index("tp")
    req_id = lax.axis_index("req")
    score_scale = HD ** (-0.5)
    query_rows = queries.reshape(slots, tree_size, heads_loc, HD)
    tree_keys = key_new.reshape(slots, tree_size, heads_loc, HD)
    tree_values = value_new.reshape(slots, tree_size, heads_loc, HD)
    visible = ancestry(parents)
    tree_scores = (
        jnp.einsum("rthd,rkhd->rhtk", query_rows, tree_keys, preferred_element_type=jnp.float32)
        * score_scale
    )
    tree_scores = jnp.where(visible[:, None], tree_scores, -jnp.inf)
    running_max = jnp.max(tree_scores, axis=3)
    weights = jnp.exp(tree_scores - running_max[..., None])
    running_sum = jnp.sum(weights, axis=3)
    running_out = jnp.einsum(
        "rhtk,rkhd->rhtd",
        weights.astype(jnp.bfloat16),
        tree_values,
        preferred_element_type=jnp.float32,
    )
    cache_cap = cache_key.shape[1]
    block_rows = min(block_limit, cache_cap)
    block_count = (jnp.max(cache_length) + block_rows - 1) // block_rows

    def visit_block(block_index, folded):
        old_max, old_sum, old_out = folded
        offset = block_index * block_rows
        past_keys = lax.dynamic_slice_in_dim(cache_key, offset, block_rows, 1).reshape(
            slots, block_rows, heads_loc, HD
        )
        past_values = lax.dynamic_slice_in_dim(cache_value, offset, block_rows, 1).reshape(
            slots, block_rows, heads_loc, HD
        )
        scores = (
            jnp.einsum("rthd,rkhd->rhtk", query_rows, past_keys, preferred_element_type=jnp.float32)
            * score_scale
        )
        live_mask = (offset + jnp.arange(block_rows, dtype=jnp.int32))[None, :] < cache_length[
            :, None
        ]
        scores = jnp.where(live_mask[:, None, None, :], scores, -jnp.inf)
        new_max = jnp.maximum(old_max, jnp.max(scores, axis=3))
        shrink = jnp.exp(old_max - new_max)
        block_weights = jnp.exp(scores - new_max[..., None])
        new_sum = old_sum * shrink + jnp.sum(block_weights, axis=3)
        contribution = lax.optimization_barrier(
            jnp.einsum(
                "rhtk,rkhd->rhtd",
                block_weights.astype(jnp.bfloat16),
                past_values,
                preferred_element_type=jnp.float32,
            )
        )
        new_out = old_out * shrink[..., None] + contribution
        return (new_max, new_sum, new_out)

    running_max, running_sum, running_out = lax.fori_loop(
        0, block_count, visit_block, (running_max, running_sum, running_out)
    )
    attention = (running_out / running_sum[..., None]).astype(jnp.bfloat16)
    attention_rows = attention.transpose(0, 2, 1, 3).reshape(slots * tree_size, qwidth)
    flat_stream = stream.reshape(slots * tree_size, model_width)
    rows_all = slots * tree_size
    quarter = rows_all // n_tp
    dslice = model_width // n_tp
    partial_out = jnp.dot(attention_rows, out_weight, preferred_element_type=jnp.float32)
    summed = lax.psum_scatter(
        partial_out.astype(jnp.bfloat16), "tp", scatter_dimension=1, tiled=True
    ).astype(jnp.float32)
    own_stream = lax.dynamic_slice_in_dim(flat_stream, tp_id * dslice, dslice, 1)
    post_rows = (own_stream.astype(jnp.float32) + summed).astype(jnp.bfloat16)
    post_float = post_rows.astype(jnp.float32)
    square = jnp.sum(post_float * post_float, axis=1)
    energy = lax.psum(square, "tp")
    inverse = lax.rsqrt(energy / model_width + EPS)
    part_gain = lax.dynamic_slice_in_dim(norm_gain, tp_id * dslice, dslice, 0)
    normed_slice = (post_float * inverse[:, None] * part_gain[None, :]).astype(jnp.bfloat16)
    compact = jnp.einsum(
        "sat,std->sad",
        accept.astype(jnp.bfloat16),
        post_rows.reshape(slots, tree_size, dslice),
        preferred_element_type=jnp.float32,
    ).astype(jnp.bfloat16)
    normed = lax.all_to_all(normed_slice, "tp", split_axis=0, concat_axis=1, tiled=True)
    vocab_loc = head_weight.shape[0]
    wanted_rows = lax.dynamic_slice_in_dim(
        candidate.reshape(n_req, rows_all), tp_id * quarter, quarter, 1
    ).reshape(-1)
    vocab_ids = req_id * vocab_loc + jnp.arange(vocab_loc, dtype=jnp.int32)
    logits = lax.dot_general(
        lax.all_gather(normed, "req", axis=0, tiled=True),
        head_weight,
        (((1,), (1,)), ((), ())),
        preferred_element_type=jnp.float32,
    )
    found_stats = vocab_stats(logits, vocab_ids, wanted_rows, 1)
    local_stats = tuple((after_part for after_part in found_stats))
    merged = combined_all((local_stats[0], local_stats[1], local_stats[2]), "req", combine_stats)
    all_stats = (
        lax.all_gather(merged[0], "tp", axis=0, tiled=True),
        lax.all_gather(merged[1], "tp", axis=0, tiled=True),
        lax.all_gather(merged[2], "tp", axis=0, tiled=True),
    )
    row_max, row_sum, picked = tuple(
        (
            member.reshape(n_tp, n_req, quarter).transpose(1, 0, 2).reshape(-1)
            for member in all_stats
        )
    )
    logprob = (picked - row_max - jnp.log(row_sum)).reshape(-1, tree_size)
    own_requests = req_id * slots + jnp.arange(slots, dtype=jnp.int32)
    selector = dealing[None, :] == own_requests[:, None]
    target_logprob = jnp.dot(selector.astype(jnp.float32), logprob, precision=HIGH)
    home_states = lax.all_gather(compact, "req", axis=0, tiled=True)
    accepted_state = jnp.einsum(
        "ks,sad->kad",
        selector.astype(jnp.bfloat16),
        home_states,
        preferred_element_type=jnp.float32,
    ).astype(jnp.bfloat16)
    return (target_logprob, accepted_state)


def solution(mesh):
    placed = (
        P("req", None, None),
        P("req", None, "tp"),
        P("req", None, "tp"),
        P("req", None, "tp"),
        P("req", None, "tp"),
        P("req", None, "tp"),
        P("req"),
        P("req", None),
        P("req", None, None),
        P("tp", None),
        P(),
        P("req", None),
        P(),
        P(),
    )
    return jax.shard_map(
        local,
        mesh=mesh,
        in_specs=placed,
        out_specs=(P("req", None), P("req", None, "tp")),
        check_vma=False,
    )
```

profile of v0, /device:TPU:0, one launch (start us, length us, event | category | flops | bytes accessed | tf_op | source)
XLA Modules:
  0.0 275.7 jit_solution(6451548967636028759)
XLA Ops:
  7.2 1.4 reduce_max.37
  9.3 1.0 fusion.21
  10.3 0.2 fusion.38
  10.5 0.9 fusion.22
  11.4 0.2 fusion.37
  11.6 0.2 fusion.39
  11.9 1.2 reshape.97
  13.1 0.7 copy.48
  13.9 1.2 reshape.98
  15.1 1.2 reshape.99
  16.3 0.2 fusion.35
  16.6 0.3 fusion.13
  16.9 12.5 %while.28 = (s32[]{:T(128)}, f32[2,4,64]{2,1,0:T(4,128)S(1)}, f32[2,4,64]{2,1,0:T(4,128)S(1)}, f32[2,4,64,224]{3,2,1,0:T(8,128)S(1)}, s32[]{:T(128)}, /*index=5*...) while((s32[]{:T(128)}, f32[2,4,64]{2,1,0:T(4,128)S(1)}, ...), condition=%wide.region_6.7_spmd, body=%wide.region_3.6_spmd.sunk | while | flops 236947968 | bytes 23599292 | solution.py:131
  17.0 4.1 %constant_dynamic-slice_fusion.9 = (bf16[2,512,896]{2,1,0:T(8,128)(2,1)}, bf16[2,512,896]{2,1,0:T(8,128)(2,1)}) fusion(bf16[2,1024,896]{2,1,0:T(8,128)(2,1)} %get-tuple-element.346, s32[]{:T(128)S(6)} %select_n.42, bf16[2,1024,896]{2,1,0:T(8,128)(2,1)} %get-tuple-element.344), kind=kLoop, calls=%fused_computation.13.clone.1 | loop fusion | bytes 7340036 | tf_op jit(solution)/shard_map/while/body/dynamic_slice | solution.py:105
  21.1 2.7 copy.80
  23.9 1.5 fusion.66
  25.4 0.3 fusion.67
  25.8 2.8 copy.81
  28.5 0.7 fusion.68
  29.2 0.2 multiply_add_fusion.7
  29.4 0.1 fusion.16
  29.6 0.2 copy.55
  29.8 0.2 reshape.100
  30.0 4.0 %convolution_convert_fusion = bf16[128,3584]{1,0:T(8,128)(2,1)S(1)} fusion(bf16[128,896]{1,0:T(8,128)(2,1)S(1)} %reshape.100, bf16[896,3584]{1,0:T(8,128)(2,1)} %param.27), kind=kOutput, calls=%fused_computation.19 | convolution fusion | flops 822542336 | bytes 7569408 | tf_op jit(solution)/shard_map/dot_general | solution.py:140
  34.0 1.3 copy.61
  35.4 0.8 dynamic_slice.26
  36.1 37.5 %reduce-scatter.4.cloned.1.call-done = bf16[896,128]{1,0:T(8,128)(2,1)} async-done(((bf16[3584,128]{1,0:T(8,128)(2,1)}), bf16[896,128]{1,0:T(8,128)(2,1)}) %reduce-scatter.4.cloned.1.call-update) | async-done | bytes 229392
  73.6 1.1 copy.62
  74.7 1.1 fusion.10
  75.8 8.0 %psum.7 = f32[128]{0:T(128)S(1)} all-reduce(f32[128]{0:T(128)S(1)} %get-tuple-element.177), channel_id=1, replica_groups=mesh['req'=32,'tp'=4] {'tp'}, use_global_device_ids=true, to_apply=%region_9.10 | all-reduce | flops 128 | bytes 1024 | tf_op jit(solution)/shard_map/psum | solution.py:148
  83.8 0.1 fusion.12
  84.0 9.3 %all_to_all.19 = bf16[4,32,896]{2,1,0:T(8,128)(2,1)S(1)} all-to-all(bf16[4,32,896]{2,1,0:T(8,128)(2,1)S(1)} %bitcast.79), channel_id=1, replica_groups=mesh['req'=32,'tp'=4] {'tp'}, dimensions={0} | all-to-all | bytes 458752 | tf_op jit(solution)/shard_map/all_to_all | solution.py:158
  93.3 0.7 copy.65
  94.3 0.1 fusion.8
  94.4 25.4 %all_gather.43 = bf16[64,8,896]{2,1,0:T(8,128)(2,1)S(1)} all-gather(bf16[2,8,896]{2,1,0:T(8,128)(2,1)S(1)} %fusion.8), channel_id=1, replica_groups=mesh['req'=32,'tp'=4] {'req'}, dimensions={0}, use_global_device_ids=true | all-gather | bytes 946176 | tf_op jit(solution)/shard_map/all_gather | solution.py:188
  119.8 0.3 convolution_convert_fusion.1
  120.1 0.6 copy.59
  120.8 23.6 %all-gather.5.cloned.1.call-done = bf16[1024,3584]{1,0:T(8,128)(2,1)} async-done(((bf16[32,3584]{1,0:T(8,128)(2,1)}), bf16[1024,3584]{1,0:T(8,128)(2,1)}) %all-gather.5.cloned.1.call-update) | async-done | bytes 7340048 | tf_op jit(solution)/shard_map/all_gather | solution.py:165
  144.3 12.1 %fusion.36 = (f32[1024]{0:T(1024)S(1)}, f32[1024,1000]{0,1:T(8,128)S(1)}) fusion(bf16[1024,3584]{1,0:T(8,128)(2,1)} %all-gather.5.cloned.1.call-done, bf16[1000,3584]{1,0:T(8,128)(2,1)} %param.29), kind=kOutput, calls=%fused_computation.70 | convolution fusion | flops 7341054976 | bytes 18608128 | tf_op jit(solution)/shard_map/dot_general | solution.py:164
  156.4 1.4 select_reduce_fusion
  157.8 24.1 %all-gather.2 = f32[32768]{0:T(1024)S(1)} all-gather(f32[1024]{0:T(1024)S(1)} %get-tuple-element.139), channel_id=4, replica_groups=mesh['req'=32,'tp'=4] {'req'}, dimensions={0}, use_global_device_ids=true | all-gather | bytes 135168 | tf_op jit(solution)/shard_map/all_gather | solution.py:16
  181.9 22.7 %all-gather = f32[32768]{0:T(1024)S(1)} all-gather(f32[1024]{0:T(1024)S(1)} %get-tuple-element.187), channel_id=2, replica_groups=mesh['req'=32,'tp'=4] {'req'}, dimensions={0}, use_global_device_ids=true | all-gather | bytes 135168 | tf_op jit(solution)/shard_map/all_gather | solution.py:16
  204.6 23.8 %all-gather.1 = f32[32768]{0:T(1024)S(1)} all-gather(f32[1024]{0:T(1024)S(1)} %get-tuple-element.140), channel_id=3, replica_groups=mesh['req'=32,'tp'=4] {'req'}, dimensions={0}, use_global_device_ids=true | all-gather | bytes 135168 | tf_op jit(solution)/shard_map/all_gather | solution.py:16
  228.5 2.8 %while.29 = (s32[]{:T(128)}, f32[1024]{0:T(1024)S(1)}, f32[1024]{0:T(1024)S(1)}, f32[1024]{0:T(1024)S(1)}, f32[31,1024]{1,0:T(8,128)S(1)}, /*index=5*/f32[31,1024]{1,0:T(8,128)S(1)}, f32[31,1024]{1,0:T(8,128)S(1)}, s32[]{:T(128)}) while((s32[]{:T(128)}, f32[1024]{0:T(1024)S(1)}, f32[1024]{0:T(1024)S(1)}, f32[1024]{0:T(1024)S(1)}, ...), condition=%wide.region_14.15_spmd, body=%wide.region_13.14_spmd.sunk | while | flops 7170 | bytes 61541 | solution.py:19
  231.3 12.5 %all_gather.40 = f32[4096]{0:T(1024)S(1)} all-gather(f32[1024]{0:T(1024)S(1)} %get-tuple-element.92), channel_id=1, replica_groups=mesh['req'=32,'tp'=4] {'tp'}, dimensions={0}, use_global_device_ids=true | all-gather | bytes 20480 | tf_op jit(solution)/shard_map/all_gather | solution.py:176
  243.8 12.0 %all_gather.41 = f32[4096]{0:T(1024)S(1)} all-gather(f32[1024]{0:T(1024)S(1)} %get-tuple-element.93), channel_id=1, replica_groups=mesh['req'=32,'tp'=4] {'tp'}, dimensions={0}, use_global_device_ids=true | all-gather | bytes 20480 | tf_op jit(solution)/shard_map/all_gather | solution.py:174
  255.9 12.0 %all_gather.42 = f32[4096]{0:T(1024)S(1)} all-gather(f32[1024]{0:T(1024)S(1)} %get-tuple-element.94), channel_id=1, replica_groups=mesh['req'=32,'tp'=4] {'tp'}, dimensions={0}, use_global_device_ids=true | all-gather | bytes 20480 | tf_op jit(solution)/shard_map/all_gather | solution.py:175
  268.1 0.8 fusion.27
  (165 shorter events, 2.5 us)
Async XLA Ops:
  7.2 9.7 %copy-start.1 = (s32[2]{0:T(128)S(1)}, s32[2]{0:T(128)}, u32[]{:S(2)}) copy-start(s32[2]{0:T(128)} %param.24) | copy-start | bytes 28
  7.2 66.4 %reduce-scatter.4.cloned.1.call-start = ((), (), s32[]{:S(2)}) async-start(), calls=%async_computation.3 | async-start | bytes 1146880
  34.0 60.1 %copy-start = (s32[64,64]{1,0:T(8,128)S(1)}, s32[64,64]{1,0:T(8,128)}, u32[]{:S(2)}) copy-start(s32[64,64]{1,0:T(8,128)} %param.30) | copy-start | bytes 49156
  34.0 60.3 %copy-start.2 = (s32[2,8,64]{2,1,0:T(8,128)S(1)}, s32[2,8,64]{2,1,0:T(8,128)}, u32[]{:S(2)}) copy-start(s32[2,8,64]{2,1,0:T(8,128)} %param.26) | copy-start | bytes 12292
  34.0 85.9 %copy-start.3 = (s32[64]{0:T(128)S(1)}, s32[64]{0:T(128)}, u32[]{:S(2)}) copy-start(s32[64]{0:T(128)} %param.31) | copy-start | bytes 772
  35.3 109.0 %all-gather.5.cloned.1.call-start = ((), (), s32[]{:S(2)}) async-start(), calls=%async_computation.2 | async-start | bytes 7569408 | tf_op jit(solution)/shard_map/all_gather | solution.py:165
Sparse Core Ops, SparseCore 0:
  35.4 38.1 reduce-scatter.3
  94.1 50.1 all-gather.4
where the time goes:
time: 276 us
  blocking collectives  150 us (54%)
  waiting for transfers between devices  61.1 us (22%)
  matrix products  22.3 us (8%)
  local copies, waits for them, and re-layouts  20.5 us (7%)
  between operations  15 us (5%)
  other arithmetic  5.41 us (2%)
    all_gather x3, blocking collectives, combined_all(): pieces = jax.tree.map(lambda part: lax.all_gather(part, axis), value)  70.6 us
    unnamed x3, waiting for transfers between devices  37.5 us
    all_gather x1, blocking collectives, local(): home_states = lax.all_gather(compact, 'req', axis=0, tiled=True)  25.4 us
    all_gather x1, waiting for transfers between devices, local(): lax.all_gather(normed, 'req', axis=0, tiled=True)  23.6 us
    all_gather x1, blocking collectives, local(): lax.all_gather(merged[2], 'tp', axis=0, tiled=True)  12.5 us
    dot_general x1, matrix products, local(): lax.dot_general(lax.all_gather(normed, 'req', axis=0, tiled=True), head_w...  12.1 us
    all_gather x1, blocking collectives, local(): lax.all_gather(merged[0], 'tp', axis=0, tiled=True)  12 us
    all_gather x1, blocking collectives, local(): lax.all_gather(merged[1], 'tp', axis=0, tiled=True)  12 us
  transfers between devices with their start and end apart: 2, of which 2 were waited for; matrix products, arithmetic and copies ran while one was open for 1% of the time, Pallas kernels for 0%

commit v1 on v0

--- a/solution.py
+++ b/solution.py
@@ -133,59 +133,77 @@
     )
     attention = (running_out / running_sum[..., None]).astype(jnp.bfloat16)
     attention_rows = attention.transpose(0, 2, 1, 3).reshape(slots * tree_size, qwidth)
-    flat_stream = stream.reshape(slots * tree_size, model_width)
     rows_all = slots * tree_size
     quarter = rows_all // n_tp
     dslice = model_width // n_tp
-    partial_out = jnp.dot(attention_rows, out_weight, preferred_element_type=jnp.float32)
-    summed = lax.psum_scatter(
-        partial_out.astype(jnp.bfloat16), "tp", scatter_dimension=1, tiled=True
+    acc_rows = accept.shape[1]
+    partial_out = jnp.dot(
+        attention_rows, out_weight, preferred_element_type=jnp.float32
+    ).astype(jnp.bfloat16)
+    accept_b = accept.astype(jnp.bfloat16)
+    partial_compact = jnp.einsum(
+        "sat,std->sad",
+        accept_b,
+        partial_out.reshape(slots, tree_size, model_width),
+        preferred_element_type=jnp.float32,
+    ).astype(jnp.bfloat16)
+    compact_pieces = (
+        partial_compact.reshape(slots * acc_rows, n_tp, dslice)
+        .transpose(1, 0, 2)
+        .reshape(n_tp * slots * acc_rows, dslice)
+    )
+    summed = lax.psum_scatter(partial_out, "tp", scatter_dimension=0, tiled=True).astype(
+        jnp.float32
+    )
+    summed_compact = lax.psum_scatter(
+        compact_pieces, "tp", scatter_dimension=0, tiled=True
     ).astype(jnp.float32)
-    own_stream = lax.dynamic_slice_in_dim(flat_stream, tp_id * dslice, dslice, 1)
+    flat_stream = stream.reshape(rows_all, model_width)
+    own_stream = lax.dynamic_slice_in_dim(flat_stream, tp_id * quarter, quarter, 0)
     post_rows = (own_stream.astype(jnp.float32) + summed).astype(jnp.bfloat16)
     post_float = post_rows.astype(jnp.float32)
     square = jnp.sum(post_float * post_float, axis=1)
-    energy = lax.psum(square, "tp")
-    inverse = lax.rsqrt(energy / model_width + EPS)
-    part_gain = lax.dynamic_slice_in_dim(norm_gain, tp_id * dslice, dslice, 0)
-    normed_slice = (post_float * inverse[:, None] * part_gain[None, :]).astype(jnp.bfloat16)
-    compact = jnp.einsum(
-        "sat,std->sad",
-        accept.astype(jnp.bfloat16),
-        post_rows.reshape(slots, tree_size, dslice),
-        preferred_element_type=jnp.float32,
-    ).astype(jnp.bfloat16)
-    normed = lax.all_to_all(normed_slice, "tp", split_axis=0, concat_axis=1, tiled=True)
+    inverse = lax.rsqrt(square / model_width + EPS)
+    normed = (post_float * inverse[:, None] * norm_gain[None, :]).astype(jnp.bfloat16)
+    stream_pick = jnp.einsum(
+        "sat,std->sad", accept_b, stream, preferred_element_type=jnp.float32
+    )
+    stream_pick = lax.dynamic_slice_in_dim(stream_pick, tp_id * dslice, dslice, 2)
+    compact = (
+        stream_pick + summed_compact.reshape(slots, acc_rows, dslice)
+    ).astype(jnp.bfloat16)
+    extra = slots * acc_rows * dslice // model_width
+    payload = jnp.concatenate(
+        [normed, compact.reshape(extra, model_width)], axis=0
+    )
+    gathered = lax.all_gather(payload, "req", axis=0, tiled=True).reshape(
+        n_req, quarter + extra, model_width
+    )
+    all_rows = gathered[:, :quarter].reshape(n_req * quarter, model_width)
     vocab_loc = head_weight.shape[0]
     wanted_rows = lax.dynamic_slice_in_dim(
         candidate.reshape(n_req, rows_all), tp_id * quarter, quarter, 1
     ).reshape(-1)
     vocab_ids = req_id * vocab_loc + jnp.arange(vocab_loc, dtype=jnp.int32)
     logits = lax.dot_general(
-        lax.all_gather(normed, "req", axis=0, tiled=True),
-        head_weight,
-        (((1,), (1,)), ((), ())),
-        preferred_element_type=jnp.float32,
-    )
-    found_stats = vocab_stats(logits, vocab_ids, wanted_rows, 1)
-    local_stats = tuple((after_part for after_part in found_stats))
-    merged = combined_all((local_stats[0], local_stats[1], local_stats[2]), "req", combine_stats)
-    all_stats = (
-        lax.all_gather(merged[0], "tp", axis=0, tiled=True),
-        lax.all_gather(merged[1], "tp", axis=0, tiled=True),
-        lax.all_gather(merged[2], "tp", axis=0, tiled=True),
-    )
-    row_max, row_sum, picked = tuple(
-        (
-            member.reshape(n_tp, n_req, quarter).transpose(1, 0, 2).reshape(-1)
-            for member in all_stats
-        )
-    )
-    logprob = (picked - row_max - jnp.log(row_sum)).reshape(-1, tree_size)
+        all_rows, head_weight, (((1,), (1,)), ((), ())), preferred_element_type=jnp.float32
+    )
+    row_max, row_sum, picked = vocab_stats(logits, vocab_ids, wanted_rows, 1)
+    stats = lax.all_gather(jnp.stack([row_max, row_sum, picked]), "req", axis=0)
+    joint_max = jnp.max(stats[:, 0], axis=0)
+    joint_sum = jnp.sum(stats[:, 1] * jnp.exp(stats[:, 0] - joint_max[None]), axis=0)
+    joint_pick = jnp.sum(stats[:, 2], axis=0)
+    plane_logprob = joint_pick - joint_max - jnp.log(joint_sum)
+    every = lax.all_gather(plane_logprob, "tp", axis=0)
+    logprob = (
+        every.reshape(n_tp // 2, 2, n_req, quarter)
+        .transpose(2, 0, 1, 3)
+        .reshape(n_req * slots, tree_size)
+    )
     own_requests = req_id * slots + jnp.arange(slots, dtype=jnp.int32)
     selector = dealing[None, :] == own_requests[:, None]
     target_logprob = jnp.dot(selector.astype(jnp.float32), logprob, precision=HIGH)
-    home_states = lax.all_gather(compact, "req", axis=0, tiled=True)
+    home_states = gathered[:, quarter:].reshape(n_req * slots, acc_rows, dslice)
     accepted_state = jnp.einsum(
         "ks,sad->kad",
         selector.astype(jnp.bfloat16),

time: 276 us -> 217 us (0.79)
  blocking collectives: 150 us -> 36.9 us
  waiting for transfers between devices: 61.1 us -> 114 us
    all_gather x7 -> x2, blocking collectives: 133 us -> 36.9 us  [the longest x1 24.4 us: local(): stats = lax.all_gather(jnp.stack([row_max, row_sum, picked]), 'req', axis=0)]
    reduce_scatter x0 -> x2, waiting for transfers between devices: none -> 59.6 us  [the longest x1 35 us: local(): lax.psum_scatter(compact_pieces, 'tp', scatter_dimension=0, tiled=True)]
    unnamed x3, waiting for transfers between devices: 37.5 us -> 0.72 us
    all_gather x1, waiting for transfers between devices: 23.6 us -> 54 us  [local(): lax.all_gather(payload, 'req', axis=0, tiled=True)]
    all_to_all x1 -> x0, blocking collectives: 9.32 us -> none  [local(): lax.all_to_all(normed_slice, 'tp', split_axis=0, concat_axis=1, tiled=True)]
    psum x1 -> x0, blocking collectives: 8 us -> none  [local(): energy = lax.psum(square, 'tp')]
    slice x9 -> x3, local copies, waits for them, and re-layouts: 0.1 us -> 4.82 us  [the longest x2 3.08 us: local(): all_rows = gathered[:, :quarter].reshape(n_req * quarter, model_width)]
    dot_general x2 -> x3, matrix products: 12.2 us -> 10.4 us  [the longest x1 9.95 us: local(): lax.dot_general(all_rows, head_weight, (((1,), (1,)), ((), ())), preferre...]
  transfers between devices with their start and end apart: 2 -> 3, of which waited for: 2 -> 3; matrix products, arithmetic and copies ran while one was open for 1% -> 1% of each run, Pallas kernels for 0% -> 0%
where the time goes in v1:
time: 217 us; the launch traced here: 216 us
  waiting for transfers between devices  114 us (53%)
  blocking collectives  36.9 us (17%)
  local copies, waits for them, and re-layouts  21.7 us (10%)
  matrix products  20.6 us (9%)
  between operations  14.7 us (7%)
  other arithmetic  7.69 us (4%)
    all_gather x1, waiting for transfers between devices, local(): lax.all_gather(payload, 'req', axis=0, tiled=True)  54 us
    reduce_scatter x1, waiting for transfers between devices, local(): lax.psum_scatter(compact_pieces, 'tp', scatter_dimension=0, tiled=True)  35 us
    reduce_scatter x1, waiting for transfers between devices, local(): lax.psum_scatter(partial_out, 'tp', scatter_dimension=0, tiled=True)  24.6 us
    all_gather x1, blocking collectives, local(): stats = lax.all_gather(jnp.stack([row_max, row_sum, picked]), 'req', axis=0)  24.4 us
    all_gather x1, blocking collectives, local(): every = lax.all_gather(plane_logprob, 'tp', axis=0)  12.5 us
    dot_general x1, matrix products, local(): lax.dot_general(all_rows, head_weight, (((1,), (1,)), ((), ())), preferre...  9.95 us
    dynamic_slice x2, local copies, waits for them, and re-layouts, visit_block(): lax.dynamic_slice_in_dim(cache_value, offset, block_rows, 1)  6.9 us
  transfers between devices with their start and end apart: 3, of which 3 were waited for; matrix products, arithmetic and copies ran while one was open for 1% of the time, Pallas kernels for 0%

profile of v1, /device:TPU:0, one launch (start us, length us, event | category | flops | bytes accessed | tf_op | source)
XLA Modules:
  0.0 216.2 jit_solution(12022398479503370900)
XLA Ops:
  7.2 1.3 reduce_max.46
  9.2 1.0 fusion.24
  10.2 0.2 fusion.44
  10.4 0.9 fusion.25
  11.3 0.2 fusion.43
  11.5 0.2 fusion.45
  11.7 0.1 copy.66
  11.8 1.2 reshape.137
  13.0 0.7 copy.67
  13.7 1.2 reshape.138
  14.9 1.2 reshape.139
  16.1 0.2 fusion.41
  16.5 0.3 fusion.13
  16.8 12.5 %while.14 = (s32[]{:T(128)}, f32[2,4,64]{2,1,0:T(4,128)S(1)}, f32[2,4,64]{2,1,0:T(4,128)S(1)}, f32[2,4,64,224]{3,2,1,0:T(8,128)S(1)}, s32[]{:T(128)}, /*index=5*...) while((s32[]{:T(128)}, f32[2,4,64]{2,1,0:T(4,128)S(1)}, ...), condition=%wide.region_6.7_spmd, body=%wide.region_3.6_spmd.sunk | while | flops 236947968 | bytes 23599292 | solution.py:131
  16.9 4.1 %constant_dynamic-slice_fusion.4 = (bf16[2,512,896]{2,1,0:T(8,128)(2,1)}, bf16[2,512,896]{2,1,0:T(8,128)(2,1)}) fusion(bf16[2,1024,896]{2,1,0:T(8,128)(2,1)} %get-tuple-element.248, s32[]{:T(128)S(6)} %select_n.42, bf16[2,1024,896]{2,1,0:T(8,128)(2,1)} %get-tuple-element.246), kind=kLoop, calls=%fused_computation.13.clone.1 | loop fusion | bytes 7340036 | tf_op jit(solution)/shard_map/while/body/dynamic_slice | solution.py:105
  21.0 2.7 %copy.105 = bf16[2,512,896]{1,2,0:T(8,128)(2,1)S(1)} copy(bf16[2,512,896]{2,1,0:T(8,128)(2,1)} %get-tuple-element.208) | data formatting | bytes 3670016 | tf_op jit(solution)/shard_map/while/body/dynamic_slice | solution.py:102
  23.8 1.5 fusion.73
  25.3 0.3 fusion.74
  25.6 2.8 %copy.106 = bf16[2,512,896]{1,2,0:T(8,128)(2,1)S(1)} copy(bf16[2,512,896]{2,1,0:T(8,128)(2,1)} %get-tuple-element.213) | data formatting | bytes 3670016 | tf_op jit(solution)/shard_map/while/body/dynamic_slice | solution.py:105
  28.4 0.7 fusion.75
  29.1 0.2 multiply_add_fusion.5
  29.3 0.1 fusion.16
  29.4 0.2 copy.74
  29.7 0.2 reshape.140
  29.9 4.0 %convolution_convert_fusion = bf16[128,3584]{1,0:T(8,128)(2,1)S(1)} fusion(bf16[128,896]{1,0:T(8,128)(2,1)S(1)} %reshape.140, bf16[896,3584]{1,0:T(8,128)(2,1)} %param.25), kind=kOutput, calls=%fused_computation.15 | convolution fusion | flops 822542336 | bytes 7569408 | tf_op jit(solution)/shard_map/dot_general | solution.py:140
  34.0 0.2 fusion.7
  34.3 0.7 copy.75
  35.0 0.7 reduce-scatter.3.cloned.1.call-update
  35.8 0.2 fusion.33
  36.0 35.0 %reduce-scatter.5.cloned.1.call-done = bf16[16,896]{1,0:T(8,128)(2,1)} async-done(((bf16[64,896]{1,0:T(8,128)(2,1)}), bf16[16,896]{1,0:T(8,128)(2,1)}) %reduce-scatter.5.cloned.1.call-update) | async-done | bytes 28688 | tf_op jit(solution)/shard_map/reduce_scatter | solution.py:158
  71.0 0.8 fusion.26
  71.8 24.6 %reduce-scatter.3.cloned.1.call-done = bf16[32,3584]{1,0:T(8,128)(2,1)} async-done(((bf16[128,3584]{1,0:T(8,128)(2,1)}), bf16[32,3584]{1,0:T(8,128)(2,1)}) %reduce-scatter.3.cloned.1.call-update) | async-done | bytes 229392 | tf_op jit(solution)/shard_map/reduce_scatter | solution.py:155
  96.4 1.1 fusion.10
  97.5 1.1 fusion.12
  98.6 0.8 maximum_bitcast_fusion
  99.6 54.0 %all-gather.6.cloned.1.call-done = bf16[32,36,3584]{2,1,0:T(8,128)(2,1)} async-done(((bf16[1,36,3584]{2,1,0:T(8,128)(2,1)}), bf16[32,36,3584]{2,1,0:T(8,128)(2,1)}) %all-gather.6.cloned.1.call-update) | async-done | bytes 8257552 | tf_op jit(solution)/shard_map/all_gather | solution.py:179
  153.6 1.7 slice.25
  155.3 0.6 reshape.152
  155.9 0.3 convolution_convert_fusion.2
  156.2 0.6 copy.79
  156.8 3.1 %slice-done = bf16[32,32,3584]{2,1,0:T(8,128)(2,1)S(1)} async-done(((bf16[32,36,3584]{2,1,0:T(8,128)(2,1)}), bf16[32,32,3584]{2,1,0:T(8,128)(2,1)S(1)}, s32[]{:S(2)}) %slice-start) | async-done | bytes 7340056 | tf_op jit(solution)/shard_map/slice | solution.py:182
  159.9 10.0 %fusion.42 = (f32[1024]{0:T(1024)S(1)}, f32[1024,1000]{0,1:T(8,128)S(1)}) fusion(bf16[1024,3584]{1,0:T(8,128)(2,1)S(1)} %bitcast.86, bf16[1000,3584]{1,0:T(8,128)(2,1)} %param.27), kind=kOutput, calls=%fused_computation.79 | convolution fusion | flops 7341054976 | bytes 18608128 | tf_op jit(solution)/shard_map/dot_general | solution.py:188
  169.9 1.4 exponential_reduce_fusion
  171.3 24.4 %all-gather.3 = f32[32,3,1024]{2,1,0:T(4,128)S(1)} all-gather(f32[1,3,1024]{2,1,0:T(4,128)S(1)} %maximum_bitcast_fusion.1), channel_id=2, replica_groups=mesh['req'=32,'tp'=4] {'req'}, dimensions={0}, use_global_device_ids=true | all-gather | bytes 405504 | tf_op jit(solution)/shard_map/all_gather | solution.py:192
  195.7 0.3 slice_reduce_fusion
  196.1 12.5 %all-gather.1 = f32[4096]{0:T(1024)S(1)} all-gather(f32[1024]{0:T(1024)S(1)} %log_subtract_fusion), channel_id=3, replica_groups=mesh['req'=32,'tp'=4] {'tp'}, dimensions={0}, use_global_device_ids=true | all-gather | bytes 20480 | tf_op jit(solution)/shard_map/all_gather | solution.py:197
  208.8 0.1 reshape.151
  208.9 0.8 fusion.30
  (42 shorter events, 0.9 us)
Async XLA Ops:
  7.2 9.6 %copy-start.5 = (s32[2]{0:T(128)S(1)}, s32[2]{0:T(128)}, u32[]{:S(2)}) copy-start(s32[2]{0:T(128)} %param.22) | copy-start | bytes 28
  7.2 63.8 %reduce-scatter.5.cloned.1.call-start = ((), (), s32[]{:S(2)}) async-start(), calls=%async_computation.3 | async-start | bytes 143360 | tf_op jit(solution)/shard_map/reduce_scatter | solution.py:158
  29.9 4.1 %copy-start.2 = (s32[2,8,64]{2,1,0:T(8,128)S(1)}, s32[2,8,64]{2,1,0:T(8,128)}, u32[]{:S(2)}) copy-start(s32[2,8,64]{2,1,0:T(8,128)} %param.24) | copy-start | bytes 12292
  29.9 5.9 %copy-start.1 = (bf16[2,64,3584]{2,1,0:T(8,128)(2,1)S(1)}, bf16[2,64,3584]{2,1,0:T(8,128)(2,1)}, u32[]{:S(2)}) copy-start(bf16[2,64,3584]{2,1,0:T(8,128)(2,1)} %param.16) | copy-start | bytes 2752516
  33.9 1.1 copy-start
  33.9 63.6 %copy-start.4 = (f32[3584]{0:T(1024)S(1)}, f32[3584]{0:T(1024)}, u32[]{:S(2)}) copy-start(f32[3584]{0:T(1024)} %param.26) | copy-start | bytes 43012
  34.0 65.4 %copy-start.3 = (s32[64,64]{1,0:T(8,128)S(1)}, s32[64,64]{1,0:T(8,128)}, u32[]{:S(2)}) copy-start(s32[64,64]{1,0:T(8,128)} %param.28) | copy-start | bytes 49156
  34.9 121.0 %copy-start.6 = (s32[64]{0:T(128)S(1)}, s32[64]{0:T(128)}, u32[]{:S(2)}) copy-start(s32[64]{0:T(128)} %param.29) | copy-start | bytes 772
  34.9 61.4 %reduce-scatter.3.cloned.1.call-start = ((), (), s32[]{:S(2)}) async-start(), calls=%async_computation.2 | async-start | bytes 1146880 | tf_op jit(solution)/shard_map/reduce_scatter | solution.py:155
  35.7 117.9 %all-gather.6.cloned.1.call-start = ((), (), s32[]{:S(2)}) async-start(), calls=%async_computation.4 | async-start | bytes 9461760 | tf_op jit(solution)/shard_map/all_gather | solution.py:179
  156.8 3.1 %slice-start = ((bf16[32,36,3584]{2,1,0:T(8,128)(2,1)}), bf16[32,32,3584]{2,1,0:T(8,128)(2,1)S(1)}, s32[]{:S(2)}) async-start(bf16[32,36,3584]{2,1,0:T(8,128)(2,1)} %all-gather.6.cloned.1.call-done), calls=%async_computation.5 | async-start | bytes 14680064 | tf_op jit(solution)/shard_map/slice | solution.py:182
Sparse Core Ops, SparseCore 0:
  35.1 35.8 reduce-scatter.4
  73.4 22.9 reduce-scatter.2
  99.5 54.0 all-gather.5

commit v2 on v1

v2 whole, which is shorter than its diff:
```python
import jax
import jax.numpy as jnp
from jax import lax
from jax.sharding import PartitionSpec as P

HD = 224
ACC = 8


EPS = 1e-05
HIGH = lax.Precision.HIGHEST
block_limit = 512


def combined_all(value, axis, join):
    pieces = jax.tree.map(lambda part: lax.all_gather(part, axis), value)
    head = jax.tree.map(lambda part: part[0], pieces)
    tail = jax.tree.map(lambda part: part[1:], pieces)
    subtotal, _ = lax.scan(lambda subtotal, share: (join(subtotal, share), None), head, tail)
    return subtotal


def ancestry(parents):
    node_count = parents.shape[-1]
    node_ids = jnp.arange(node_count, dtype=jnp.int32)
    stride_map = (parents[..., :, None] == node_ids).astype(jnp.float32)
    reached = jnp.broadcast_to(jnp.eye(node_count, dtype=jnp.float32), stride_map.shape) > 0.5
    for doubling in range((ACC - 1).bit_length()):
        further = lax.optimization_barrier(
            jnp.einsum("rtk,rku->rtu", reached.astype(jnp.float32), stride_map, precision=HIGH)
        )
        reached = jnp.logical_or(reached, further > 0.5)
        stride_map = jnp.einsum("rtk,rku->rtu", stride_map, stride_map, precision=HIGH)
    return reached


def combine_stats(earlier, later):
    joint_max = jnp.maximum(earlier[0], later[0])
    joint_sum = earlier[1] * jnp.exp(earlier[0] - joint_max) + later[1] * jnp.exp(
        later[0] - joint_max
    )
    return (joint_max, joint_sum, earlier[2] + later[2])


def vocab_stats(logits, vocab_ids, wanted, along):
    row_max = jnp.max(logits, axis=along)
    row_sum = jnp.sum(jnp.exp(logits - jnp.expand_dims(row_max, along)), axis=along)
    matches = jnp.expand_dims(vocab_ids, 1 - along) == jnp.expand_dims(wanted, along)
    picked = jnp.sum(jnp.where(matches, logits, 0.0), axis=along)
    return (row_max, row_sum, picked)


def local(
    stream,
    queries,
    key_new,
    value_new,
    cache_key,
    cache_value,
    cache_length,
    parents,
    accept,
    out_weight,
    norm_gain,
    head_weight,
    candidate,
    dealing,
):
    slots, tree_size, qwidth = queries.shape
    model_width = stream.shape[2]
    heads_loc = qwidth // HD
    n_tp = lax.axis_size("tp")
    n_req = lax.axis_size("req")
    tp_id = lax.axis_index("tp")
    req_id = lax.axis_index("req")
    score_scale = HD ** (-0.5)
    cache_cap = cache_key.shape[1]
    column_head = jnp.arange(qwidth, dtype=jnp.int32) // HD
    head_mask = column_head[None, :] == jnp.arange(heads_loc, dtype=jnp.int32)[:, None]
    spread_q = jnp.where(
        head_mask[None, :, None, :], queries[:, None, :, :], jnp.zeros((), queries.dtype)
    ).reshape(slots, heads_loc * tree_size, qwidth)
    past_scores = (
        jnp.einsum("rnd,rkd->rnk", spread_q, cache_key, preferred_element_type=jnp.float32)
        * score_scale
    )
    live = jnp.arange(cache_cap, dtype=jnp.int32)[None, :] < cache_length[:, None]
    past_scores = jnp.where(live[:, None, :], past_scores, -jnp.inf)
    visible = ancestry(parents)
    seen = jnp.broadcast_to(
        visible[:, None], (slots, heads_loc, tree_size, tree_size)
    ).reshape(slots, heads_loc * tree_size, tree_size)
    tree_scores = (
        jnp.einsum("rnd,rkd->rnk", spread_q, key_new, preferred_element_type=jnp.float32)
        * score_scale
    )
    tree_scores = jnp.where(seen, tree_scores, -jnp.inf)
    highest = jnp.maximum(jnp.max(past_scores, axis=2), jnp.max(tree_scores, axis=2))
    past_weights = jnp.exp(past_scores - highest[..., None])
    tree_weights = jnp.exp(tree_scores - highest[..., None])
    denominator = jnp.sum(past_weights, axis=2) + jnp.sum(tree_weights, axis=2)
    mixed = jnp.einsum(
        "rnk,rkd->rnd",
        past_weights.astype(jnp.bfloat16),
        cache_value,
        preferred_element_type=jnp.float32,
    ) + jnp.einsum(
        "rnk,rkd->rnd",
        tree_weights.astype(jnp.bfloat16),
        value_new,
        preferred_element_type=jnp.float32,
    )
    mixed = (mixed / denominator[..., None]).reshape(slots, heads_loc, tree_size, qwidth)
    attention = jnp.sum(
        jnp.where(head_mask[None, :, None, :], mixed, 0.0), axis=1
    ).astype(jnp.bfloat16)
    attention_rows = attention.reshape(slots * tree_size, qwidth)
    rows_all = slots * tree_size
    quarter = rows_all // n_tp
    dslice = model_width // n_tp
    halves = tree_size // quarter
    acc_rows = accept.shape[1]
    own_slot = tp_id // halves
    node_off = (tp_id % halves) * quarter
    partial_out = jnp.dot(
        attention_rows, out_weight, preferred_element_type=jnp.float32
    ).astype(jnp.bfloat16)
    summed = lax.psum_scatter(partial_out, "tp", scatter_dimension=0, tiled=True).astype(
        jnp.float32
    )
    flat_stream = stream.reshape(rows_all, model_width)
    own_stream = lax.dynamic_slice_in_dim(flat_stream, tp_id * quarter, quarter, 0)
    post_rows = (own_stream.astype(jnp.float32) + summed).astype(jnp.bfloat16)
    post_float = post_rows.astype(jnp.float32)
    square = jnp.sum(post_float * post_float, axis=1)
    inverse = lax.rsqrt(square / model_width + EPS)
    normed = (post_float * inverse[:, None] * norm_gain[None, :]).astype(jnp.bfloat16)
    accept_own = lax.dynamic_slice_in_dim(
        lax.dynamic_index_in_dim(accept, own_slot, 0, keepdims=False), node_off, quarter, 1
    )
    picked_rows = jnp.dot(
        accept_own.astype(jnp.bfloat16), post_rows, preferred_element_type=jnp.float32
    ).astype(jnp.bfloat16)
    payload = jnp.concatenate([normed, picked_rows], axis=0)
    gathered = lax.all_gather(payload, "req", axis=0, tiled=True).reshape(
        n_req, quarter + acc_rows, model_width
    )
    all_rows = gathered[:, :quarter].reshape(n_req * quarter, model_width)
    vocab_loc = head_weight.shape[0]
    wanted_rows = lax.dynamic_slice_in_dim(
        candidate.reshape(n_req, rows_all), tp_id * quarter, quarter, 1
    ).reshape(-1)
    vocab_ids = req_id * vocab_loc + jnp.arange(vocab_loc, dtype=jnp.int32)
    logits = lax.dot_general(
        all_rows, head_weight, (((1,), (1,)), ((), ())), preferred_element_type=jnp.float32
    )
    row_max, row_sum, picked = vocab_stats(logits, vocab_ids, wanted_rows, 1)
    stats = lax.all_gather(jnp.stack([row_max, row_sum, picked]), "req", axis=0)
    joint_max = jnp.max(stats[:, 0], axis=0)
    joint_sum = jnp.sum(stats[:, 1] * jnp.exp(stats[:, 0] - joint_max[None]), axis=0)
    joint_pick = jnp.sum(stats[:, 2], axis=0)
    plane_logprob = (joint_pick - joint_max - jnp.log(joint_sum)).reshape(n_req, quarter)
    own_requests = req_id * slots + jnp.arange(slots, dtype=jnp.int32)
    slot_ids = jnp.arange(dealing.shape[0], dtype=jnp.int32)
    serving = jnp.sum(
        jnp.where(dealing[None, :] == own_requests[:, None], slot_ids[None, :], 0), axis=1
    )
    source = serving // slots
    held = (serving % slots) == own_slot
    lp_rows = jnp.take(plane_logprob, source, axis=0)
    node_half = jnp.arange(tree_size, dtype=jnp.int32) // quarter == tp_id % halves
    lp_full = jnp.where(
        held[:, None] & node_half[None, :], jnp.tile(lp_rows, (1, halves)), 0.0
    )
    state_rows = jnp.take(gathered[:, quarter:], source, axis=0).astype(jnp.float32)
    state_rows = jnp.where(held[:, None, None], state_rows, 0.0)
    state_parts = state_rows.reshape(slots * acc_rows, n_tp, dslice).transpose(1, 0, 2)
    outgoing = jnp.concatenate(
        [
            state_parts.reshape(n_tp, slots * acc_rows * dslice),
            jnp.broadcast_to(lp_full.reshape(1, -1), (n_tp, slots * tree_size)),
        ],
        axis=1,
    )
    incoming = lax.all_to_all(outgoing, "tp", split_axis=0, concat_axis=0, tiled=True)
    merged = jnp.sum(incoming, axis=0)
    accepted_state = (
        merged[: slots * acc_rows * dslice].reshape(slots, acc_rows, dslice).astype(jnp.bfloat16)
    )
    target_logprob = merged[slots * acc_rows * dslice :].reshape(slots, tree_size)
    return (target_logprob, accepted_state)


def solution(mesh):
    placed = (
        P("req", None, None),
        P("req", None, "tp"),
        P("req", None, "tp"),
        P("req", None, "tp"),
        P("req", None, "tp"),
        P("req", None, "tp"),
        P("req"),
        P("req", None),
        P("req", None, None),
        P("tp", None),
        P(),
        P("req", None),
        P(),
        P(),
    )
    return jax.shard_map(
        local,
        mesh=mesh,
        in_specs=placed,
        out_specs=(P("req", None), P("req", None, "tp")),
        check_vma=False,
    )
```

time: 217 us -> 174 us (0.80)
  waiting for transfers between devices: 114 us -> 79.1 us
  local copies, waits for them, and re-layouts: 21.7 us -> 14 us
    reduce_scatter x1 -> x0, waiting for transfers between devices: 35 us -> none  [local(): lax.psum_scatter(compact_pieces, 'tp', scatter_dimension=0, tiled=True)]
    all_gather x1 -> x0, blocking collectives: 12.5 us -> none  [local(): every = lax.all_gather(plane_logprob, 'tp', axis=0)]
    all_to_all x0 -> x1, blocking collectives: none -> 11.1 us  [local(): lax.all_to_all(outgoing, 'tp', split_axis=0, concat_axis=0, tiled=True)]
    dynamic_slice x3 -> x0, local copies, waits for them, and re-layouts: 9.64 us -> none  [the longest x2 6.9 us: visit_block(): lax.dynamic_slice_in_dim(cache_value, offset, block_rows, 1)]
    reshape x10 -> x2, local copies, waits for them, and re-layouts: 5.37 us -> 0.8 us  [the longest x1 0.64 us: local(): merged[slots * acc_rows * dslice:].reshape(slots, tree_size)]
    slice x2 -> x1, local copies, waits for them, and re-layouts: 3.08 us -> 6.77 us  [local(): all_rows = gathered[:, :quarter].reshape(n_req * quarter, model_width)]
    dot_general x8 -> x5, matrix products: 4.21 us -> 6 us  [the longest x1 3.58 us: local(): jnp.einsum('rnd,rkd->rnk', spread_q, cache_key, preferred_element_type=jn...]
  transfers between devices with their start and end apart: 3 -> 2, of which waited for: 3 -> 2; matrix products, arithmetic and copies ran while one was open for 1% -> 1% of each run, Pallas kernels for 0% -> 0%
where the time goes in v2:
time: 174 us; the launch traced here: 173 us
  waiting for transfers between devices  79.1 us (45%)
  blocking collectives  35.7 us (21%)
  matrix products  22.5 us (13%)
  between operations  14.4 us (8%)
  local copies, waits for them, and re-layouts  14 us (8%)
  other arithmetic  7.43 us (4%)
    all_gather x1, waiting for transfers between devices, local(): lax.all_gather(payload, 'req', axis=0, tiled=True)  53.2 us
    reduce_scatter x1, waiting for transfers between devices, local(): lax.psum_scatter(partial_out, 'tp', scatter_dimension=0, tiled=True)  25.9 us
    all_gather x1, blocking collectives, local(): stats = lax.all_gather(jnp.stack([row_max, row_sum, picked]), 'req', axis=0)  24.6 us
    dot_general x1, matrix products, local(): lax.dot_general(all_rows, head_weight, (((1,), (1,)), ((), ())), preferre...  12.1 us
    all_to_all x1, blocking collectives, local(): lax.all_to_all(outgoing, 'tp', split_axis=0, concat_axis=0, tiled=True)  11.1 us
    slice x1, local copies, waits for them, and re-layouts, local(): all_rows = gathered[:, :quarter].reshape(n_req * quarter, model_width)  6.77 us
    dot_general x1, matrix products, local(): jnp.einsum('rnd,rkd->rnk', spread_q, cache_key, preferred_element_type=jn...  3.58 us
  transfers between devices with their start and end apart: 2, of which 2 were waited for; matrix products, arithmetic and copies ran while one was open for 1% of the time, Pallas kernels for 0%

profile of v2, /device:TPU:0, one launch (start us, length us, event | category | flops | bytes accessed | tf_op | source)
XLA Modules:
  0.0 173.2 jit_solution(4912301310798418574)
XLA Ops:
  7.3 0.8 iota_compare_fusion.5
  8.0 1.0 fusion.20
  9.0 0.9 fusion.21
  9.9 0.2 fusion.40
  10.1 0.2 fusion.39
  10.3 0.2 fusion.41
  10.5 0.1 copy.21
  10.6 0.1 broadcast_in_dim.172
  10.7 0.2 reshape.283
  10.9 1.1 bitcast_select_fusion
  12.0 3.6 %fusion = (f32[2,256]{1,0:T(2,128)S(1)}, f32[2,256,1024]{2,1,0:T(8,128)S(1)}) fusion(pred[2,1024]{1,0:T(4,128)(4,1)S(1)} %iota_compare_fusion.5, bf16[2,256,896]{2,1,0:T(8,128)(2,1)S(1)} %bitcast_select_fusion, bf16[2,1024,896]{2,1,0:T(8,128)(2,1)} %param.18), kind=kOutput, calls=%fused_computation.8 | convolution fusion | flops 941096448 | bytes 6688768 | tf_op jit(solution)/shard_map/rnd,rkd->rnk/dot_general | solution.py:84
  15.6 0.4 fusion.37
  16.1 0.6 fusion.1
  16.7 1.3 fusion.4
  18.1 0.5 add_divide_fusion
  18.5 0.1 select_reduce_fusion.1
  18.7 1.6 slice-done.1
  20.3 2.1 %convolution_convert_fusion = bf16[128,3584]{1,0:T(8,128)(2,1)} fusion(bf16[128,896]{1,0:T(8,128)(2,1)S(1)} %bitcast.69, bf16[896,3584]{1,0:T(8,128)(2,1)S(1)} %bitcast.64), kind=kOutput, calls=%fused_computation.2 | convolution fusion | flops 822542336 | bytes 7569408 | tf_op jit(solution)/shard_map/dot_general | solution.py:125
  22.5 25.9 %reduce-scatter.2.cloned.1.call-done = bf16[32,3584]{1,0:T(8,128)(2,1)} async-done(((bf16[128,3584]{1,0:T(8,128)(2,1)}), bf16[32,3584]{1,0:T(8,128)(2,1)}) %reduce-scatter.2.cloned.1.call-update) | async-done | bytes 229392 | tf_op jit(solution)/shard_map/reduce_scatter | solution.py:128
  48.4 1.2 fusion.10
  49.7 0.1 fusion.12
  49.8 0.2 convolution_convert_fusion.1
  50.0 0.8 pad_maximum_fusion
  50.8 0.2 fusion.30
  51.1 0.1 broadcast_in_dim.160
  51.2 0.1 broadcast_in_dim.157
  51.3 0.1 broadcast_and_fusion
  51.4 0.1 and.121
  51.6 0.1 constant_dynamic-slice_fusion
  51.7 0.1 eq.113
  51.8 53.2 %all-gather.4.cloned.1.call-done = bf16[1280,3584]{1,0:T(8,128)(2,1)} async-done(((bf16[40,3584]{1,0:T(8,128)(2,1)}), bf16[1280,3584]{1,0:T(8,128)(2,1)}) %all-gather.4.cloned.1.call-update) | async-done | bytes 9175056 | tf_op jit(solution)/shard_map/all_gather | solution.py:145
  105.0 1.6 slice.42
  106.6 6.8 %slice.43 = bf16[32,32,3584]{2,1,0:T(8,128)(2,1)} slice(bf16[32,40,3584]{2,1,0:T(8,128)(2,1)} %bitcast.66), slice={[0:32], [0:32], [0:3584]} | slice | bytes 14680064 | tf_op jit(solution)/shard_map/slice | solution.py:148
  113.4 0.6 gather_fusion
  114.0 0.1 select_bitcast_fusion
  114.1 0.1 copy.26
  114.2 12.1 %fusion.38 = (f32[1024]{0:T(1024)S(1)}, f32[1024,1000]{0,1:T(8,128)S(1)}) fusion(bf16[1024,3584]{1,0:T(8,128)(2,1)} %bitcast.67, bf16[1000,3584]{1,0:T(8,128)(2,1)} %param.25), kind=kOutput, calls=%fused_computation.101 | convolution fusion | flops 7341054976 | bytes 18608128 | tf_op jit(solution)/shard_map/dot_general | solution.py:154
  126.2 1.4 exponential_reduce_fusion
  127.7 24.6 %all-gather.1 = f32[32,3,1024]{2,1,0:T(4,128)S(1)} all-gather(f32[1,3,1024]{2,1,0:T(4,128)S(1)} %maximum_bitcast_fusion), channel_id=2, replica_groups=mesh['req'=32,'tp'=4] {'req'}, dimensions={0}, use_global_device_ids=true | all-gather | bytes 405504 | tf_op jit(solution)/shard_map/all_gather | solution.py:158
  152.3 0.3 slice_reduce_fusion
  152.8 0.6 gather_fusion.1
  153.4 0.1 tile.10
  153.5 0.1 pad_maximum_fusion.1
  153.6 0.2 all_to_all.6
  153.8 11.1 %all_to_all.9 = f32[4,1,14464]{2,1,0:T(1,128)S(1)} all-to-all(f32[4,1,14464]{2,1,0:T(1,128)S(1)} %all_to_all.6), channel_id=1, replica_groups=mesh['req'=32,'tp'=4] {'tp'}, dimensions={0} | all-to-all | bytes 462848 | tf_op jit(solution)/shard_map/all_to_all | solution.py:185
  164.8 0.2 reduce_sum.102
  165.1 0.6 reshape.289
  165.7 0.7 convert_element_type.72
  (52 shorter events, 0.9 us)
Async XLA Ops:
  7.2 10.9 %copy-start = (bf16[2,64,896]{2,1,0:T(8,128)(2,1)S(1)}, bf16[2,64,896]{2,1,0:T(8,128)(2,1)}, u32[]{:S(2)}) copy-start(bf16[2,64,896]{2,1,0:T(8,128)(2,1)} %param.17) | copy-start | bytes 688132
  7.2 41.2 %reduce-scatter.2.cloned.1.call-start = ((), (), s32[]{:S(2)}) async-start(), calls=%async_computation.2 | async-start | bytes 1146880 | tf_op jit(solution)/shard_map/reduce_scatter | solution.py:128
  12.0 3.6 %copy-start.2 = (bf16[2,64,896]{2,1,0:T(8,128)(2,1)S(1)}, bf16[2,64,896]{2,1,0:T(8,128)(2,1)}, u32[]{:S(2)}) copy-start(bf16[2,64,896]{2,1,0:T(8,128)(2,1)} %param.16) | copy-start | bytes 688132
  12.0 4.6 %copy-start.1 = (bf16[2,1024,896]{2,1,0:T(8,128)(2,1)S(1)}, bf16[2,1024,896]{2,1,0:T(8,128)(2,1)}, u32[]{:S(2)}) copy-start(bf16[2,1024,896]{2,1,0:T(8,128)(2,1)} %param.19) | copy-start | bytes 11010052
  16.6 2.0 %slice-start = ((s8[6422528]{0:T(1024)(128)(4,1)}), s8[2228224]{0:T(1024)(128)(4,1)S(1)}, s32[]{:S(2)}) async-start(s8[6422528]{0:T(1024)(128)(4,1)} %bitcast.63), calls=%async_computation.4 | async-start | bytes 4456448
  18.1 2.2 %slice-start.1 = ((s8[6422528]{0:T(1024)(128)(4,1)}), s8[4194304]{0:T(1024)(128)(4,1)S(1)}, s32[]{:S(2)}) async-start(s8[6422528]{0:T(1024)(128)(4,1)} %bitcast.63), calls=%async_computation.5 | async-start | bytes 8388608
  20.3 29.3 %copy-start.4 = (f32[3584]{0:T(1024)S(1)}, f32[3584]{0:T(1024)}, u32[]{:S(2)}) copy-start(f32[3584]{0:T(1024)} %param.24) | copy-start | bytes 43012
  22.4 27.4 %copy-start.5 = (s32[2,8,64]{2,1,0:T(8,128)S(1)}, s32[2,8,64]{2,1,0:T(8,128)}, u32[]{:S(2)}) copy-start(s32[2,8,64]{2,1,0:T(8,128)} %param.22) | copy-start | bytes 12292
  22.4 28.4 %copy-start.6 = (s32[64]{0:T(128)S(1)}, s32[64]{0:T(128)}, u32[]{:S(2)}) copy-start(s32[64]{0:T(128)} %param.27) | copy-start | bytes 772
  22.4 29.1 %copy-start.3 = (s32[64,64]{1,0:T(8,128)S(1)}, s32[64,64]{1,0:T(8,128)}, u32[]{:S(2)}) copy-start(s32[64,64]{1,0:T(8,128)} %param.26) | copy-start | bytes 49156
  22.4 82.6 %all-gather.4.cloned.1.call-start = ((), (), s32[]{:S(2)}) async-start(), calls=%async_computation.3 | async-start | bytes 9461760 | tf_op jit(solution)/shard_map/all_gather | solution.py:145
Sparse Core Ops, SparseCore 0:
  22.5 25.8 reduce-scatter.1
  50.9 54.0 all-gather.3

commit v3 on v2

--- a/solution.py
+++ b/solution.py
@@ -125,9 +125,10 @@
     partial_out = jnp.dot(
         attention_rows, out_weight, preferred_element_type=jnp.float32
     ).astype(jnp.bfloat16)
-    summed = lax.psum_scatter(partial_out, "tp", scatter_dimension=0, tiled=True).astype(
-        jnp.float32
-    )
+    arriving = lax.all_to_all(
+        partial_out.reshape(n_tp, quarter, model_width), "tp", split_axis=0, concat_axis=0, tiled=True
+    )
+    summed = jnp.sum(arriving.astype(jnp.float32), axis=0)
     flat_stream = stream.reshape(rows_all, model_width)
     own_stream = lax.dynamic_slice_in_dim(flat_stream, tp_id * quarter, quarter, 0)
     post_rows = (own_stream.astype(jnp.float32) + summed).astype(jnp.bfloat16)
@@ -145,17 +146,31 @@
     gathered = lax.all_gather(payload, "req", axis=0, tiled=True).reshape(
         n_req, quarter + acc_rows, model_width
     )
-    all_rows = gathered[:, :quarter].reshape(n_req * quarter, model_width)
+    all_rows = gathered.reshape(n_req * (quarter + acc_rows), model_width)
     vocab_loc = head_weight.shape[0]
-    wanted_rows = lax.dynamic_slice_in_dim(
-        candidate.reshape(n_req, rows_all), tp_id * quarter, quarter, 1
+    wanted_rows = jnp.concatenate(
+        [
+            lax.dynamic_slice_in_dim(
+                candidate.reshape(n_req, rows_all), tp_id * quarter, quarter, 1
+            ),
+            jnp.zeros((n_req, acc_rows), candidate.dtype),
+        ],
+        axis=1,
     ).reshape(-1)
     vocab_ids = req_id * vocab_loc + jnp.arange(vocab_loc, dtype=jnp.int32)
     logits = lax.dot_general(
         all_rows, head_weight, (((1,), (1,)), ((), ())), preferred_element_type=jnp.float32
     )
     row_max, row_sum, picked = vocab_stats(logits, vocab_ids, wanted_rows, 1)
-    stats = lax.all_gather(jnp.stack([row_max, row_sum, picked]), "req", axis=0)
+    local_stats = jnp.stack([row_max, row_sum, picked]).reshape(3, n_req, quarter + acc_rows)
+    local_stats = local_stats[:, :, :quarter].reshape(3, n_req * quarter)
+    stats = lax.all_to_all(
+        jnp.broadcast_to(local_stats[None], (n_req,) + local_stats.shape),
+        "req",
+        split_axis=0,
+        concat_axis=0,
+        tiled=True,
+    )
     joint_max = jnp.max(stats[:, 0], axis=0)
     joint_sum = jnp.sum(stats[:, 1] * jnp.exp(stats[:, 0] - joint_max[None]), axis=0)
     joint_pick = jnp.sum(stats[:, 2], axis=0)

time: 174 us -> 157 us (0.902)
  blocking collectives: 35.7 us -> 11.5 us
  starting transfers between devices: 0.08 us -> 11 us
  local copies, waits for them, and re-layouts: 14 us -> 8.37 us
  waiting for transfers between devices: 79.1 us -> 75.4 us
  matrix products: 22.5 us -> 26 us
  other arithmetic: 7.43 us -> 9.34 us
    reduce_scatter x1 -> x0, waiting for transfers between devices: 25.9 us -> none  [local(): lax.psum_scatter(partial_out, 'tp', scatter_dimension=0, tiled=True)]
    all_gather x1 -> x0, blocking collectives: 24.6 us -> none  [local(): stats = lax.all_gather(jnp.stack([row_max, row_sum, picked]), 'req', axis=0)]
    all_to_all x0 -> x2, waiting for transfers between devices: none -> 21.8 us  [the longest x1 13.6 us: local(): lax.all_to_all(partial_out.reshape(n_tp, quarter, model_width), 'tp', spl...]
    all_to_all x0 -> x2, starting transfers between devices: none -> 11 us  [the longest x1 5.54 us: local(): lax.all_to_all(partial_out.reshape(n_tp, quarter, model_width), 'tp', spl...]
    slice x1 -> x0, local copies, waits for them, and re-layouts: 6.77 us -> none  [local(): all_rows = gathered[:, :quarter].reshape(n_req * quarter, model_width)]
    dot_general x1, matrix products: 12.1 us -> 15.5 us  [local(): lax.dot_general(all_rows, head_weight, (((1,), (1,)), ((), ())), preferre...]
    reduce_sum x1, other arithmetic: 1.41 us -> 3.25 us  [vocab_stats(): jnp.sum(jnp.exp(logits - jnp.expand_dims(row_max, along)), axis=along)]
  transfers between devices with their start and end apart: 2 -> 3, of which waited for: 2 -> 3; matrix products, arithmetic and copies ran while one was open for 1% -> 2% of each run, Pallas kernels for 0% -> 0%
where the time goes in v3:
time: 157 us; the launch traced here: 156 us
  waiting for transfers between devices  75.4 us (48%)
  matrix products  26 us (17%)
  between operations  14.5 us (9%)
  blocking collectives  11.5 us (7%)
  starting transfers between devices  11 us (7%)
  other arithmetic  9.34 us (6%)
  local copies, waits for them, and re-layouts  8.37 us (5%)
    all_gather x1, waiting for transfers between devices, local(): lax.all_gather(payload, 'req', axis=0, tiled=True)  53.5 us
    dot_general x1, matrix products, local(): lax.dot_general(all_rows, head_weight, (((1,), (1,)), ((), ())), preferre...  15.5 us
    all_to_all x1, waiting for transfers between devices, local(): lax.all_to_all(partial_out.reshape(n_tp, quarter, model_width), 'tp', spl...  13.6 us
    all_to_all x1, blocking collectives, local(): lax.all_to_all(outgoing, 'tp', split_axis=0, concat_axis=0, tiled=True)  11.5 us
    all_to_all x1, waiting for transfers between devices, local(): lax.all_to_all(jnp.broadcast_to(local_stats[None], (n_req,) + local_stats...  8.24 us
    all_to_all x1, starting transfers between devices, local(): lax.all_to_all(partial_out.reshape(n_tp, quarter, model_width), 'tp', spl...  5.54 us
    all_to_all x1, starting transfers between devices, local(): lax.all_to_all(jnp.broadcast_to(local_stats[None], (n_req,) + local_stats...  5.44 us
    dot_general x1, matrix products, local(): jnp.einsum('rnd,rkd->rnk', spread_q, cache_key, preferred_element_type=jn...  3.56 us
  transfers between devices with their start and end apart: 3, of which 3 were waited for; matrix products, arithmetic and copies ran while one was open for 2% of the time, Pallas kernels for 0%

profile of v3, /device:TPU:0, one launch (start us, length us, event | category | flops | bytes accessed | tf_op | source)
XLA Modules:
  0.0 156.1 jit_solution(7671912278460875458)
XLA Ops:
  7.2 1.0 fusion.21
  8.2 0.9 fusion.22
  9.1 0.2 fusion.41
  9.3 0.2 fusion.40
  9.5 0.2 fusion.42
  9.7 0.1 copy.23
  9.9 0.2 reshape.291
  10.1 0.7 iota_compare_fusion.5
  10.9 1.1 bitcast_select_fusion
  12.0 0.4 fusion.38
  12.4 3.6 %fusion = (f32[2,256]{1,0:T(2,128)S(1)}, f32[2,256,1024]{2,1,0:T(8,128)S(1)}) fusion(pred[2,1024]{1,0:T(4,128)(4,1)S(1)} %iota_compare_fusion.5, bf16[2,256,896]{2,1,0:T(8,128)(2,1)S(1)} %bitcast_select_fusion, bf16[2,1024,896]{2,1,0:T(8,128)(2,1)} %param.18), kind=kOutput, calls=%fused_computation.8 | convolution fusion | flops 941096448 | bytes 6688768 | tf_op jit(solution)/shard_map/rnd,rkd->rnk/dot_general | solution.py:84
  16.1 0.6 fusion.1
  16.7 1.3 fusion.4
  18.0 0.5 add_divide_fusion
  18.5 0.1 select_reduce_fusion.1
  18.7 1.6 %slice-done.1 = s8[4194304]{0:T(1024)(128)(4,1)S(1)} async-done(((s8[6422528]{0:T(1024)(128)(4,1)}), s8[4194304]{0:T(1024)(128)(4,1)S(1)}, s32[]{:S(2)}) %slice-start.1) | async-done | bytes 4194328
  20.3 2.1 %convolution_convert_fusion = bf16[128,3584]{1,0:T(8,128)(2,1)} fusion(bf16[128,896]{1,0:T(8,128)(2,1)S(1)} %bitcast.60, bf16[896,3584]{1,0:T(8,128)(2,1)S(1)} %bitcast.58), kind=kOutput, calls=%fused_computation.4 | convolution fusion | flops 822542336 | bytes 7569408 | tf_op jit(solution)/shard_map/dot_general | solution.py:125
  22.3 5.5 %all-to-all-start = ((bf16[4,32,3584]{2,1,0:T(8,128)(2,1)}), bf16[4,32,3584]{2,1,0:T(8,128)(2,1)S(1)}, u32[]{:S(2)}, u32[]{:S(2)}) async-start(bf16[4,32,3584]{2,1,0:T(8,128)(2,1)} %bitcast.5), calls=%async_computation | async-start | bytes 1835008 | tf_op jit(solution)/shard_map/all_to_all | solution.py:128
  28.0 13.6 %all-to-all-done = bf16[4,32,3584]{2,1,0:T(8,128)(2,1)S(1)} async-done(((bf16[4,32,3584]{2,1,0:T(8,128)(2,1)}), bf16[4,32,3584]{2,1,0:T(8,128)(2,1)S(1)}, u32[]{:S(2)}, u32[]{:S(2)}) %all-to-all-start) | async-done | bytes 917536 | tf_op jit(solution)/shard_map/all_to_all | solution.py:128
  41.6 0.1 convert_reduce_fusion
  41.7 1.1 fusion.10
  42.8 0.1 fusion.12
  43.0 0.2 convolution_convert_fusion.1
  43.2 0.8 pad_maximum_fusion
  44.1 0.1 eq.113
  44.3 0.2 fusion.31
  44.6 53.5 %all-gather.2.cloned.1.call-done = bf16[1280,3584]{1,0:T(8,128)(2,1)} async-done(((bf16[40,3584]{1,0:T(8,128)(2,1)}), bf16[1280,3584]{1,0:T(8,128)(2,1)}) %all-gather.2.cloned.1.call-update) | async-done | bytes 9175056 | tf_op jit(solution)/shard_map/all_gather | solution.py:146
  98.1 15.5 %fusion.39 = (f32[1280]{0:T(1024)S(1)}, f32[1280,1000]{0,1:T(8,128)}) fusion(bf16[1280,3584]{1,0:T(8,128)(2,1)} %all-gather.2.cloned.1.call-done, bf16[1000,3584]{1,0:T(8,128)(2,1)} %param.25), kind=kOutput, calls=%fused_computation.102 | convolution fusion | flops 9176318976 | bytes 21468160 | tf_op jit(solution)/shard_map/dot_general | solution.py:161
  113.7 3.3 %exponential_reduce_fusion = (f32[1280]{0:T(1024)S(1)}, f32[1280]{0:T(1024)S(1)}) fusion(f32[1280,1000]{0,1:T(8,128)} %get-tuple-element.17, f32[1280]{0:T(1024)S(1)} %get-tuple-element.16, s32[1280]{0:T(1024)S(1)} %eq.113, s32[1000]{0:T(1024)S(1)} %iota_add_fusion), kind=kLoop, calls=%fused_computation.3 | loop fusion | flops 6397440 | bytes 5144480 | tf_op jit(solution)/shard_map/reduce_sum | solution.py:47
  117.0 0.1 stack.13
  117.2 0.1 broadcast_in_dim.187
  117.3 0.9 broadcast_in_dim.188
  118.2 5.4 %all-to-all-start.1 = ((f32[32,3,1024]{2,1,0:T(4,128)}), f32[32,3,1024]{2,1,0:T(4,128)S(1)}, u32[]{:S(2)}, u32[]{:S(2)}) async-start(f32[32,3,1024]{2,1,0:T(4,128)} %broadcast_in_dim.188), calls=%async_computation.1 | async-start | bytes 1048576 | tf_op jit(solution)/shard_map/all_to_all | solution.py:167
  123.7 0.1 and.121
  123.8 0.1 broadcast_in_dim.165
  124.0 0.1 broadcast_in_dim.168
  124.1 1.6 %slice.42 = bf16[32,8,3584]{2,1,0:T(8,128)(2,1)S(1)} slice(bf16[32,40,3584]{2,1,0:T(8,128)(2,1)} %bitcast.63), slice={[0:32], [32:40], [0:3584]} | slice | bytes 3670016 | tf_op jit(solution)/shard_map/slice | solution.py:190
  125.7 0.6 gather_fusion
  126.3 0.2 convert_select_fusion
  126.5 8.2 %all-to-all-done.1 = f32[32,3,1024]{2,1,0:T(4,128)S(1)} async-done(((f32[32,3,1024]{2,1,0:T(4,128)}), f32[32,3,1024]{2,1,0:T(4,128)S(1)}, u32[]{:S(2)}, u32[]{:S(2)}) %all-to-all-start.1) | async-done | bytes 393248 | tf_op jit(solution)/shard_map/all_to_all | solution.py:167
  134.7 0.3 slice_reduce_fusion
  135.2 0.6 gather_fusion.1
  135.8 0.1 tile.10
  136.0 0.2 all_to_all.14
  136.2 11.5 %all_to_all.19 = f32[4,1,14464]{2,1,0:T(1,128)S(1)} all-to-all(f32[4,1,14464]{2,1,0:T(1,128)S(1)} %all_to_all.14), channel_id=1, replica_groups=mesh['req'=32,'tp'=4] {'tp'}, dimensions={0} | all-to-all | bytes 462848 | tf_op jit(solution)/shard_map/all_to_all | solution.py:200
  147.7 0.2 reduce_sum.112
  148.0 0.7 convert_element_type.72
  148.6 0.6 reshape.297
  (57 shorter events, 1.3 us)
Async XLA Ops:
  7.2 10.8 %copy-start = (bf16[2,64,896]{2,1,0:T(8,128)(2,1)S(1)}, bf16[2,64,896]{2,1,0:T(8,128)(2,1)}, u32[]{:S(2)}) copy-start(bf16[2,64,896]{2,1,0:T(8,128)(2,1)} %param.17) | copy-start | bytes 688132
  7.2 4.8 %copy-start.2 = (bf16[2,64,896]{2,1,0:T(8,128)(2,1)S(1)}, bf16[2,64,896]{2,1,0:T(8,128)(2,1)}, u32[]{:S(2)}) copy-start(bf16[2,64,896]{2,1,0:T(8,128)(2,1)} %param.16) | copy-start | bytes 688132
  12.4 4.2 %copy-start.1 = (bf16[2,1024,896]{2,1,0:T(8,128)(2,1)S(1)}, bf16[2,1024,896]{2,1,0:T(8,128)(2,1)}, u32[]{:S(2)}) copy-start(bf16[2,1024,896]{2,1,0:T(8,128)(2,1)} %param.19) | copy-start | bytes 11010052
  16.6 2.0 %slice-start = ((s8[6422528]{0:T(1024)(128)(4,1)}), s8[2228224]{0:T(1024)(128)(4,1)S(1)}, s32[]{:S(2)}) async-start(s8[6422528]{0:T(1024)(128)(4,1)} %bitcast.57), calls=%async_computation.4 | async-start | bytes 4456448
  18.0 2.3 %slice-start.1 = ((s8[6422528]{0:T(1024)(128)(4,1)}), s8[4194304]{0:T(1024)(128)(4,1)S(1)}, s32[]{:S(2)}) async-start(s8[6422528]{0:T(1024)(128)(4,1)} %bitcast.57), calls=%async_computation.5 | async-start | bytes 8388608
  22.3 20.5 %copy-start.4 = (f32[3584]{0:T(1024)S(1)}, f32[3584]{0:T(1024)}, u32[]{:S(2)}) copy-start(f32[3584]{0:T(1024)} %param.24) | copy-start | bytes 43012
  22.3 20.6 %copy-start.5 = (s32[2,8,64]{2,1,0:T(8,128)S(1)}, s32[2,8,64]{2,1,0:T(8,128)}, u32[]{:S(2)}) copy-start(s32[2,8,64]{2,1,0:T(8,128)} %param.22) | copy-start | bytes 12292
  22.3 19.2 %all-to-all-start = ((bf16[4,32,3584]{2,1,0:T(8,128)(2,1)}), bf16[4,32,3584]{2,1,0:T(8,128)(2,1)S(1)}, u32[]{:S(2)}, u32[]{:S(2)}) async-start(bf16[4,32,3584]{2,1,0:T(8,128)(2,1)} %bitcast.5), calls=%async_computation | async-start | bytes 1835008 | tf_op jit(solution)/shard_map/all_to_all | solution.py:128
  27.9 16.1 %copy-start.3 = (s32[64,64]{1,0:T(8,128)S(1)}, s32[64,64]{1,0:T(8,128)}, u32[]{:S(2)}) copy-start(s32[64,64]{1,0:T(8,128)} %param.26) | copy-start | bytes 49156
  27.9 16.4 %copy-start.6 = (s32[64]{0:T(128)S(1)}, s32[64]{0:T(128)}, u32[]{:S(2)}) copy-start(s32[64]{0:T(128)} %param.27) | copy-start | bytes 772
  27.9 70.2 %all-gather.2.cloned.1.call-start = ((), (), s32[]{:S(2)}) async-start(), calls=%async_computation.3 | async-start | bytes 9461760 | tf_op jit(solution)/shard_map/all_gather | solution.py:146
  118.2 16.5 %all-to-all-start.1 = ((f32[32,3,1024]{2,1,0:T(4,128)}), f32[32,3,1024]{2,1,0:T(4,128)S(1)}, u32[]{:S(2)}, u32[]{:S(2)}) async-start(f32[32,3,1024]{2,1,0:T(4,128)} %broadcast_in_dim.188), calls=%async_computation.1 | async-start | bytes 1048576 | tf_op jit(solution)/shard_map/all_to_all | solution.py:167
Sparse Core Ops, SparseCore 0:
  44.1 53.9 all-gather.1

commit v4 on v3

--- a/solution.py
+++ b/solution.py
@@ -142,28 +142,20 @@
     picked_rows = jnp.dot(
         accept_own.astype(jnp.bfloat16), post_rows, preferred_element_type=jnp.float32
     ).astype(jnp.bfloat16)
-    payload = jnp.concatenate([normed, picked_rows], axis=0)
-    gathered = lax.all_gather(payload, "req", axis=0, tiled=True).reshape(
-        n_req, quarter + acc_rows, model_width
-    )
-    all_rows = gathered.reshape(n_req * (quarter + acc_rows), model_width)
+    all_rows = lax.all_gather(normed, "req", axis=0, tiled=True)
+    picked_all = lax.all_gather(picked_rows, "req", axis=0, tiled=True).reshape(
+        n_req, acc_rows, model_width
+    )
     vocab_loc = head_weight.shape[0]
-    wanted_rows = jnp.concatenate(
-        [
-            lax.dynamic_slice_in_dim(
-                candidate.reshape(n_req, rows_all), tp_id * quarter, quarter, 1
-            ),
-            jnp.zeros((n_req, acc_rows), candidate.dtype),
-        ],
-        axis=1,
+    wanted_rows = lax.dynamic_slice_in_dim(
+        candidate.reshape(n_req, rows_all), tp_id * quarter, quarter, 1
     ).reshape(-1)
     vocab_ids = req_id * vocab_loc + jnp.arange(vocab_loc, dtype=jnp.int32)
     logits = lax.dot_general(
         all_rows, head_weight, (((1,), (1,)), ((), ())), preferred_element_type=jnp.float32
     )
     row_max, row_sum, picked = vocab_stats(logits, vocab_ids, wanted_rows, 1)
-    local_stats = jnp.stack([row_max, row_sum, picked]).reshape(3, n_req, quarter + acc_rows)
-    local_stats = local_stats[:, :, :quarter].reshape(3, n_req * quarter)
+    local_stats = jnp.stack([row_max, row_sum, picked])
     stats = lax.all_to_all(
         jnp.broadcast_to(local_stats[None], (n_req,) + local_stats.shape),
         "req",
@@ -187,7 +179,7 @@
     lp_full = jnp.where(
         held[:, None] & node_half[None, :], jnp.tile(lp_rows, (1, halves)), 0.0
     )
-    state_rows = jnp.take(gathered[:, quarter:], source, axis=0).astype(jnp.float32)
+    state_rows = jnp.take(picked_all, source, axis=0).astype(jnp.float32)
     state_rows = jnp.where(held[:, None, None], state_rows, 0.0)
     state_parts = state_rows.reshape(slots * acc_rows, n_tp, dslice).transpose(1, 0, 2)
     outgoing = jnp.concatenate(

time: 157 us -> 162 us (1.032)
  waiting for transfers between devices: 75.4 us -> 87.2 us
  matrix products: 26 us -> 23.2 us
  other arithmetic: 9.34 us -> 7.46 us
    all_gather x1 -> x2, waiting for transfers between devices: 53.5 us -> 73.5 us  [the longest x1 48.8 us: local(): all_rows = lax.all_gather(normed, 'req', axis=0, tiled=True)]
    all_to_all x1, waiting for transfers between devices: 8.24 us -> 0.01 us  [local(): lax.all_to_all(jnp.broadcast_to(local_stats[None], (n_req,) + local_stats...]
    dot_general x1, matrix products: 15.5 us -> 12.1 us  [local(): lax.dot_general(all_rows, head_weight, (((1,), (1,)), ((), ())), preferre...]
    reduce_sum x1, other arithmetic: 3.25 us -> 1.4 us  [vocab_stats(): jnp.sum(jnp.exp(logits - jnp.expand_dims(row_max, along)), axis=along)]
  transfers between devices with their start and end apart: 3 -> 4, of which waited for: 3 -> 3; matrix products, arithmetic and copies ran while one was open for 2% -> 11% of each run, Pallas kernels for 0% -> 0%
where the time goes in v4:
time: 162 us
  waiting for transfers between devices  87.2 us (54%)
  matrix products  23.2 us (14%)
  between operations  14.4 us (9%)
  blocking collectives  10.9 us (7%)
  starting transfers between devices  10.6 us (7%)
  local copies, waits for them, and re-layouts  7.98 us (5%)
  other arithmetic  7.46 us (5%)
    all_gather x1, waiting for transfers between devices, local(): all_rows = lax.all_gather(normed, 'req', axis=0, tiled=True)  48.8 us
    all_gather x1, waiting for transfers between devices, local(): lax.all_gather(picked_rows, 'req', axis=0, tiled=True)  24.8 us
    all_to_all x1, waiting for transfers between devices, local(): lax.all_to_all(partial_out.reshape(n_tp, quarter, model_width), 'tp', spl...  13.7 us
    dot_general x1, matrix products, local(): lax.dot_general(all_rows, head_weight, (((1,), (1,)), ((), ())), preferre...  12.1 us
    all_to_all x1, blocking collectives, local(): lax.all_to_all(outgoing, 'tp', split_axis=0, concat_axis=0, tiled=True)  10.9 us
    all_to_all x1, starting transfers between devices, local(): lax.all_to_all(partial_out.reshape(n_tp, quarter, model_width), 'tp', spl...  5.56 us
    all_to_all x1, starting transfers between devices, local(): lax.all_to_all(jnp.broadcast_to(local_stats[None], (n_req,) + local_stats...  5.02 us
    dot_general x1, matrix products, local(): jnp.einsum('rnd,rkd->rnk', spread_q, cache_key, preferred_element_type=jn...  3.59 us
  transfers between devices with their start and end apart: 4, of which 3 were waited for; matrix products, arithmetic and copies ran while one was open for 11% of the time, Pallas kernels for 0%

profile of v4, /device:TPU:0, one launch (start us, length us, event | category | flops | bytes accessed | tf_op | source)
XLA Modules:
  0.0 161.9 jit_solution(8078916401921907731)
XLA Ops:
  7.2 0.8 iota_compare_fusion.5
  8.1 1.0 fusion.21
  9.0 0.2 fusion.41
  9.2 0.9 fusion.22
  10.1 0.2 fusion.40
  10.3 0.2 fusion.42
  10.5 0.1 copy.23
  10.6 0.1 broadcast_in_dim.178
  10.7 0.2 reshape.284
  10.9 1.1 bitcast_select_fusion
  12.1 0.4 fusion.38
  12.5 3.6 %fusion = (f32[2,256]{1,0:T(2,128)S(1)}, f32[2,256,1024]{2,1,0:T(8,128)S(1)}) fusion(pred[2,1024]{1,0:T(4,128)(4,1)S(1)} %iota_compare_fusion.5, bf16[2,256,896]{2,1,0:T(8,128)(2,1)S(1)} %bitcast_select_fusion, bf16[2,1024,896]{2,1,0:T(8,128)(2,1)} %param.18), kind=kOutput, calls=%fused_computation.8 | convolution fusion | flops 941096448 | bytes 6688768 | tf_op jit(solution)/shard_map/rnd,rkd->rnk/dot_general | solution.py:84
  16.1 0.6 fusion.1
  16.7 1.3 fusion.4
  18.1 0.5 add_divide_fusion
  18.6 0.1 select_reduce_fusion.1
  18.7 1.6 %slice-done.1 = s8[4194304]{0:T(1024)(128)(4,1)S(1)} async-done(((s8[6422528]{0:T(1024)(128)(4,1)}), s8[4194304]{0:T(1024)(128)(4,1)S(1)}, s32[]{:S(2)}) %slice-start.1) | async-done | bytes 4194328
  20.4 2.1 %convolution_convert_fusion = bf16[128,3584]{1,0:T(8,128)(2,1)} fusion(bf16[128,896]{1,0:T(8,128)(2,1)S(1)} %bitcast.64, bf16[896,3584]{1,0:T(8,128)(2,1)S(1)} %bitcast.62), kind=kOutput, calls=%fused_computation.2 | convolution fusion | flops 822542336 | bytes 7569408 | tf_op jit(solution)/shard_map/dot_general | solution.py:125
  22.5 5.6 %all-to-all-start = ((bf16[4,32,3584]{2,1,0:T(8,128)(2,1)}), bf16[4,32,3584]{2,1,0:T(8,128)(2,1)S(1)}, u32[]{:S(2)}, u32[]{:S(2)}) async-start(bf16[4,32,3584]{2,1,0:T(8,128)(2,1)} %bitcast.6), calls=%async_computation | async-start | bytes 1835008 | tf_op jit(solution)/shard_map/all_to_all | solution.py:128
  28.0 13.7 %all-to-all-done = bf16[4,32,3584]{2,1,0:T(8,128)(2,1)S(1)} async-done(((bf16[4,32,3584]{2,1,0:T(8,128)(2,1)}), bf16[4,32,3584]{2,1,0:T(8,128)(2,1)S(1)}, u32[]{:S(2)}, u32[]{:S(2)}) %all-to-all-start) | async-done | bytes 917536 | tf_op jit(solution)/shard_map/all_to_all | solution.py:128
  41.7 0.1 convert_reduce_fusion
  41.9 1.1 fusion.10
  43.0 0.8 fusion.12
  44.0 0.8 convolution_convert_fusion.1
  44.9 0.1 constant_dynamic-slice_fusion
  45.1 0.2 fusion.31
  45.3 0.1 broadcast_and_fusion
  45.3 48.8 %all-gather.5.cloned.1.call-done = bf16[1024,3584]{1,0:T(8,128)(2,1)} async-done(((bf16[32,3584]{1,0:T(8,128)(2,1)}), bf16[1024,3584]{1,0:T(8,128)(2,1)}) %all-gather.5.cloned.1.call-update) | async-done | bytes 7340048 | tf_op jit(solution)/shard_map/all_gather | solution.py:145
  94.1 12.1 %fusion.39 = (f32[1024]{0:T(1024)S(1)}, f32[1024,1000]{0,1:T(8,128)S(1)}) fusion(bf16[1024,3584]{1,0:T(8,128)(2,1)} %all-gather.5.cloned.1.call-done, bf16[1000,3584]{1,0:T(8,128)(2,1)} %param.25), kind=kOutput, calls=%fused_computation.101 | convolution fusion | flops 7341054976 | bytes 18608128 | tf_op jit(solution)/shard_map/dot_general | solution.py:154
  106.2 1.4 exponential_reduce_fusion
  107.6 0.9 broadcast_in_dim.185
  108.5 5.0 %all-to-all-start.1 = ((f32[32,3,1024]{2,1,0:T(4,128)}), f32[32,3,1024]{2,1,0:T(4,128)S(1)}, u32[]{:S(2)}, u32[]{:S(2)}) async-start(f32[32,3,1024]{2,1,0:T(4,128)} %broadcast_in_dim.185), calls=%async_computation.1 | async-start | bytes 1048576 | tf_op jit(solution)/shard_map/all_to_all | solution.py:159
  113.6 0.1 broadcast_in_dim.163
  113.7 0.1 and.121
  113.9 0.1 broadcast_in_dim.166
  114.0 24.8 %all-gather.3.cloned.1.call-done = bf16[256,3584]{1,0:T(8,128)(2,1)} async-done(((bf16[8,3584]{1,0:T(8,128)(2,1)}), bf16[256,3584]{1,0:T(8,128)(2,1)}) %all-gather.3.cloned.1.call-update) | async-done | bytes 1835024 | tf_op jit(solution)/shard_map/all_gather | solution.py:146
  138.7 2.1 %gather_fusion = bf16[2,8,3584]{2,1,0:T(8,128)(2,1)S(1)} fusion(bf16[32,8,3584]{2,1,0:T(8,128)(2,1)} %bitcast.71, s32[1024]{0:T(1024)S(1)} %pad_clamp_fusion), kind=kCustom, calls=%fused_computation | custom fusion | bytes 229384 | tf_op jit(solution)/shard_map/jit(_take)/gather | solution.py:182
  140.8 0.1 select_bitcast_fusion
  140.9 0.1 copy.31
  141.0 0.3 slice_reduce_fusion
  141.5 0.6 gather_fusion.1
  142.2 0.1 tile.10
  142.3 0.1 pad_maximum_fusion
  142.4 0.2 all_to_all.14
  142.5 10.9 %all_to_all.19 = f32[4,1,14464]{2,1,0:T(1,128)S(1)} all-to-all(f32[4,1,14464]{2,1,0:T(1,128)S(1)} %all_to_all.14), channel_id=1, replica_groups=mesh['req'=32,'tp'=4] {'tp'}, dimensions={0} | all-to-all | bytes 462848 | tf_op jit(solution)/shard_map/all_to_all | solution.py:192
  153.5 0.2 reduce_sum.112
  153.7 0.7 convert_element_type.72
  154.4 0.6 reshape.290
  (54 shorter events, 1.0 us)
Async XLA Ops:
  7.2 10.9 %copy-start = (bf16[2,64,896]{2,1,0:T(8,128)(2,1)S(1)}, bf16[2,64,896]{2,1,0:T(8,128)(2,1)}, u32[]{:S(2)}) copy-start(bf16[2,64,896]{2,1,0:T(8,128)(2,1)} %param.17) | copy-start | bytes 688132
  7.2 4.9 %copy-start.2 = (bf16[2,64,896]{2,1,0:T(8,128)(2,1)S(1)}, bf16[2,64,896]{2,1,0:T(8,128)(2,1)}, u32[]{:S(2)}) copy-start(bf16[2,64,896]{2,1,0:T(8,128)(2,1)} %param.16) | copy-start | bytes 688132
  12.5 4.2 %copy-start.1 = (bf16[2,1024,896]{2,1,0:T(8,128)(2,1)S(1)}, bf16[2,1024,896]{2,1,0:T(8,128)(2,1)}, u32[]{:S(2)}) copy-start(bf16[2,1024,896]{2,1,0:T(8,128)(2,1)} %param.19) | copy-start | bytes 11010052
  16.7 2.0 %slice-start = ((s8[6422528]{0:T(1024)(128)(4,1)}), s8[2228224]{0:T(1024)(128)(4,1)S(1)}, s32[]{:S(2)}) async-start(s8[6422528]{0:T(1024)(128)(4,1)} %bitcast.61), calls=%async_computation.5 | async-start | bytes 4456448
  18.1 2.3 %slice-start.1 = ((s8[6422528]{0:T(1024)(128)(4,1)}), s8[4194304]{0:T(1024)(128)(4,1)S(1)}, s32[]{:S(2)}) async-start(s8[6422528]{0:T(1024)(128)(4,1)} %bitcast.61), calls=%async_computation.6 | async-start | bytes 8388608
  22.5 20.5 %copy-start.4 = (f32[3584]{0:T(1024)S(1)}, f32[3584]{0:T(1024)}, u32[]{:S(2)}) copy-start(f32[3584]{0:T(1024)} %param.24) | copy-start | bytes 43012
  22.5 21.5 %copy-start.3 = (s32[64,64]{1,0:T(8,128)S(1)}, s32[64,64]{1,0:T(8,128)}, u32[]{:S(2)}) copy-start(s32[64,64]{1,0:T(8,128)} %param.26) | copy-start | bytes 49156
  22.5 21.5 %copy-start.5 = (s32[2,8,64]{2,1,0:T(8,128)S(1)}, s32[2,8,64]{2,1,0:T(8,128)}, u32[]{:S(2)}) copy-start(s32[2,8,64]{2,1,0:T(8,128)} %param.22) | copy-start | bytes 12292
  22.5 19.2 %all-to-all-start = ((bf16[4,32,3584]{2,1,0:T(8,128)(2,1)}), bf16[4,32,3584]{2,1,0:T(8,128)(2,1)S(1)}, u32[]{:S(2)}, u32[]{:S(2)}) async-start(bf16[4,32,3584]{2,1,0:T(8,128)(2,1)} %bitcast.6), calls=%async_computation | async-start | bytes 1835008 | tf_op jit(solution)/shard_map/all_to_all | solution.py:128
  28.0 17.0 %copy-start.6 = (s32[64]{0:T(128)S(1)}, s32[64]{0:T(128)}, u32[]{:S(2)}) copy-start(s32[64]{0:T(128)} %param.27) | copy-start | bytes 772
  28.0 66.1 %all-gather.5.cloned.1.call-start = ((), (), s32[]{:S(2)}) async-start(), calls=%async_computation.4 | async-start | bytes 7569408 | tf_op jit(solution)/shard_map/all_gather | solution.py:145
  43.8 94.9 %all-gather.3.cloned.1.call-start = ((), (), s32[]{:S(2)}) async-start(), calls=%async_computation.3 | async-start | bytes 1892352 | tf_op jit(solution)/shard_map/all_gather | solution.py:146
  108.5 32.5 %all-to-all-start.1 = ((f32[32,3,1024]{2,1,0:T(4,128)}), f32[32,3,1024]{2,1,0:T(4,128)S(1)}, u32[]{:S(2)}, u32[]{:S(2)}) async-start(f32[32,3,1024]{2,1,0:T(4,128)} %broadcast_in_dim.185), calls=%async_computation.1 | async-start | bytes 1048576 | tf_op jit(solution)/shard_map/all_to_all | solution.py:159
Sparse Core Ops, SparseCore 0:
  44.0 50.1 all-gather.4
  96.4 42.3 all-gather.2

commit v5 on v3

--- a/solution.py
+++ b/solution.py
@@ -161,48 +161,48 @@
     logits = lax.dot_general(
         all_rows, head_weight, (((1,), (1,)), ((), ())), preferred_element_type=jnp.float32
     )
+    n_slots = dealing.shape[0]
+    slot_ids = jnp.arange(n_slots, dtype=jnp.int32)
+    serving_all = jnp.sum(
+        jnp.where(dealing[None, :] == slot_ids[:, None], slot_ids[None, :], 0), axis=1
+    )
+    own_serving = lax.dynamic_slice_in_dim(serving_all, req_id * slots, slots, 0)
+    held = (own_serving % slots) == own_slot
+    state_rows = jnp.take(gathered[:, quarter:], own_serving // slots, axis=0)
+    state_rows = jnp.where(held[:, None, None], state_rows, jnp.zeros((), state_rows.dtype))
+    state_parts = state_rows.reshape(slots * acc_rows, n_tp, dslice).transpose(1, 0, 2)
+    state_in = lax.all_to_all(state_parts, "tp", split_axis=0, concat_axis=0, tiled=True)
+    accepted_state = (
+        jnp.sum(state_in.astype(jnp.float32), axis=0)
+        .reshape(slots, acc_rows, dslice)
+        .astype(jnp.bfloat16)
+    )
     row_max, row_sum, picked = vocab_stats(logits, vocab_ids, wanted_rows, 1)
     local_stats = jnp.stack([row_max, row_sum, picked]).reshape(3, n_req, quarter + acc_rows)
-    local_stats = local_stats[:, :, :quarter].reshape(3, n_req * quarter)
-    stats = lax.all_to_all(
-        jnp.broadcast_to(local_stats[None], (n_req,) + local_stats.shape),
-        "req",
-        split_axis=0,
-        concat_axis=0,
-        tiled=True,
-    )
-    joint_max = jnp.max(stats[:, 0], axis=0)
-    joint_sum = jnp.sum(stats[:, 1] * jnp.exp(stats[:, 0] - joint_max[None]), axis=0)
-    joint_pick = jnp.sum(stats[:, 2], axis=0)
-    plane_logprob = (joint_pick - joint_max - jnp.log(joint_sum)).reshape(n_req, quarter)
-    own_requests = req_id * slots + jnp.arange(slots, dtype=jnp.int32)
-    slot_ids = jnp.arange(dealing.shape[0], dtype=jnp.int32)
-    serving = jnp.sum(
-        jnp.where(dealing[None, :] == own_requests[:, None], slot_ids[None, :], 0), axis=1
-    )
-    source = serving // slots
-    held = (serving % slots) == own_slot
-    lp_rows = jnp.take(plane_logprob, source, axis=0)
-    node_half = jnp.arange(tree_size, dtype=jnp.int32) // quarter == tp_id % halves
-    lp_full = jnp.where(
-        held[:, None] & node_half[None, :], jnp.tile(lp_rows, (1, halves)), 0.0
-    )
-    state_rows = jnp.take(gathered[:, quarter:], source, axis=0).astype(jnp.float32)
-    state_rows = jnp.where(held[:, None, None], state_rows, 0.0)
-    state_parts = state_rows.reshape(slots * acc_rows, n_tp, dslice).transpose(1, 0, 2)
-    outgoing = jnp.concatenate(
+    local_stats = local_stats[:, :, :quarter].transpose(1, 0, 2)
+    dest_blocks = (serving_all // slots).reshape(n_req, 1, slots)
+    dest_blocks = jnp.broadcast_to(dest_blocks, (n_req, n_tp, slots)).reshape(-1)
+    outgoing = jnp.take(local_stats, dest_blocks, axis=0).reshape(
+        n_req * n_tp, slots, 3, quarter
+    )
+    incoming = lax.all_to_all(
+        outgoing, ("req", "tp"), split_axis=0, concat_axis=0, tiled=True
+    ).reshape(n_req, n_tp, slots, 3, quarter)
+    plane_of = (own_serving % slots)[:, None] * halves + jnp.arange(halves, dtype=jnp.int32)[None, :]
+    chosen = jnp.stack(
         [
-            state_parts.reshape(n_tp, slots * acc_rows * dslice),
-            jnp.broadcast_to(lp_full.reshape(1, -1), (n_tp, slots * tree_size)),
+            jnp.stack(
+                [jnp.take(incoming[:, :, i], plane_of[i, h], axis=1) for h in range(halves)],
+                axis=1,
+            )
+            for i in range(slots)
         ],
         axis=1,
     )
-    incoming = lax.all_to_all(outgoing, "tp", split_axis=0, concat_axis=0, tiled=True)
-    merged = jnp.sum(incoming, axis=0)
-    accepted_state = (
-        merged[: slots * acc_rows * dslice].reshape(slots, acc_rows, dslice).astype(jnp.bfloat16)
-    )
-    target_logprob = merged[slots * acc_rows * dslice :].reshape(slots, tree_size)
+    joint_max = jnp.max(chosen[:, :, :, 0], axis=0)
+    joint_sum = jnp.sum(chosen[:, :, :, 1] * jnp.exp(chosen[:, :, :, 0] - joint_max[None]), axis=0)
+    joint_pick = jnp.sum(chosen[:, :, :, 2], axis=0)
+    target_logprob = (joint_pick - joint_max - jnp.log(joint_sum)).reshape(slots, tree_size)
     return (target_logprob, accepted_state)
 
 

time: 157 us -> 157 us (level)
  blocking collectives: 11.5 us -> 0 us
  between operations: 14.5 us -> 22.1 us
  starting transfers between devices: 11 us -> 16.3 us
  waiting for transfers between devices: 75.4 us -> 70.2 us
  local copies, waits for them, and re-layouts: 8.37 us -> 10.2 us
    all_to_all x1 -> x0, blocking collectives: 11.5 us -> none  [local(): lax.all_to_all(outgoing, 'tp', split_axis=0, concat_axis=0, tiled=True)]
    all_to_all x1 -> x2, starting transfers between devices: 5.44 us -> 10.7 us  [the longest x1 6.34 us: local(): lax.all_to_all(outgoing, ('req', 'tp'), split_axis=0, concat_axis=0, tile...]
    all_to_all x1 -> x2, waiting for transfers between devices: 8.24 us -> 3.74 us  [the longest x1 3.46 us: local(): lax.all_to_all(state_parts, 'tp', split_axis=0, concat_axis=0, tiled=True)]
  transfers between devices with their start and end apart: 3 -> 4, of which waited for: 3 -> 4; matrix products, arithmetic and copies ran while one was open for 2% -> 3% of each run, Pallas kernels for 0% -> 0%
where the time goes in v5:
time: 157 us; the launch traced here: 156 us
  waiting for transfers between devices  70.2 us (45%)
  matrix products  26 us (17%)
  between operations  22.1 us (14%)
  starting transfers between devices  16.3 us (10%)
  other arithmetic  10.8 us (7%)
  local copies, waits for them, and re-layouts  10.2 us (6%)
    all_gather x1, waiting for transfers between devices, local(): lax.all_gather(payload, 'req', axis=0, tiled=True)  52.8 us
    dot_general x1, matrix products, local(): lax.dot_general(all_rows, head_weight, (((1,), (1,)), ((), ())), preferre...  15.5 us
    all_to_all x1, waiting for transfers between devices, local(): lax.all_to_all(partial_out.reshape(n_tp, quarter, model_width), 'tp', spl...  13.6 us
    all_to_all x1, starting transfers between devices, local(): lax.all_to_all(outgoing, ('req', 'tp'), split_axis=0, concat_axis=0, tile...  6.34 us
    all_to_all x1, starting transfers between devices, local(): lax.all_to_all(partial_out.reshape(n_tp, quarter, model_width), 'tp', spl...  5.54 us
    all_to_all x1, starting transfers between devices, local(): lax.all_to_all(state_parts, 'tp', split_axis=0, concat_axis=0, tiled=True)  4.4 us
    dot_general x1, matrix products, local(): jnp.einsum('rnd,rkd->rnk', spread_q, cache_key, preferred_element_type=jn...  3.56 us
    all_to_all x1, waiting for transfers between devices, local(): lax.all_to_all(state_parts, 'tp', split_axis=0, concat_axis=0, tiled=True)  3.46 us
  transfers between devices with their start and end apart: 4, of which 4 were waited for; matrix products, arithmetic and copies ran while one was open for 3% of the time, Pallas kernels for 0%

profile of v5, /device:TPU:0, one launch (start us, length us, event | category | flops | bytes accessed | tf_op | source)
XLA Modules:
  0.0 155.7 jit_solution(9285138842036555557)
XLA Ops:
  7.2 1.0 fusion.25
  8.2 0.9 fusion.26
  9.1 0.2 fusion.46
  9.3 0.2 fusion.45
  9.5 0.2 fusion.47
  9.7 0.1 copy.45
  9.9 0.2 reshape.213
  10.1 0.7 iota_compare_fusion.6
  10.9 1.1 bitcast_select_fusion
  12.0 0.4 fusion.42
  12.4 3.6 %fusion = (f32[2,256]{1,0:T(2,128)S(1)}, f32[2,256,1024]{2,1,0:T(8,128)S(1)}) fusion(pred[2,1024]{1,0:T(4,128)(4,1)S(1)} %iota_compare_fusion.6, bf16[2,256,896]{2,1,0:T(8,128)(2,1)S(1)} %bitcast_select_fusion, bf16[2,1024,896]{2,1,0:T(8,128)(2,1)} %param.20), kind=kOutput, calls=%fused_computation.8 | convolution fusion | flops 941096448 | bytes 6688768 | tf_op jit(solution)/shard_map/rnd,rkd->rnk/dot_general | solution.py:84
  16.1 0.6 fusion.1
  16.7 1.3 fusion.4
  18.0 0.5 add_divide_fusion
  18.5 0.1 select_reduce_fusion.1
  18.7 1.6 %slice-done.1 = s8[4194304]{0:T(1024)(128)(4,1)S(1)} async-done(((s8[6422528]{0:T(1024)(128)(4,1)}), s8[4194304]{0:T(1024)(128)(4,1)S(1)}, s32[]{:S(2)}) %slice-start.1) | async-done | bytes 4194328
  20.3 2.1 %convolution_convert_fusion = bf16[128,3584]{1,0:T(8,128)(2,1)} fusion(bf16[128,896]{1,0:T(8,128)(2,1)S(1)} %bitcast.80, bf16[896,3584]{1,0:T(8,128)(2,1)S(1)} %bitcast.77), kind=kOutput, calls=%fused_computation.4 | convolution fusion | flops 822542336 | bytes 7569408 | tf_op jit(solution)/shard_map/dot_general | solution.py:125
  22.3 5.5 %all-to-all-start = ((bf16[4,32,3584]{2,1,0:T(8,128)(2,1)}), bf16[4,32,3584]{2,1,0:T(8,128)(2,1)S(1)}, u32[]{:S(2)}, u32[]{:S(2)}) async-start(bf16[4,32,3584]{2,1,0:T(8,128)(2,1)} %bitcast.7), calls=%async_computation | async-start | bytes 1835008 | tf_op jit(solution)/shard_map/all_to_all | solution.py:128
  28.0 13.6 %all-to-all-done = bf16[4,32,3584]{2,1,0:T(8,128)(2,1)S(1)} async-done(((bf16[4,32,3584]{2,1,0:T(8,128)(2,1)}), bf16[4,32,3584]{2,1,0:T(8,128)(2,1)S(1)}, u32[]{:S(2)}, u32[]{:S(2)}) %all-to-all-start) | async-done | bytes 917536 | tf_op jit(solution)/shard_map/all_to_all | solution.py:128
  41.6 0.1 convert_reduce_fusion
  41.7 1.1 fusion.10
  42.8 0.1 fusion.12
  43.0 0.2 convolution_convert_fusion.1
  43.2 0.8 pad_maximum_fusion
  44.2 0.1 select_reduce_fusion.2
  44.4 0.1 reduce_sum.105
  44.5 0.1 reshape.217
  45.3 52.8 %all-gather.2.cloned.1.call-done = bf16[1280,3584]{1,0:T(8,128)(2,1)} async-done(((bf16[40,3584]{1,0:T(8,128)(2,1)}), bf16[1280,3584]{1,0:T(8,128)(2,1)}) %all-gather.2.cloned.1.call-update) | async-done | bytes 9175056 | tf_op jit(solution)/shard_map/all_gather | solution.py:146
  98.1 15.5 %fusion.43 = (f32[1280]{0:T(1024)S(1)}, f32[1280,1000]{0,1:T(8,128)}) fusion(bf16[1280,3584]{1,0:T(8,128)(2,1)} %all-gather.2.cloned.1.call-done, bf16[1000,3584]{1,0:T(8,128)(2,1)} %param.27), kind=kOutput, calls=%fused_computation.117 | convolution fusion | flops 9176318976 | bytes 21468160 | tf_op jit(solution)/shard_map/dot_general | solution.py:161
  113.7 3.2 %exponential_reduce_fusion = (f32[1280]{0:T(1024)S(1)}, f32[1280]{0:T(1024)S(1)}) fusion(f32[1280,1000]{0,1:T(8,128)} %get-tuple-element.37, f32[1280]{0:T(1024)S(1)} %get-tuple-element.36, s32[1280]{0:T(1024)S(1)} %eq.91, s32[1000]{0:T(1024)S(1)} %iota_add_fusion), kind=kLoop, calls=%fused_computation.3 | loop fusion | flops 6397440 | bytes 5144480 | tf_op jit(solution)/shard_map/reduce_sum | solution.py:47
  117.2 1.6 %slice.68 = bf16[32,8,3584]{2,1,0:T(8,128)(2,1)S(1)} slice(bf16[32,40,3584]{2,1,0:T(8,128)(2,1)} %bitcast.86), slice={[0:32], [32:40], [0:3584]} | slice | bytes 3670016 | tf_op jit(solution)/shard_map/slice | solution.py:171
  118.8 0.6 gather_fusion.1
  119.4 0.1 select_bitcast_fusion
  119.6 0.7 copy.51
  120.2 4.4 %all-to-all-start.2 = ((bf16[4,16,896]{2,1,0:T(8,128)(2,1)}), bf16[4,16,896]{2,1,0:T(8,128)(2,1)S(1)}, u32[]{:S(2)}, u32[]{:S(2)}) async-start(bf16[4,16,896]{2,1,0:T(8,128)(2,1)} %copy.51), calls=%async_computation.2 | async-start | bytes 229376 | tf_op jit(solution)/shard_map/all_to_all | solution.py:174
  124.7 1.0 gather_fusion
  125.7 0.3 fusion.44
  126.0 1.1 reshape.334
  127.0 3.5 %all-to-all-done.2 = bf16[4,16,896]{2,1,0:T(8,128)(2,1)S(1)} async-done(((bf16[4,16,896]{2,1,0:T(8,128)(2,1)}), bf16[4,16,896]{2,1,0:T(8,128)(2,1)S(1)}, u32[]{:S(2)}, u32[]{:S(2)}) %all-to-all-start.2) | async-done | bytes 114720 | tf_op jit(solution)/shard_map/all_to_all | solution.py:174
  130.5 6.3 %all-to-all-start.1 = ((f32[128,1,192]{2,1,0:T(1,128)}), f32[128,1,192]{2,1,0:T(1,128)S(1)}, u32[]{:S(2)}, u32[]{:S(2)}) async-start(f32[128,1,192]{2,1,0:T(1,128)} %reshape.334), calls=%async_computation.1 | async-start | bytes 262144 | tf_op jit(solution)/shard_map/all_to_all | solution.py:188
  136.9 0.7 fusion.41
  145.1 0.6 reduce_sum.115
  145.8 0.3 all-to-all-done.1
  146.0 0.5 broadcast.280
  146.6 1.0 reduce.3
  147.5 0.3 reshape.335
  147.9 0.1 constant_dynamic-slice_fusion
  148.2 0.6 sub.79
  (65 shorter events, 1.9 us)
Async XLA Ops:
  7.2 10.8 %copy-start = (bf16[2,64,896]{2,1,0:T(8,128)(2,1)S(1)}, bf16[2,64,896]{2,1,0:T(8,128)(2,1)}, u32[]{:S(2)}) copy-start(bf16[2,64,896]{2,1,0:T(8,128)(2,1)} %param.19) | copy-start | bytes 688132
  7.2 4.8 %copy-start.2 = (bf16[2,64,896]{2,1,0:T(8,128)(2,1)S(1)}, bf16[2,64,896]{2,1,0:T(8,128)(2,1)}, u32[]{:S(2)}) copy-start(bf16[2,64,896]{2,1,0:T(8,128)(2,1)} %param.18) | copy-start | bytes 688132
  12.4 4.2 %copy-start.1 = (bf16[2,1024,896]{2,1,0:T(8,128)(2,1)S(1)}, bf16[2,1024,896]{2,1,0:T(8,128)(2,1)}, u32[]{:S(2)}) copy-start(bf16[2,1024,896]{2,1,0:T(8,128)(2,1)} %param.21) | copy-start | bytes 11010052
  16.6 2.0 %slice-start = ((s8[6422528]{0:T(1024)(128)(4,1)}), s8[2228224]{0:T(1024)(128)(4,1)S(1)}, s32[]{:S(2)}) async-start(s8[6422528]{0:T(1024)(128)(4,1)} %bitcast.76), calls=%async_computation.4 | async-start | bytes 4456448
  18.0 2.3 %slice-start.1 = ((s8[6422528]{0:T(1024)(128)(4,1)}), s8[4194304]{0:T(1024)(128)(4,1)S(1)}, s32[]{:S(2)}) async-start(s8[6422528]{0:T(1024)(128)(4,1)} %bitcast.76), calls=%async_computation.5 | async-start | bytes 8388608
  22.3 20.5 %copy-start.4 = (f32[3584]{0:T(1024)S(1)}, f32[3584]{0:T(1024)}, u32[]{:S(2)}) copy-start(f32[3584]{0:T(1024)} %param.26) | copy-start | bytes 43012
  22.3 20.6 %copy-start.5 = (s32[2,8,64]{2,1,0:T(8,128)S(1)}, s32[2,8,64]{2,1,0:T(8,128)}, u32[]{:S(2)}) copy-start(s32[2,8,64]{2,1,0:T(8,128)} %param.24) | copy-start | bytes 12292
  22.3 19.2 %all-to-all-start = ((bf16[4,32,3584]{2,1,0:T(8,128)(2,1)}), bf16[4,32,3584]{2,1,0:T(8,128)(2,1)S(1)}, u32[]{:S(2)}, u32[]{:S(2)}) async-start(bf16[4,32,3584]{2,1,0:T(8,128)(2,1)} %bitcast.7), calls=%async_computation | async-start | bytes 1835008 | tf_op jit(solution)/shard_map/all_to_all | solution.py:128
  27.9 16.1 %copy-start.3 = (s32[64,64]{1,0:T(8,128)S(1)}, s32[64,64]{1,0:T(8,128)}, u32[]{:S(2)}) copy-start(s32[64,64]{1,0:T(8,128)} %param.28) | copy-start | bytes 49156
  27.9 16.4 %copy-start.6 = (s32[64]{0:T(128)S(1)}, s32[64]{0:T(128)}, u32[]{:S(2)}) copy-start(s32[64]{0:T(128)} %param.29) | copy-start | bytes 772
  27.9 70.2 %all-gather.2.cloned.1.call-start = ((), (), s32[]{:S(2)}) async-start(), calls=%async_computation.3 | async-start | bytes 9461760 | tf_op jit(solution)/shard_map/all_gather | solution.py:146
  120.2 10.3 %all-to-all-start.2 = ((bf16[4,16,896]{2,1,0:T(8,128)(2,1)}), bf16[4,16,896]{2,1,0:T(8,128)(2,1)S(1)}, u32[]{:S(2)}, u32[]{:S(2)}) async-start(bf16[4,16,896]{2,1,0:T(8,128)(2,1)} %copy.51), calls=%async_computation.2 | async-start | bytes 229376 | tf_op jit(solution)/shard_map/all_to_all | solution.py:174
  130.5 15.5 %all-to-all-start.1 = ((f32[128,1,192]{2,1,0:T(1,128)}), f32[128,1,192]{2,1,0:T(1,128)S(1)}, u32[]{:S(2)}, u32[]{:S(2)}) async-start(f32[128,1,192]{2,1,0:T(1,128)} %reshape.334), calls=%async_computation.1 | async-start | bytes 262144 | tf_op jit(solution)/shard_map/all_to_all | solution.py:188
Sparse Core Ops, SparseCore 0:
  44.1 53.9 all-gather.1

commit v6 on v5

--- a/solution.py
+++ b/solution.py
@@ -142,44 +142,48 @@
     picked_rows = jnp.dot(
         accept_own.astype(jnp.bfloat16), post_rows, preferred_element_type=jnp.float32
     ).astype(jnp.bfloat16)
-    payload = jnp.concatenate([normed, picked_rows], axis=0)
-    gathered = lax.all_gather(payload, "req", axis=0, tiled=True).reshape(
-        n_req, quarter + acc_rows, model_width
-    )
-    all_rows = gathered.reshape(n_req * (quarter + acc_rows), model_width)
+    n_slots = dealing.shape[0]
+    global_slot = req_id * slots + own_slot
+    owner = lax.dynamic_index_in_dim(dealing, global_slot, 0, keepdims=False) // slots
+    dest_req = jnp.arange(n_req * n_tp, dtype=jnp.int32) // n_tp
+    picked_parts = picked_rows.reshape(acc_rows, n_tp, dslice).transpose(1, 0, 2)
+    picked_out = jnp.where(
+        (dest_req == owner)[:, None, None],
+        jnp.tile(picked_parts, (n_req, 1, 1)),
+        jnp.zeros((), picked_parts.dtype),
+    )
+    picked_in = lax.all_to_all(
+        picked_out, ("req", "tp"), split_axis=0, concat_axis=0, tiled=True
+    )
+    all_rows = lax.all_gather(normed, "req", axis=0, tiled=True)
     vocab_loc = head_weight.shape[0]
-    wanted_rows = jnp.concatenate(
-        [
-            lax.dynamic_slice_in_dim(
-                candidate.reshape(n_req, rows_all), tp_id * quarter, quarter, 1
-            ),
-            jnp.zeros((n_req, acc_rows), candidate.dtype),
-        ],
-        axis=1,
+    wanted_rows = lax.dynamic_slice_in_dim(
+        candidate.reshape(n_req, rows_all), tp_id * quarter, quarter, 1
     ).reshape(-1)
     vocab_ids = req_id * vocab_loc + jnp.arange(vocab_loc, dtype=jnp.int32)
     logits = lax.dot_general(
         all_rows, head_weight, (((1,), (1,)), ((), ())), preferred_element_type=jnp.float32
     )
-    n_slots = dealing.shape[0]
     slot_ids = jnp.arange(n_slots, dtype=jnp.int32)
     serving_all = jnp.sum(
         jnp.where(dealing[None, :] == slot_ids[:, None], slot_ids[None, :], 0), axis=1
     )
     own_serving = lax.dynamic_slice_in_dim(serving_all, req_id * slots, slots, 0)
-    held = (own_serving % slots) == own_slot
-    state_rows = jnp.take(gathered[:, quarter:], own_serving // slots, axis=0)
-    state_rows = jnp.where(held[:, None, None], state_rows, jnp.zeros((), state_rows.dtype))
-    state_parts = state_rows.reshape(slots * acc_rows, n_tp, dslice).transpose(1, 0, 2)
-    state_in = lax.all_to_all(state_parts, "tp", split_axis=0, concat_axis=0, tiled=True)
-    accepted_state = (
-        jnp.sum(state_in.astype(jnp.float32), axis=0)
-        .reshape(slots, acc_rows, dslice)
-        .astype(jnp.bfloat16)
-    )
+    source_slot = (
+        jnp.arange(n_req * n_tp, dtype=jnp.int32) // n_tp * slots
+        + jnp.arange(n_req * n_tp, dtype=jnp.int32) % n_tp // halves
+    )
+    source_request = jnp.take(dealing, source_slot)
+    routed = (source_request[None, :] == (req_id * slots + jnp.arange(slots, dtype=jnp.int32))[:, None])
+    accepted_state = jnp.einsum(
+        "ks,sad->kad",
+        routed.astype(jnp.bfloat16),
+        picked_in,
+        preferred_element_type=jnp.float32,
+    ).astype(jnp.bfloat16)
     row_max, row_sum, picked = vocab_stats(logits, vocab_ids, wanted_rows, 1)
-    local_stats = jnp.stack([row_max, row_sum, picked]).reshape(3, n_req, quarter + acc_rows)
-    local_stats = local_stats[:, :, :quarter].transpose(1, 0, 2)
+    local_stats = jnp.stack([row_max, row_sum, picked]).reshape(3, n_req, quarter)
+    local_stats = local_stats.transpose(1, 0, 2)
     dest_blocks = (serving_all // slots).reshape(n_req, 1, slots)
     dest_blocks = jnp.broadcast_to(dest_blocks, (n_req, n_tp, slots)).reshape(-1)
     outgoing = jnp.take(local_stats, dest_blocks, axis=0).reshape(

time: 157 us -> 154 us (0.981)
  waiting for transfers between devices: 70.2 us -> 60.3 us
  starting transfers between devices: 16.3 us -> 22.7 us
  between operations: 22.1 us -> 24.8 us
  matrix products: 26 us -> 24.4 us
    all_gather x1, waiting for transfers between devices: 52.8 us -> 38.5 us  [local(): all_rows = lax.all_gather(normed, 'req', axis=0, tiled=True)]
    all_to_all x1, waiting for transfers between devices: 0.28 us -> 8.14 us  [local(): lax.all_to_all(outgoing, ('req', 'tp'), split_axis=0, concat_axis=0, tile...]
    all_to_all x1, starting transfers between devices: 4.4 us -> 8.36 us  [local(): lax.all_to_all(picked_out, ('req', 'tp'), split_axis=0, concat_axis=0, ti...]
    all_to_all x1, waiting for transfers between devices: 3.46 us -> 0.01 us  [local(): lax.all_to_all(picked_out, ('req', 'tp'), split_axis=0, concat_axis=0, ti...]
    all_to_all x1, starting transfers between devices: 6.34 us -> 8.69 us  [local(): lax.all_to_all(outgoing, ('req', 'tp'), split_axis=0, concat_axis=0, tile...]
    dot_general x1, matrix products: 15.5 us -> 13.4 us  [local(): lax.dot_general(all_rows, head_weight, (((1,), (1,)), ((), ())), preferre...]
    slice x1 -> x0, local copies, waits for them, and re-layouts: 1.62 us -> none  [local(): state_rows = jnp.take(gathered[:, quarter:], own_serving // slots, axis=0)]
    select_n x0 -> x3, other arithmetic: none -> 1.62 us  [the longest x1 1.59 us: local(): jnp.where((dest_req == owner)[:, None, None], jnp.tile(picked_parts, (n_r...]
  transfers between devices with their start and end apart: 4 -> 4, of which waited for: 4 -> 3; matrix products, arithmetic and copies ran while one was open for 3% -> 16% of each run, Pallas kernels for 0% -> 0%
where the time goes in v6:
time: 154 us; the launch traced here: 153 us
  waiting for transfers between devices  60.3 us (39%)
  between operations  24.8 us (16%)
  matrix products  24.4 us (16%)
  starting transfers between devices  22.7 us (15%)
  other arithmetic  11.2 us (7%)
  local copies, waits for them, and re-layouts  9.46 us (6%)
    all_gather x1, waiting for transfers between devices, local(): all_rows = lax.all_gather(normed, 'req', axis=0, tiled=True)  38.5 us
    all_to_all x1, waiting for transfers between devices, local(): lax.all_to_all(partial_out.reshape(n_tp, quarter, model_width), 'tp', spl...  13.6 us
    dot_general x1, matrix products, local(): lax.dot_general(all_rows, head_weight, (((1,), (1,)), ((), ())), preferre...  13.4 us
    all_to_all x1, starting transfers between devices, local(): lax.all_to_all(outgoing, ('req', 'tp'), split_axis=0, concat_axis=0, tile...  8.69 us
    all_to_all x1, starting transfers between devices, local(): lax.all_to_all(picked_out, ('req', 'tp'), split_axis=0, concat_axis=0, ti...  8.36 us
    all_to_all x1, waiting for transfers between devices, local(): lax.all_to_all(outgoing, ('req', 'tp'), split_axis=0, concat_axis=0, tile...  8.14 us
    all_to_all x1, starting transfers between devices, local(): lax.all_to_all(partial_out.reshape(n_tp, quarter, model_width), 'tp', spl...  5.56 us
    unnamed x22, local copies, waits for them, and re-layouts  3.65 us
  transfers between devices with their start and end apart: 4, of which 3 were waited for; matrix products, arithmetic and copies ran while one was open for 16% of the time, Pallas kernels for 0%

profile of v6, /device:TPU:0, one launch (start us, length us, event | category | flops | bytes accessed | tf_op | source)
XLA Modules:
  0.0 152.8 jit_solution(3728767302893841345)
XLA Ops:
  7.2 0.8 iota_compare_fusion.6
  8.1 1.0 fusion.29
  9.0 0.2 fusion.59
  9.2 0.9 fusion.30
  10.1 0.2 fusion.58
  10.3 0.2 fusion.60
  10.5 0.1 copy.46
  10.7 0.2 reshape.387
  10.9 1.1 bitcast_select_fusion.1
  12.1 0.4 fusion.55
  12.5 3.6 %fusion = (f32[2,256]{1,0:T(2,128)S(1)}, f32[2,256,1024]{2,1,0:T(8,128)S(1)}) fusion(pred[2,1024]{1,0:T(4,128)(4,1)S(1)} %iota_compare_fusion.6, bf16[2,256,896]{2,1,0:T(8,128)(2,1)S(1)} %bitcast_select_fusion.1, bf16[2,1024,896]{2,1,0:T(8,128)(2,1)} %param.20), kind=kOutput, calls=%fused_computation.8 | convolution fusion | flops 941096448 | bytes 6688768 | tf_op jit(solution)/shard_map/rnd,rkd->rnk/dot_general | solution.py:84
  16.2 0.6 fusion.3
  16.7 1.3 fusion.9
  18.1 0.5 add_divide_fusion
  18.6 0.1 select_reduce_fusion.1
  18.7 1.6 %slice-done.1 = s8[4194304]{0:T(1024)(128)(4,1)S(1)} async-done(((s8[6422528]{0:T(1024)(128)(4,1)}), s8[4194304]{0:T(1024)(128)(4,1)S(1)}, s32[]{:S(2)}) %slice-start.1) | async-done | bytes 4194328
  20.4 2.1 %convolution_convert_fusion = bf16[128,3584]{1,0:T(8,128)(2,1)} fusion(bf16[128,896]{1,0:T(8,128)(2,1)S(1)} %bitcast.87, bf16[896,3584]{1,0:T(8,128)(2,1)S(1)} %bitcast.84), kind=kOutput, calls=%fused_computation.2 | convolution fusion | flops 822542336 | bytes 7569408 | tf_op jit(solution)/shard_map/dot_general | solution.py:125
  22.5 5.6 %all-to-all-start = ((bf16[4,32,3584]{2,1,0:T(8,128)(2,1)}), bf16[4,32,3584]{2,1,0:T(8,128)(2,1)S(1)}, u32[]{:S(2)}, u32[]{:S(2)}) async-start(bf16[4,32,3584]{2,1,0:T(8,128)(2,1)} %bitcast.7), calls=%async_computation | async-start | bytes 1835008 | tf_op jit(solution)/shard_map/all_to_all | solution.py:128
  28.1 13.6 %all-to-all-done = bf16[4,32,3584]{2,1,0:T(8,128)(2,1)S(1)} async-done(((bf16[4,32,3584]{2,1,0:T(8,128)(2,1)}), bf16[4,32,3584]{2,1,0:T(8,128)(2,1)S(1)}, u32[]{:S(2)}, u32[]{:S(2)}) %all-to-all-start) | async-done | bytes 917536 | tf_op jit(solution)/shard_map/all_to_all | solution.py:128
  41.7 0.1 convert_reduce_fusion
  41.9 1.1 fusion.15
  43.0 0.8 fusion.17
  43.9 0.6 dynamic_slice.21
  47.1 0.1 select_reduce_fusion.2
  47.3 0.7 fusion.54
  55.6 0.1 reduce_sum.93
  55.8 1.2 gather_fusion.1
  57.3 0.1 reshape.391
  57.6 0.2 convolution_convert_fusion.1
  57.8 1.6 %bitcast_select_fusion = bf16[128,8,896]{2,1,0:T(8,128)(2,1)} fusion(pred[128]{0:T(512)(128)(4,1)S(1)} %broadcast_compare_fusion, bf16[4,8,896]{2,1,0:T(8,128)(2,1)S(1)} %bitcast.93), kind=kLoop, calls=%fused_computation.9 | loop fusion | flops 917504 | bytes 1892480 | tf_op jit(solution)/shard_map/jit(_where)/select_n | solution.py:150
  59.4 8.4 %all-to-all-start.2 = ((bf16[128,8,896]{2,1,0:T(8,128)(2,1)}), bf16[128,8,896]{2,1,0:T(8,128)(2,1)S(1)}, u32[]{:S(2)}, u32[]{:S(2)}) async-start(bf16[128,8,896]{2,1,0:T(8,128)(2,1)} %bitcast_select_fusion), calls=%async_computation.2 | async-start | bytes 3670016 | tf_op jit(solution)/shard_map/all_to_all | solution.py:155
  67.8 38.5 %all-gather.2.cloned.1.call-done = bf16[1024,3584]{1,0:T(8,128)(2,1)} async-done(((bf16[32,3584]{1,0:T(8,128)(2,1)}), bf16[1024,3584]{1,0:T(8,128)(2,1)}) %all-gather.2.cloned.1.call-update) | async-done | bytes 7340048 | tf_op jit(solution)/shard_map/all_gather | solution.py:158
  106.3 13.4 %fusion.56 = (f32[1024]{0:T(1024)S(1)}, f32[1024,1000]{0,1:T(8,128)}) fusion(bf16[1024,3584]{1,0:T(8,128)(2,1)} %all-gather.2.cloned.1.call-done, bf16[1000,3584]{1,0:T(8,128)(2,1)} %param.27), kind=kOutput, calls=%fused_computation.143 | convolution fusion | flops 7341054976 | bytes 18608128 | tf_op jit(solution)/shard_map/dot_general | solution.py:164
  119.8 2.8 %exponential_reduce_fusion = (f32[1024]{0:T(1024)S(1)}, f32[1024]{0:T(1024)S(1)}) fusion(f32[1024,1000]{0,1:T(8,128)} %get-tuple-element.43, f32[1024]{0:T(1024)S(1)} %get-tuple-element.42, s32[1024]{0:T(1024)S(1)} %eq.109, s32[1000]{0:T(1024)S(1)} %iota_add_fusion), kind=kLoop, calls=%fused_computation.5 | loop fusion | flops 5117952 | bytes 4116384 | tf_op jit(solution)/shard_map/reduce_sum | solution.py:47
  122.7 0.1 stack.40
  122.8 0.1 stack.41
  122.9 1.0 gather_fusion
  123.9 0.3 fusion.57
  124.2 1.1 reshape.508
  125.3 8.7 %all-to-all-start.1 = ((f32[128,1,192]{2,1,0:T(1,128)}), f32[128,1,192]{2,1,0:T(1,128)S(1)}, u32[]{:S(2)}, u32[]{:S(2)}) async-start(f32[128,1,192]{2,1,0:T(1,128)} %reshape.508), calls=%async_computation.1 | async-start | bytes 262144 | tf_op jit(solution)/shard_map/all_to_all | solution.py:192
  134.0 0.4 fusion.6
  134.4 0.6 copy.53
  135.1 8.1 %all-to-all-done.1 = f32[128,1,192]{2,1,0:T(1,128)S(1)} async-done(((f32[128,1,192]{2,1,0:T(1,128)}), f32[128,1,192]{2,1,0:T(1,128)S(1)}, u32[]{:S(2)}, u32[]{:S(2)}) %all-to-all-start.1) | async-done | bytes 98336 | tf_op jit(solution)/shard_map/all_to_all | solution.py:192
  143.2 0.5 broadcast.550
  143.7 1.0 reduce.2
  144.7 0.3 reshape.509
  145.1 0.1 constant_dynamic-slice_fusion
  145.3 0.6 sub.95
  (60 shorter events, 1.2 us)
Async XLA Ops:
  7.2 10.9 %copy-start = (bf16[2,64,896]{2,1,0:T(8,128)(2,1)S(1)}, bf16[2,64,896]{2,1,0:T(8,128)(2,1)}, u32[]{:S(2)}) copy-start(bf16[2,64,896]{2,1,0:T(8,128)(2,1)} %param.19) | copy-start | bytes 688132
  7.2 4.9 %copy-start.3 = (bf16[2,64,896]{2,1,0:T(8,128)(2,1)S(1)}, bf16[2,64,896]{2,1,0:T(8,128)(2,1)}, u32[]{:S(2)}) copy-start(bf16[2,64,896]{2,1,0:T(8,128)(2,1)} %param.18) | copy-start | bytes 688132
  12.5 4.2 %copy-start.2 = (bf16[2,1024,896]{2,1,0:T(8,128)(2,1)S(1)}, bf16[2,1024,896]{2,1,0:T(8,128)(2,1)}, u32[]{:S(2)}) copy-start(bf16[2,1024,896]{2,1,0:T(8,128)(2,1)} %param.21) | copy-start | bytes 11010052
  16.7 2.0 %slice-start = ((s8[6422528]{0:T(1024)(128)(4,1)}), s8[2228224]{0:T(1024)(128)(4,1)S(1)}, s32[]{:S(2)}) async-start(s8[6422528]{0:T(1024)(128)(4,1)} %bitcast.83), calls=%async_computation.4 | async-start | bytes 4456448
  18.1 2.3 %slice-start.1 = ((s8[6422528]{0:T(1024)(128)(4,1)}), s8[4194304]{0:T(1024)(128)(4,1)S(1)}, s32[]{:S(2)}) async-start(s8[6422528]{0:T(1024)(128)(4,1)} %bitcast.83), calls=%async_computation.5 | async-start | bytes 8388608
  22.5 20.5 %copy-start.5 = (f32[3584]{0:T(1024)S(1)}, f32[3584]{0:T(1024)}, u32[]{:S(2)}) copy-start(f32[3584]{0:T(1024)} %param.26) | copy-start | bytes 43012
  22.5 21.4 %copy-start.1 = (s32[64]{0:T(128)S(1)}, s32[64]{0:T(128)}, u32[]{:S(2)}) copy-start(s32[64]{0:T(128)} %param.29) | copy-start | bytes 772
  22.5 19.2 %all-to-all-start = ((bf16[4,32,3584]{2,1,0:T(8,128)(2,1)}), bf16[4,32,3584]{2,1,0:T(8,128)(2,1)S(1)}, u32[]{:S(2)}, u32[]{:S(2)}) async-start(bf16[4,32,3584]{2,1,0:T(8,128)(2,1)} %bitcast.7), calls=%async_computation | async-start | bytes 1835008 | tf_op jit(solution)/shard_map/all_to_all | solution.py:128
  28.0 29.0 %copy-start.4 = (s32[64,64]{1,0:T(8,128)S(1)}, s32[64,64]{1,0:T(8,128)}, u32[]{:S(2)}) copy-start(s32[64,64]{1,0:T(8,128)} %param.28) | copy-start | bytes 49156
  28.0 29.6 %copy-start.6 = (s32[2,8,64]{2,1,0:T(8,128)S(1)}, s32[2,8,64]{2,1,0:T(8,128)}, u32[]{:S(2)}) copy-start(s32[2,8,64]{2,1,0:T(8,128)} %param.24) | copy-start | bytes 12292
  28.0 78.3 %all-gather.2.cloned.1.call-start = ((), (), s32[]{:S(2)}) async-start(), calls=%async_computation.3 | async-start | bytes 7569408 | tf_op jit(solution)/shard_map/all_gather | solution.py:158
  59.4 65.9 %all-to-all-start.2 = ((bf16[128,8,896]{2,1,0:T(8,128)(2,1)}), bf16[128,8,896]{2,1,0:T(8,128)(2,1)S(1)}, u32[]{:S(2)}, u32[]{:S(2)}) async-start(bf16[128,8,896]{2,1,0:T(8,128)(2,1)} %bitcast_select_fusion), calls=%async_computation.2 | async-start | bytes 3670016 | tf_op jit(solution)/shard_map/all_to_all | solution.py:155
  125.3 17.9 %all-to-all-start.1 = ((f32[128,1,192]{2,1,0:T(1,128)}), f32[128,1,192]{2,1,0:T(1,128)S(1)}, u32[]{:S(2)}, u32[]{:S(2)}) async-start(f32[128,1,192]{2,1,0:T(1,128)} %reshape.508), calls=%async_computation.1 | async-start | bytes 262144 | tf_op jit(solution)/shard_map/all_to_all | solution.py:192
Sparse Core Ops, SparseCore 0:
  44.0 62.3 all-gather.1

commit v7 on v6

--- a/solution.py
+++ b/solution.py
@@ -144,7 +144,8 @@
     ).astype(jnp.bfloat16)
     n_slots = dealing.shape[0]
     global_slot = req_id * slots + own_slot
-    owner = lax.dynamic_index_in_dim(dealing, global_slot, 0, keepdims=False) // slots
+    slot_ids = jnp.arange(n_slots, dtype=jnp.int32)
+    owner = jnp.sum(jnp.where(slot_ids == global_slot, dealing, 0)) // slots
     dest_req = jnp.arange(n_req * n_tp, dtype=jnp.int32) // n_tp
     picked_parts = picked_rows.reshape(acc_rows, n_tp, dslice).transpose(1, 0, 2)
     picked_out = jnp.where(
@@ -164,17 +165,21 @@
     logits = lax.dot_general(
         all_rows, head_weight, (((1,), (1,)), ((), ())), preferred_element_type=jnp.float32
     )
-    slot_ids = jnp.arange(n_slots, dtype=jnp.int32)
     serving_all = jnp.sum(
         jnp.where(dealing[None, :] == slot_ids[:, None], slot_ids[None, :], 0), axis=1
     )
-    own_serving = lax.dynamic_slice_in_dim(serving_all, req_id * slots, slots, 0)
+    own_requests = req_id * slots + jnp.arange(slots, dtype=jnp.int32)
+    own_serving = jnp.sum(
+        jnp.where(dealing[None, :] == own_requests[:, None], slot_ids[None, :], 0), axis=1
+    )
     source_slot = (
         jnp.arange(n_req * n_tp, dtype=jnp.int32) // n_tp * slots
         + jnp.arange(n_req * n_tp, dtype=jnp.int32) % n_tp // halves
     )
-    source_request = jnp.take(dealing, source_slot)
-    routed = (source_request[None, :] == (req_id * slots + jnp.arange(slots, dtype=jnp.int32))[:, None])
+    source_request = jnp.sum(
+        jnp.where(source_slot[:, None] == slot_ids[None, :], dealing[None, :], 0), axis=1
+    )
+    routed = source_request[None, :] == own_requests[:, None]
     accepted_state = jnp.einsum(
         "ks,sad->kad",
         routed.astype(jnp.bfloat16),
@@ -186,22 +191,27 @@
     local_stats = local_stats.transpose(1, 0, 2)
     dest_blocks = (serving_all // slots).reshape(n_req, 1, slots)
     dest_blocks = jnp.broadcast_to(dest_blocks, (n_req, n_tp, slots)).reshape(-1)
-    outgoing = jnp.take(local_stats, dest_blocks, axis=0).reshape(
-        n_req * n_tp, slots, 3, quarter
-    )
+    block_ids = jnp.arange(n_req, dtype=jnp.int32)
+    outgoing = jnp.sum(
+        jnp.where(
+            (dest_blocks[:, None] == block_ids[None, :])[:, :, None, None],
+            local_stats[None],
+            0.0,
+        ),
+        axis=1,
+    ).reshape(n_req * n_tp, slots, 3, quarter)
     incoming = lax.all_to_all(
         outgoing, ("req", "tp"), split_axis=0, concat_axis=0, tiled=True
     ).reshape(n_req, n_tp, slots, 3, quarter)
     plane_of = (own_serving % slots)[:, None] * halves + jnp.arange(halves, dtype=jnp.int32)[None, :]
-    chosen = jnp.stack(
-        [
-            jnp.stack(
-                [jnp.take(incoming[:, :, i], plane_of[i, h], axis=1) for h in range(halves)],
-                axis=1,
-            )
-            for i in range(slots)
-        ],
-        axis=1,
+    plane_ids = jnp.arange(n_tp, dtype=jnp.int32)
+    chosen = jnp.sum(
+        jnp.where(
+            (plane_of[:, :, None] == plane_ids[None, None, :])[None, :, :, :, None, None],
+            incoming.transpose(0, 2, 1, 3, 4)[:, :, None],
+            0.0,
+        ),
+        axis=3,
     )
     joint_max = jnp.max(chosen[:, :, :, 0], axis=0)
     joint_sum = jnp.sum(chosen[:, :, :, 1] * jnp.exp(chosen[:, :, :, 0] - joint_max[None]), axis=0)

time: 154 us -> 154 us (level)
  waiting for transfers between devices: 60.3 us -> 70.8 us
  between operations: 24.8 us -> 17.1 us
  local copies, waits for them, and re-layouts: 9.46 us -> 6.3 us
    all_gather x1, waiting for transfers between devices: 38.5 us -> 49 us  [local(): all_rows = lax.all_gather(normed, 'req', axis=0, tiled=True)]
    gather x2 -> x0, local copies, waits for them, and re-layouts: 2.22 us -> none  [the longest x1 1.23 us: local(): source_request = jnp.take(dealing, source_slot)]
    reduce_sum x0 -> x5, other arithmetic: none -> 1.59 us  [the longest x1 0.63 us: local(): owner = jnp.sum(jnp.where(slot_ids == global_slot, dealing, 0)) // slots]
    unnamed x22 -> x21, local copies, waits for them, and re-layouts: 3.65 us -> 3.64 us
  transfers between devices with their start and end apart: 4 -> 4, of which waited for: 3 -> 3; matrix products, arithmetic and copies ran while one was open for 16% -> 15% of each run, Pallas kernels for 0% -> 0%
where the time goes in v7:
time: 154 us; the launch traced here: 152 us
  waiting for transfers between devices  70.8 us (46%)
  matrix products  24.4 us (16%)
  starting transfers between devices  21.6 us (14%)
  between operations  17.1 us (11%)
  other arithmetic  12.3 us (8%)
  local copies, waits for them, and re-layouts  6.3 us (4%)
    all_gather x1, waiting for transfers between devices, local(): all_rows = lax.all_gather(normed, 'req', axis=0, tiled=True)  49 us
    all_to_all x1, waiting for transfers between devices, local(): lax.all_to_all(partial_out.reshape(n_tp, quarter, model_width), 'tp', spl...  13.7 us
    dot_general x1, matrix products, local(): lax.dot_general(all_rows, head_weight, (((1,), (1,)), ((), ())), preferre...  13.4 us
    all_to_all x1, starting transfers between devices, local(): lax.all_to_all(picked_out, ('req', 'tp'), split_axis=0, concat_axis=0, ti...  8.19 us
    all_to_all x1, waiting for transfers between devices, local(): lax.all_to_all(outgoing, ('req', 'tp'), split_axis=0, concat_axis=0, tile...  8.14 us
    all_to_all x1, starting transfers between devices, local(): lax.all_to_all(outgoing, ('req', 'tp'), split_axis=0, concat_axis=0, tile...  7.88 us
    all_to_all x1, starting transfers between devices, local(): lax.all_to_all(partial_out.reshape(n_tp, quarter, model_width), 'tp', spl...  5.56 us
    unnamed x21, local copies, waits for them, and re-layouts  3.64 us
  transfers between devices with their start and end apart: 4, of which 3 were waited for; matrix products, arithmetic and copies ran while one was open for 15% of the time, Pallas kernels for 0%

profile of v7, /device:TPU:0, one launch (start us, length us, event | category | flops | bytes accessed | tf_op | source)
XLA Modules:
  0.0 152.5 jit_solution(17125082058006111383)
XLA Ops:
  7.2 0.8 iota_compare_fusion.8
  8.1 1.0 fusion.25
  9.0 0.2 fusion.52
  9.2 0.9 fusion.26
  10.1 0.2 fusion.51
  10.3 0.2 fusion.53
  10.5 0.1 copy.38
  10.7 0.2 reshape.283
  10.9 1.1 bitcast_select_fusion.1
  12.1 0.4 fusion.49
  12.5 3.6 %fusion = (f32[2,256]{1,0:T(2,128)S(1)}, f32[2,256,1024]{2,1,0:T(8,128)S(1)}) fusion(pred[2,1024]{1,0:T(4,128)(4,1)S(1)} %iota_compare_fusion.8, bf16[2,256,896]{2,1,0:T(8,128)(2,1)S(1)} %bitcast_select_fusion.1, bf16[2,1024,896]{2,1,0:T(8,128)(2,1)} %param.18), kind=kOutput, calls=%fused_computation.7 | convolution fusion | flops 941096448 | bytes 6688768 | tf_op jit(solution)/shard_map/rnd,rkd->rnk/dot_general | solution.py:84
  16.1 0.6 fusion.3
  16.7 1.3 fusion.9
  18.1 0.5 add_divide_fusion
  18.6 0.1 select_reduce_fusion.2
  18.7 1.6 %slice-done.1 = s8[4194304]{0:T(1024)(128)(4,1)S(1)} async-done(((s8[6422528]{0:T(1024)(128)(4,1)}), s8[4194304]{0:T(1024)(128)(4,1)S(1)}, s32[]{:S(2)}) %slice-start.1) | async-done | bytes 4194328
  20.4 2.1 %convolution_convert_fusion = bf16[128,3584]{1,0:T(8,128)(2,1)} fusion(bf16[128,896]{1,0:T(8,128)(2,1)S(1)} %bitcast.66, bf16[896,3584]{1,0:T(8,128)(2,1)S(1)} %bitcast.64), kind=kOutput, calls=%fused_computation | convolution fusion | flops 822542336 | bytes 7569408 | tf_op jit(solution)/shard_map/dot_general | solution.py:125
  22.5 5.6 %all-to-all-start = ((bf16[4,32,3584]{2,1,0:T(8,128)(2,1)}), bf16[4,32,3584]{2,1,0:T(8,128)(2,1)S(1)}, u32[]{:S(2)}, u32[]{:S(2)}) async-start(bf16[4,32,3584]{2,1,0:T(8,128)(2,1)} %bitcast.5), calls=%async_computation | async-start | bytes 1835008 | tf_op jit(solution)/shard_map/all_to_all | solution.py:128
  28.0 13.7 %all-to-all-done = bf16[4,32,3584]{2,1,0:T(8,128)(2,1)S(1)} async-done(((bf16[4,32,3584]{2,1,0:T(8,128)(2,1)}), bf16[4,32,3584]{2,1,0:T(8,128)(2,1)S(1)}, u32[]{:S(2)}, u32[]{:S(2)}) %all-to-all-start) | async-done | bytes 917536 | tf_op jit(solution)/shard_map/all_to_all | solution.py:128
  41.7 0.1 convert_reduce_fusion
  41.9 1.1 fusion.15
  43.0 0.8 fusion.17
  43.9 0.6 fusion.42
  47.1 0.1 select_reduce_fusion.5
  47.2 0.1 reduce_sum.139
  47.6 0.2 eq.175
  47.8 0.2 fusion.39
  48.0 0.1 select_reduce_fusion.4
  48.3 0.2 convolution_convert_fusion.1
  48.5 1.6 %bitcast_select_fusion = bf16[128,8,896]{2,1,0:T(8,128)(2,1)} fusion(pred[128]{0:T(512)(128)(4,1)S(1)} %broadcast_compare_fusion, bf16[4,8,896]{2,1,0:T(8,128)(2,1)S(1)} %bitcast.72), kind=kLoop, calls=%fused_computation.8 | loop fusion | flops 917504 | bytes 1892480 | tf_op jit(solution)/shard_map/jit(_where)/select_n | solution.py:151
  50.1 8.2 %all-to-all-start.2 = ((bf16[128,8,896]{2,1,0:T(8,128)(2,1)}), bf16[128,8,896]{2,1,0:T(8,128)(2,1)S(1)}, u32[]{:S(2)}, u32[]{:S(2)}) async-start(bf16[128,8,896]{2,1,0:T(8,128)(2,1)} %bitcast_select_fusion), calls=%async_computation.2 | async-start | bytes 3670016 | tf_op jit(solution)/shard_map/all_to_all | solution.py:156
  58.3 49.0 %all-gather.2.cloned.1.call-done = bf16[1024,3584]{1,0:T(8,128)(2,1)} async-done(((bf16[32,3584]{1,0:T(8,128)(2,1)}), bf16[1024,3584]{1,0:T(8,128)(2,1)}) %all-gather.2.cloned.1.call-update) | async-done | bytes 7340048 | tf_op jit(solution)/shard_map/all_gather | solution.py:159
  107.3 13.4 %fusion.50 = (f32[1024]{0:T(1024)S(1)}, f32[1024,1000]{0,1:T(8,128)}) fusion(bf16[1024,3584]{1,0:T(8,128)(2,1)} %all-gather.2.cloned.1.call-done, bf16[1000,3584]{1,0:T(8,128)(2,1)} %param.25), kind=kOutput, calls=%fused_computation.113 | convolution fusion | flops 7341054976 | bytes 18608128 | tf_op jit(solution)/shard_map/dot_general | solution.py:165
  120.8 2.8 %exponential_reduce_fusion = (f32[1024]{0:T(1024)S(1)}, f32[1024]{0:T(1024)S(1)}) fusion(f32[1024,1000]{0,1:T(8,128)} %get-tuple-element.23, f32[1024]{0:T(1024)S(1)} %get-tuple-element.22, s32[1024]{0:T(1024)S(1)} %eq.187, s32[1000]{0:T(1024)S(1)} %iota_add_fusion), kind=kLoop, calls=%fused_computation.3 | loop fusion | flops 5117952 | bytes 4116384 | tf_op jit(solution)/shard_map/reduce_sum | solution.py:47
  123.7 0.1 stack.14
  123.9 0.5 select_reduce_fusion.1
  124.4 0.2 copy.39
  124.6 0.1 copy.53
  124.7 1.1 reshape.291
  125.8 7.9 %all-to-all-start.1 = ((f32[128,1,192]{2,1,0:T(1,128)}), f32[128,1,192]{2,1,0:T(1,128)S(1)}, u32[]{:S(2)}, u32[]{:S(2)}) async-start(f32[128,1,192]{2,1,0:T(1,128)} %reshape.291), calls=%async_computation.1 | async-start | bytes 262144 | tf_op jit(solution)/shard_map/all_to_all | solution.py:203
  133.7 0.4 fusion.6
  134.1 0.6 copy.46
  134.7 8.1 %all-to-all-done.1 = f32[128,1,192]{2,1,0:T(1,128)S(1)} async-done(((f32[128,1,192]{2,1,0:T(1,128)}), f32[128,1,192]{2,1,0:T(1,128)S(1)}, u32[]{:S(2)}, u32[]{:S(2)}) %all-to-all-start.1) | async-done | bytes 98336 | tf_op jit(solution)/shard_map/all_to_all | solution.py:203
  142.9 0.5 broadcast.309
  143.4 1.0 reduce.2
  144.4 0.3 reshape.292
  144.7 0.2 select_reduce_fusion.3
  145.0 0.6 sub.91
  (53 shorter events, 1.2 us)
Async XLA Ops:
  7.2 10.9 %copy-start = (bf16[2,64,896]{2,1,0:T(8,128)(2,1)S(1)}, bf16[2,64,896]{2,1,0:T(8,128)(2,1)}, u32[]{:S(2)}) copy-start(bf16[2,64,896]{2,1,0:T(8,128)(2,1)} %param.17) | copy-start | bytes 688132
  7.2 4.9 %copy-start.2 = (bf16[2,64,896]{2,1,0:T(8,128)(2,1)S(1)}, bf16[2,64,896]{2,1,0:T(8,128)(2,1)}, u32[]{:S(2)}) copy-start(bf16[2,64,896]{2,1,0:T(8,128)(2,1)} %param.16) | copy-start | bytes 688132
  12.5 4.2 %copy-start.1 = (bf16[2,1024,896]{2,1,0:T(8,128)(2,1)S(1)}, bf16[2,1024,896]{2,1,0:T(8,128)(2,1)}, u32[]{:S(2)}) copy-start(bf16[2,1024,896]{2,1,0:T(8,128)(2,1)} %param.19) | copy-start | bytes 11010052
  16.7 2.0 %slice-start = ((s8[6422528]{0:T(1024)(128)(4,1)}), s8[2228224]{0:T(1024)(128)(4,1)S(1)}, s32[]{:S(2)}) async-start(s8[6422528]{0:T(1024)(128)(4,1)} %bitcast.63), calls=%async_computation.4 | async-start | bytes 4456448
  18.1 2.3 %slice-start.1 = ((s8[6422528]{0:T(1024)(128)(4,1)}), s8[4194304]{0:T(1024)(128)(4,1)S(1)}, s32[]{:S(2)}) async-start(s8[6422528]{0:T(1024)(128)(4,1)} %bitcast.63), calls=%async_computation.5 | async-start | bytes 8388608
  22.5 20.5 %copy-start.4 = (f32[3584]{0:T(1024)S(1)}, f32[3584]{0:T(1024)}, u32[]{:S(2)}) copy-start(f32[3584]{0:T(1024)} %param.24) | copy-start | bytes 43012
  22.5 21.4 %copy-start.6 = (s32[64]{0:T(128)S(1)}, s32[64]{0:T(128)}, u32[]{:S(2)}) copy-start(s32[64]{0:T(128)} %param.27) | copy-start | bytes 772
  22.5 24.9 %copy-start.3 = (s32[64,64]{1,0:T(8,128)S(1)}, s32[64,64]{1,0:T(8,128)}, u32[]{:S(2)}) copy-start(s32[64,64]{1,0:T(8,128)} %param.26) | copy-start | bytes 49156
  22.5 19.2 %all-to-all-start = ((bf16[4,32,3584]{2,1,0:T(8,128)(2,1)}), bf16[4,32,3584]{2,1,0:T(8,128)(2,1)S(1)}, u32[]{:S(2)}, u32[]{:S(2)}) async-start(bf16[4,32,3584]{2,1,0:T(8,128)(2,1)} %bitcast.5), calls=%async_computation | async-start | bytes 1835008 | tf_op jit(solution)/shard_map/all_to_all | solution.py:128
  28.0 20.2 %copy-start.5 = (s32[2,8,64]{2,1,0:T(8,128)S(1)}, s32[2,8,64]{2,1,0:T(8,128)}, u32[]{:S(2)}) copy-start(s32[2,8,64]{2,1,0:T(8,128)} %param.22) | copy-start | bytes 12292
  28.0 79.2 %all-gather.2.cloned.1.call-start = ((), (), s32[]{:S(2)}) async-start(), calls=%async_computation.3 | async-start | bytes 7569408 | tf_op jit(solution)/shard_map/all_gather | solution.py:159
  50.1 75.7 %all-to-all-start.2 = ((bf16[128,8,896]{2,1,0:T(8,128)(2,1)}), bf16[128,8,896]{2,1,0:T(8,128)(2,1)S(1)}, u32[]{:S(2)}, u32[]{:S(2)}) async-start(bf16[128,8,896]{2,1,0:T(8,128)(2,1)} %bitcast_select_fusion), calls=%async_computation.2 | async-start | bytes 3670016 | tf_op jit(solution)/shard_map/all_to_all | solution.py:156
  125.8 17.1 %all-to-all-start.1 = ((f32[128,1,192]{2,1,0:T(1,128)}), f32[128,1,192]{2,1,0:T(1,128)S(1)}, u32[]{:S(2)}, u32[]{:S(2)}) async-start(f32[128,1,192]{2,1,0:T(1,128)} %reshape.291), calls=%async_computation.1 | async-start | bytes 262144 | tf_op jit(solution)/shard_map/all_to_all | solution.py:203
Sparse Core Ops, SparseCore 0:
  43.9 63.2 all-gather.1

commit v8 on v7

--- a/solution.py
+++ b/solution.py
@@ -125,10 +125,13 @@
     partial_out = jnp.dot(
         attention_rows, out_weight, preferred_element_type=jnp.float32
     ).astype(jnp.bfloat16)
-    arriving = lax.all_to_all(
-        partial_out.reshape(n_tp, quarter, model_width), "tp", split_axis=0, concat_axis=0, tiled=True
-    )
-    summed = jnp.sum(arriving.astype(jnp.float32), axis=0)
+    blocks = partial_out.reshape(n_tp, quarter, model_width)
+    summed = lax.dynamic_index_in_dim(blocks, tp_id, 0, keepdims=False).astype(jnp.float32)
+    for shift in range(1, n_tp):
+        outbound = lax.dynamic_index_in_dim(blocks, (tp_id + shift) % n_tp, 0, keepdims=False)
+        summed = summed + lax.ppermute(
+            outbound, "tp", [(t, (t + shift) % n_tp) for t in range(n_tp)]
+        ).astype(jnp.float32)
     flat_stream = stream.reshape(rows_all, model_width)
     own_stream = lax.dynamic_slice_in_dim(flat_stream, tp_id * quarter, quarter, 0)
     post_rows = (own_stream.astype(jnp.float32) + summed).astype(jnp.bfloat16)

time: 154 us -> 151 us (0.981)
  waiting for transfers between devices: 70.8 us -> 66.8 us
  matrix products: 24.4 us -> 26.2 us
  local copies, waits for them, and re-layouts: 6.3 us -> 4.71 us
    all_to_all x1 -> x0, waiting for transfers between devices: 13.7 us -> none  [local(): lax.all_to_all(partial_out.reshape(n_tp, quarter, model_width), 'tp', spl...]
    ppermute x0 -> x3, waiting for transfers between devices: none -> 9.83 us  [local(): lax.ppermute(outbound, 'tp', [(t, (t + shift) % n_tp) for t in range(n_tp)])]
    ppermute x0 -> x3, starting transfers between devices: none -> 6.08 us  [local(): lax.ppermute(outbound, 'tp', [(t, (t + shift) % n_tp) for t in range(n_tp)])]
    all_to_all x1 -> x0, starting transfers between devices: 5.56 us -> none  [local(): lax.all_to_all(partial_out.reshape(n_tp, quarter, model_width), 'tp', spl...]
    dot_general x1, matrix products: 2.12 us -> 3.95 us  [local(): jnp.dot(attention_rows, out_weight, preferred_element_type=jnp.float32)]
    unnamed x21 -> x17, local copies, waits for them, and re-layouts: 3.64 us -> 2.01 us
  transfers between devices with their start and end apart: 4 -> 6, of which waited for: 3 -> 5; matrix products, arithmetic and copies ran while one was open for 15% -> 15% of each run, Pallas kernels for 0% -> 0%
where the time goes in v8:
time: 151 us; the launch traced here: 150 us
  waiting for transfers between devices  66.8 us (44%)
  matrix products  26.2 us (17%)
  starting transfers between devices  23.1 us (15%)
  between operations  17.2 us (11%)
  other arithmetic  12.2 us (8%)
  local copies, waits for them, and re-layouts  4.71 us (3%)
    all_gather x1, waiting for transfers between devices, local(): all_rows = lax.all_gather(normed, 'req', axis=0, tiled=True)  48.8 us
    dot_general x1, matrix products, local(): lax.dot_general(all_rows, head_weight, (((1,), (1,)), ((), ())), preferre...  13.4 us
    ppermute x3, waiting for transfers between devices, local(): lax.ppermute(outbound, 'tp', [(t, (t + shift) % n_tp) for t in range(n_tp)])  9.83 us
    all_to_all x1, starting transfers between devices, local(): lax.all_to_all(picked_out, ('req', 'tp'), split_axis=0, concat_axis=0, ti...  9.06 us
    all_to_all x1, waiting for transfers between devices, local(): lax.all_to_all(outgoing, ('req', 'tp'), split_axis=0, concat_axis=0, tile...  8.14 us
    all_to_all x1, starting transfers between devices, local(): lax.all_to_all(outgoing, ('req', 'tp'), split_axis=0, concat_axis=0, tile...  7.88 us
    ppermute x3, starting transfers between devices, local(): lax.ppermute(outbound, 'tp', [(t, (t + shift) % n_tp) for t in range(n_tp)])  6.08 us
    dot_general x1, matrix products, local(): jnp.dot(attention_rows, out_weight, preferred_element_type=jnp.float32)  3.95 us
  transfers between devices with their start and end apart: 6, of which 5 were waited for; matrix products, arithmetic and copies ran while one was open for 15% of the time, Pallas kernels for 0%

profile of v8, /device:TPU:0, one launch (start us, length us, event | category | flops | bytes accessed | tf_op | source)
XLA Modules:
  0.0 150.1 jit_solution(12769802866500657270)
XLA Ops:
  7.3 0.8 iota_compare_fusion.8
  8.1 1.0 fusion.29
  9.1 0.2 fusion.57
  9.3 0.9 fusion.30
  10.1 0.2 fusion.56
  10.4 0.2 fusion.58
  10.6 0.1 copy.38
  10.7 0.2 reshape.285
  11.0 1.1 bitcast_select_fusion.1
  12.1 0.4 fusion.54
  12.5 3.6 %fusion = (f32[2,256]{1,0:T(2,128)S(1)}, f32[2,256,1024]{2,1,0:T(8,128)S(1)}) fusion(pred[2,1024]{1,0:T(4,128)(4,1)S(1)} %iota_compare_fusion.8, bf16[2,256,896]{2,1,0:T(8,128)(2,1)S(1)} %bitcast_select_fusion.1, bf16[2,1024,896]{2,1,0:T(8,128)(2,1)} %param.18), kind=kOutput, calls=%fused_computation.7 | convolution fusion | flops 941096448 | bytes 6688768 | tf_op jit(solution)/shard_map/rnd,rkd->rnk/dot_general | solution.py:84
  16.2 0.6 fusion.3
  16.8 1.3 fusion.9
  18.1 0.5 add_divide_fusion
  18.6 0.1 select_reduce_fusion.2
  18.7 3.9 %convolution_convert_fusion = bf16[128,3584]{1,0:T(8,128)(2,1)S(1)} fusion(bf16[128,896]{1,0:T(8,128)(2,1)S(1)} %bitcast.76, bf16[896,3584]{1,0:T(8,128)(2,1)} %param.23), kind=kOutput, calls=%fused_computation | convolution fusion | flops 822542336 | bytes 7569408 | tf_op jit(solution)/shard_map/dot_general | solution.py:125
  22.8 2.1 %collective-permute-start = (bf16[32,3584]{1,0:T(8,128)(2,1)S(1)}, bf16[32,3584]{1,0:T(8,128)(2,1)S(1)}, u32[]{:S(2)}, u32[]{:S(2)}) collective-permute-start(bf16[32,3584]{1,0:T(8,128)(2,1)S(1)} %get-tuple-element.18), channel_id=1, source_target_pairs={{0,1},{1,2},{2,3},{3,0},{4,5},{5,6},{6,7},{7,4},{8,9},{9,10},{10,1... | collective-permute-start | bytes 688136 | tf_op jit(solution)/shard_map/ppermute | solution.py:132
  24.9 2.2 %collective-permute-start.2 = (bf16[32,3584]{1,0:T(8,128)(2,1)S(1)}, bf16[32,3584]{1,0:T(8,128)(2,1)S(1)}, u32[]{:S(2)}, u32[]{:S(2)}) collective-permute-start(bf16[32,3584]{1,0:T(8,128)(2,1)S(1)} %get-tuple-element.19), channel_id=1, source_target_pairs={{0,3},{1,0},{2,1},{3,2},{4,7},{5,4},{6,5},{7,6},{8,11},{9,8},{10,9... | collective-permute-start | bytes 688136 | tf_op jit(solution)/shard_map/ppermute | solution.py:132
  27.1 1.8 %collective-permute-start.1 = (bf16[32,3584]{1,0:T(8,128)(2,1)S(1)}, bf16[32,3584]{1,0:T(8,128)(2,1)S(1)}, u32[]{:S(2)}, u32[]{:S(2)}) collective-permute-start(bf16[32,3584]{1,0:T(8,128)(2,1)S(1)} %get-tuple-element.20), channel_id=1, source_target_pairs={{0,2},{1,3},{2,0},{3,1},{4,6},{5,7},{6,4},{7,5},{8,10},{9,11},{10,... | collective-permute-start | bytes 688136 | tf_op jit(solution)/shard_map/ppermute | solution.py:132
  28.9 3.7 %collective-permute-done = bf16[32,3584]{1,0:T(8,128)(2,1)S(1)} collective-permute-done((bf16[32,3584]{1,0:T(8,128)(2,1)S(1)}, bf16[32,3584]{1,0:T(8,128)(2,1)S(1)}, u32[]{:S(2)}, u32[]{:S(2)}) %collective-permute-start) | collective-permute-done | bytes 229408 | tf_op jit(solution)/shard_map/ppermute | solution.py:132
  32.6 4.3 %collective-permute-done.2 = bf16[32,3584]{1,0:T(8,128)(2,1)S(1)} collective-permute-done((bf16[32,3584]{1,0:T(8,128)(2,1)S(1)}, bf16[32,3584]{1,0:T(8,128)(2,1)S(1)}, u32[]{:S(2)}, u32[]{:S(2)}) %collective-permute-start.2) | collective-permute-done | bytes 229408 | tf_op jit(solution)/shard_map/ppermute | solution.py:132
  36.9 1.8 %collective-permute-done.1 = bf16[32,3584]{1,0:T(8,128)(2,1)S(1)} collective-permute-done((bf16[32,3584]{1,0:T(8,128)(2,1)S(1)}, bf16[32,3584]{1,0:T(8,128)(2,1)S(1)}, u32[]{:S(2)}, u32[]{:S(2)}) %collective-permute-start.1) | collective-permute-done | bytes 229408 | tf_op jit(solution)/shard_map/ppermute | solution.py:132
  38.7 1.2 fusion.15
  39.9 0.8 fusion.17
  40.8 0.6 fusion.46
  44.1 0.1 select_reduce_fusion.5
  44.2 0.1 reduce_sum.130
  44.6 0.1 eq.178
  44.8 0.2 fusion.44
  45.2 0.2 convolution_convert_fusion.1
  45.5 1.6 %bitcast_select_fusion = bf16[128,8,896]{2,1,0:T(8,128)(2,1)} fusion(pred[128]{0:T(512)(128)(4,1)S(1)} %broadcast_compare_fusion, bf16[4,8,896]{2,1,0:T(8,128)(2,1)S(1)} %bitcast.82), kind=kLoop, calls=%fused_computation.8 | loop fusion | flops 917504 | bytes 1892480 | tf_op jit(solution)/shard_map/jit(_where)/select_n | solution.py:154
  47.1 9.1 %all-to-all-start.1 = ((bf16[128,8,896]{2,1,0:T(8,128)(2,1)}), bf16[128,8,896]{2,1,0:T(8,128)(2,1)S(1)}, u32[]{:S(2)}, u32[]{:S(2)}) async-start(bf16[128,8,896]{2,1,0:T(8,128)(2,1)} %bitcast_select_fusion), calls=%async_computation.1 | async-start | bytes 3670016 | tf_op jit(solution)/shard_map/all_to_all | solution.py:159
  56.1 48.8 %all-gather.2.cloned.1.call-done = bf16[1024,3584]{1,0:T(8,128)(2,1)} async-done(((bf16[32,3584]{1,0:T(8,128)(2,1)}), bf16[1024,3584]{1,0:T(8,128)(2,1)}) %all-gather.2.cloned.1.call-update) | async-done | bytes 7340048 | tf_op jit(solution)/shard_map/all_gather | solution.py:162
  104.9 13.4 %fusion.55 = (f32[1024]{0:T(1024)S(1)}, f32[1024,1000]{0,1:T(8,128)}) fusion(bf16[1024,3584]{1,0:T(8,128)(2,1)} %all-gather.2.cloned.1.call-done, bf16[1000,3584]{1,0:T(8,128)(2,1)} %param.25), kind=kOutput, calls=%fused_computation.119 | convolution fusion | flops 7341054976 | bytes 18608128 | tf_op jit(solution)/shard_map/dot_general | solution.py:168
  118.4 2.8 %exponential_reduce_fusion = (f32[1024]{0:T(1024)S(1)}, f32[1024]{0:T(1024)S(1)}) fusion(f32[1024,1000]{0,1:T(8,128)} %get-tuple-element.26, f32[1024]{0:T(1024)S(1)} %get-tuple-element.25, s32[1024]{0:T(1024)S(1)} %eq.190, s32[1000]{0:T(1024)S(1)} %iota_add_fusion), kind=kLoop, calls=%fused_computation.3 | loop fusion | flops 5117952 | bytes 4116384 | tf_op jit(solution)/shard_map/reduce_sum | solution.py:47
  121.5 0.5 select_reduce_fusion.1
  122.1 0.2 copy.39
  122.2 0.1 copy.53
  122.4 1.1 reshape.294
  123.4 7.9 %all-to-all-start = ((f32[128,1,192]{2,1,0:T(1,128)}), f32[128,1,192]{2,1,0:T(1,128)S(1)}, u32[]{:S(2)}, u32[]{:S(2)}) async-start(f32[128,1,192]{2,1,0:T(1,128)} %reshape.294), calls=%async_computation | async-start | bytes 262144 | tf_op jit(solution)/shard_map/all_to_all | solution.py:206
  131.3 0.4 fusion.6
  131.8 0.6 copy.46
  132.4 8.1 %all-to-all-done = f32[128,1,192]{2,1,0:T(1,128)S(1)} async-done(((f32[128,1,192]{2,1,0:T(1,128)}), f32[128,1,192]{2,1,0:T(1,128)S(1)}, u32[]{:S(2)}, u32[]{:S(2)}) %all-to-all-start) | async-done | bytes 98336 | tf_op jit(solution)/shard_map/all_to_all | solution.py:206
  140.5 0.5 broadcast.329
  141.0 1.0 reduce.2
  142.0 0.3 reshape.295
  142.4 0.2 select_reduce_fusion.3
  142.6 0.6 sub.91
  (52 shorter events, 1.4 us)
Async XLA Ops:
  7.2 10.9 %copy-start = (bf16[2,64,896]{2,1,0:T(8,128)(2,1)S(1)}, bf16[2,64,896]{2,1,0:T(8,128)(2,1)}, u32[]{:S(2)}) copy-start(bf16[2,64,896]{2,1,0:T(8,128)(2,1)} %param.17) | copy-start | bytes 688132
  7.2 4.9 %copy-start.2 = (bf16[2,64,896]{2,1,0:T(8,128)(2,1)S(1)}, bf16[2,64,896]{2,1,0:T(8,128)(2,1)}, u32[]{:S(2)}) copy-start(bf16[2,64,896]{2,1,0:T(8,128)(2,1)} %param.16) | copy-start | bytes 688132
  7.2 97.7 %all-gather.2.cloned.1.call-start = ((), (), s32[]{:S(2)}) async-start(), calls=%async_computation.2 | async-start | bytes 7569408 | tf_op jit(solution)/shard_map/all_gather | solution.py:162
  12.5 4.2 %copy-start.1 = (bf16[2,1024,896]{2,1,0:T(8,128)(2,1)S(1)}, bf16[2,1024,896]{2,1,0:T(8,128)(2,1)}, u32[]{:S(2)}) copy-start(bf16[2,1024,896]{2,1,0:T(8,128)(2,1)} %param.19) | copy-start | bytes 11010052
  22.7 17.3 %copy-start.4 = (f32[3584]{0:T(1024)S(1)}, f32[3584]{0:T(1024)}, u32[]{:S(2)}) copy-start(f32[3584]{0:T(1024)} %param.24) | copy-start | bytes 43012
  22.7 18.1 %copy-start.6 = (s32[64]{0:T(128)S(1)}, s32[64]{0:T(128)}, u32[]{:S(2)}) copy-start(s32[64]{0:T(128)} %param.27) | copy-start | bytes 772
  22.7 21.6 %copy-start.3 = (s32[64,64]{1,0:T(8,128)S(1)}, s32[64,64]{1,0:T(8,128)}, u32[]{:S(2)}) copy-start(s32[64,64]{1,0:T(8,128)} %param.26) | copy-start | bytes 49156
  22.7 22.5 %copy-start.5 = (s32[2,8,64]{2,1,0:T(8,128)S(1)}, s32[2,8,64]{2,1,0:T(8,128)}, u32[]{:S(2)}) copy-start(s32[2,8,64]{2,1,0:T(8,128)} %param.22) | copy-start | bytes 12292
  22.8 9.8 %collective-permute-start = (bf16[32,3584]{1,0:T(8,128)(2,1)S(1)}, bf16[32,3584]{1,0:T(8,128)(2,1)S(1)}, u32[]{:S(2)}, u32[]{:S(2)}) collective-permute-start(bf16[32,3584]{1,0:T(8,128)(2,1)S(1)} %get-tuple-element.18), channel_id=1, source_target_pairs={{0,1},{1,2},{2,3},{3,0},{4,5},{5,6},{6,7},{7,4},{8,9},{9,10},{10,1... | collective-permute-start | bytes 688136 | tf_op jit(solution)/shard_map/ppermute | solution.py:132
  24.9 12.0 %collective-permute-start.2 = (bf16[32,3584]{1,0:T(8,128)(2,1)S(1)}, bf16[32,3584]{1,0:T(8,128)(2,1)S(1)}, u32[]{:S(2)}, u32[]{:S(2)}) collective-permute-start(bf16[32,3584]{1,0:T(8,128)(2,1)S(1)} %get-tuple-element.19), channel_id=1, source_target_pairs={{0,3},{1,0},{2,1},{3,2},{4,7},{5,4},{6,5},{7,6},{8,11},{9,8},{10,9... | collective-permute-start | bytes 688136 | tf_op jit(solution)/shard_map/ppermute | solution.py:132
  27.1 11.6 %collective-permute-start.1 = (bf16[32,3584]{1,0:T(8,128)(2,1)S(1)}, bf16[32,3584]{1,0:T(8,128)(2,1)S(1)}, u32[]{:S(2)}, u32[]{:S(2)}) collective-permute-start(bf16[32,3584]{1,0:T(8,128)(2,1)S(1)} %get-tuple-element.20), channel_id=1, source_target_pairs={{0,2},{1,3},{2,0},{3,1},{4,6},{5,7},{6,4},{7,5},{8,10},{9,11},{10,... | collective-permute-start | bytes 688136 | tf_op jit(solution)/shard_map/ppermute | solution.py:132
  47.1 76.4 %all-to-all-start.1 = ((bf16[128,8,896]{2,1,0:T(8,128)(2,1)}), bf16[128,8,896]{2,1,0:T(8,128)(2,1)S(1)}, u32[]{:S(2)}, u32[]{:S(2)}) async-start(bf16[128,8,896]{2,1,0:T(8,128)(2,1)} %bitcast_select_fusion), calls=%async_computation.1 | async-start | bytes 3670016 | tf_op jit(solution)/shard_map/all_to_all | solution.py:159
  123.4 17.1 %all-to-all-start = ((f32[128,1,192]{2,1,0:T(1,128)}), f32[128,1,192]{2,1,0:T(1,128)S(1)}, u32[]{:S(2)}, u32[]{:S(2)}) async-start(f32[128,1,192]{2,1,0:T(1,128)} %reshape.294), calls=%async_computation | async-start | bytes 262144 | tf_op jit(solution)/shard_map/all_to_all | solution.py:206
Sparse Core Ops, SparseCore 0:
  40.9 63.9 all-gather.1

commit v9 on v8

--- a/solution.py
+++ b/solution.py
@@ -1,7 +1,7 @@
 import jax
 import jax.numpy as jnp
 from jax import lax
-from jax.sharding import PartitionSpec as P
+from jax.sharding import Mesh, PartitionSpec as P
 
 HD = 224
 ACC = 8
@@ -70,9 +70,13 @@
     model_width = stream.shape[2]
     heads_loc = qwidth // HD
     n_tp = lax.axis_size("tp")
-    n_req = lax.axis_size("req")
+    n_chip = lax.axis_size("chip")
+    n_core = lax.axis_size("core")
+    n_req = n_chip * n_core
     tp_id = lax.axis_index("tp")
-    req_id = lax.axis_index("req")
+    chip_id = lax.axis_index("chip")
+    core_id = lax.axis_index("core")
+    req_id = chip_id * n_core + core_id
     score_scale = HD ** (-0.5)
     cache_cap = cache_key.shape[1]
     column_head = jnp.arange(qwidth, dtype=jnp.int32) // HD
@@ -157,17 +161,28 @@
         jnp.zeros((), picked_parts.dtype),
     )
     picked_in = lax.all_to_all(
-        picked_out, ("req", "tp"), split_axis=0, concat_axis=0, tiled=True
-    )
-    all_rows = lax.all_gather(normed, "req", axis=0, tiled=True)
+        picked_out, ("chip", "core", "tp"), split_axis=0, concat_axis=0, tiled=True
+    )
+    own_rows = lax.all_gather(normed, "chip", axis=0, tiled=True)
+    partner_rows = lax.ppermute(
+        own_rows, "core", [(c, (c + 1) % n_core) for c in range(n_core)]
+    )
     vocab_loc = head_weight.shape[0]
-    wanted_rows = lax.dynamic_slice_in_dim(
+    wanted = lax.dynamic_slice_in_dim(
         candidate.reshape(n_req, rows_all), tp_id * quarter, quarter, 1
-    ).reshape(-1)
+    ).reshape(n_chip, n_core, quarter)
     vocab_ids = req_id * vocab_loc + jnp.arange(vocab_loc, dtype=jnp.int32)
-    logits = lax.dot_general(
-        all_rows, head_weight, (((1,), (1,)), ((), ())), preferred_element_type=jnp.float32
-    )
+
+    def block_stats(rows, core_of_rows):
+        block_logits = lax.dot_general(
+            rows, head_weight, (((1,), (1,)), ((), ())), preferred_element_type=jnp.float32
+        )
+        block_wanted = lax.dynamic_index_in_dim(wanted, core_of_rows, 1, keepdims=False)
+        found = vocab_stats(block_logits, vocab_ids, block_wanted.reshape(-1), 1)
+        return jnp.stack(found).reshape(3, n_chip, quarter)
+
+    own_stats = block_stats(own_rows, core_id)
+    partner_stats = block_stats(partner_rows, (core_id + n_core - 1) % n_core)
     serving_all = jnp.sum(
         jnp.where(dealing[None, :] == slot_ids[:, None], slot_ids[None, :], 0), axis=1
     )
@@ -189,9 +204,12 @@
         picked_in,
         preferred_element_type=jnp.float32,
     ).astype(jnp.bfloat16)
-    row_max, row_sum, picked = vocab_stats(logits, vocab_ids, wanted_rows, 1)
-    local_stats = jnp.stack([row_max, row_sum, picked]).reshape(3, n_req, quarter)
-    local_stats = local_stats.transpose(1, 0, 2)
+    core_ids = jnp.arange(n_core, dtype=jnp.int32)
+    local_stats = jnp.where(
+        (core_ids == core_id)[None, :, None, None],
+        own_stats.transpose(1, 0, 2)[:, None],
+        partner_stats.transpose(1, 0, 2)[:, None],
+    ).reshape(n_req, 3, quarter)
     dest_blocks = (serving_all // slots).reshape(n_req, 1, slots)
     dest_blocks = jnp.broadcast_to(dest_blocks, (n_req, n_tp, slots)).reshape(-1)
     block_ids = jnp.arange(n_req, dtype=jnp.int32)
@@ -204,7 +222,7 @@
         axis=1,
     ).reshape(n_req * n_tp, slots, 3, quarter)
     incoming = lax.all_to_all(
-        outgoing, ("req", "tp"), split_axis=0, concat_axis=0, tiled=True
+        outgoing, ("chip", "core", "tp"), split_axis=0, concat_axis=0, tiled=True
     ).reshape(n_req, n_tp, slots, 3, quarter)
     plane_of = (own_serving % slots)[:, None] * halves + jnp.arange(halves, dtype=jnp.int32)[None, :]
     plane_ids = jnp.arange(n_tp, dtype=jnp.int32)
@@ -224,26 +242,29 @@
 
 
 def solution(mesh):
+    n_req, n_tp = mesh.devices.shape
+    fine = Mesh(mesh.devices.reshape(n_req // 2, 2, n_tp), ("chip", "core", "tp"))
+    req = ("chip", "core")
     placed = (
-        P("req", None, None),
-        P("req", None, "tp"),
-        P("req", None, "tp"),
-        P("req", None, "tp"),
-        P("req", None, "tp"),
-        P("req", None, "tp"),
-        P("req"),
-        P("req", None),
-        P("req", None, None),
+        P(req, None, None),
+        P(req, None, "tp"),
+        P(req, None, "tp"),
+        P(req, None, "tp"),
+        P(req, None, "tp"),
+        P(req, None, "tp"),
+        P(req),
+        P(req, None),
+        P(req, None, None),
         P("tp", None),
         P(),
-        P("req", None),
+        P(req, None),
         P(),
         P(),
     )
     return jax.shard_map(
         local,
-        mesh=mesh,
+        mesh=fine,
         in_specs=placed,
-        out_specs=(P("req", None), P("req", None, "tp")),
+        out_specs=(P(req, None), P(req, None, "tp")),
         check_vma=False,
     )

time: 151 us -> 157 us (1.040)
  waiting for transfers between devices: 66.8 us -> 72.7 us
  starting transfers between devices: 23.1 us -> 18.9 us
  matrix products: 26.2 us -> 29.4 us
    all_to_all x2, waiting for transfers between devices: 8.14 us -> 13.1 us  [the longest x1 8.14 us: local(): lax.all_to_all(outgoing, ('chip', 'core', 'tp'), split_axis=0, concat_axi...]
    all_to_all x2, starting transfers between devices: 16.9 us -> 12.7 us  [the longest x1 8.12 us: local(): lax.all_to_all(picked_out, ('chip', 'core', 'tp'), split_axis=0, concat_a...]
    dot_general x1 -> x2, matrix products: 13.4 us -> 16.7 us  [block_stats(): lax.dot_general(rows, head_weight, (((1,), (1,)), ((), ())), preferred_el...]
  transfers between devices with their start and end apart: 6 -> 7, of which waited for: 5 -> 6; matrix products, arithmetic and copies ran while one was open for 15% -> 17% of each run, Pallas kernels for 0% -> 0%
where the time goes in v9:
time: 157 us; the launch traced here: 156 us
  waiting for transfers between devices  72.7 us (46%)
  matrix products  29.4 us (19%)
  starting transfers between devices  18.9 us (12%)
  between operations  17.2 us (11%)
  other arithmetic  12.2 us (8%)
  local copies, waits for them, and re-layouts  5.21 us (3%)
    all_gather x1, waiting for transfers between devices, local(): own_rows = lax.all_gather(normed, 'chip', axis=0, tiled=True)  49.7 us
    dot_general x2, matrix products, block_stats(): lax.dot_general(rows, head_weight, (((1,), (1,)), ((), ())), preferred_el...  16.7 us
    ppermute x3, waiting for transfers between devices, local(): lax.ppermute(outbound, 'tp', [(t, (t + shift) % n_tp) for t in range(n_tp)])  9.83 us
    all_to_all x1, waiting for transfers between devices, local(): lax.all_to_all(outgoing, ('chip', 'core', 'tp'), split_axis=0, concat_axi...  8.14 us
    all_to_all x1, starting transfers between devices, local(): lax.all_to_all(picked_out, ('chip', 'core', 'tp'), split_axis=0, concat_a...  8.12 us
    ppermute x3, starting transfers between devices, local(): lax.ppermute(outbound, 'tp', [(t, (t + shift) % n_tp) for t in range(n_tp)])  6.08 us
    all_to_all x1, waiting for transfers between devices, local(): lax.all_to_all(picked_out, ('chip', 'core', 'tp'), split_axis=0, concat_a...  4.98 us
    all_to_all x1, starting transfers between devices, local(): lax.all_to_all(outgoing, ('chip', 'core', 'tp'), split_axis=0, concat_axi...  4.62 us
  transfers between devices with their start and end apart: 7, of which 6 were waited for; matrix products, arithmetic and copies ran while one was open for 17% of the time, Pallas kernels for 0%

profile of v9, /device:TPU:0, one launch (start us, length us, event | category | flops | bytes accessed | tf_op | source)
XLA Modules:
  0.0 155.6 jit_solution(1203827057334020481)
XLA Ops:
  7.3 0.8 iota_compare_fusion.8
  8.1 1.0 fusion.29
  9.1 0.2 fusion.57
  9.3 0.9 fusion.30
  10.1 0.2 fusion.56
  10.4 0.2 fusion.58
  10.7 0.2 reshape.318
  11.0 1.1 bitcast_select_fusion.1
  12.1 0.4 fusion.53
  12.5 3.6 %fusion = (f32[2,256]{1,0:T(2,128)S(1)}, f32[2,256,1024]{2,1,0:T(8,128)S(1)}) fusion(pred[2,1024]{1,0:T(4,128)(4,1)S(1)} %iota_compare_fusion.8, bf16[2,256,896]{2,1,0:T(8,128)(2,1)S(1)} %bitcast_select_fusion.1, bf16[2,1024,896]{2,1,0:T(8,128)(2,1)} %param.18), kind=kOutput, calls=%fused_computation.9 | convolution fusion | flops 941096448 | bytes 6688768 | tf_op jit(solution)/shard_map/rnd,rkd->rnk/dot_general | solution.py:88
  16.1 0.6 fusion.3
  16.7 1.3 fusion.9
  18.1 0.5 add_divide_fusion
  18.6 0.1 select_reduce_fusion.3
  18.7 3.9 %convolution_convert_fusion = bf16[128,3584]{1,0:T(8,128)(2,1)S(1)} fusion(bf16[128,896]{1,0:T(8,128)(2,1)S(1)} %bitcast.85, bf16[896,3584]{1,0:T(8,128)(2,1)} %param.23), kind=kOutput, calls=%fused_computation | convolution fusion | flops 822542336 | bytes 7569408 | tf_op jit(solution)/shard_map/dot_general | solution.py:129
  22.8 2.1 %collective-permute-start = (bf16[32,3584]{1,0:T(8,128)(2,1)S(1)}, bf16[32,3584]{1,0:T(8,128)(2,1)S(1)}, u32[]{:S(2)}, u32[]{:S(2)}) collective-permute-start(bf16[32,3584]{1,0:T(8,128)(2,1)S(1)} %get-tuple-element.22), channel_id=1, source_target_pairs={{0,1},{1,2},{2,3},{3,0},{4,5},{5,6},{6,7},{7,4},{8,9},{9,10},{10,1... | collective-permute-start | bytes 688136 | tf_op jit(solution)/shard_map/ppermute | solution.py:136
  24.9 2.2 %collective-permute-start.2 = (bf16[32,3584]{1,0:T(8,128)(2,1)S(1)}, bf16[32,3584]{1,0:T(8,128)(2,1)S(1)}, u32[]{:S(2)}, u32[]{:S(2)}) collective-permute-start(bf16[32,3584]{1,0:T(8,128)(2,1)S(1)} %get-tuple-element.23), channel_id=1, source_target_pairs={{0,3},{1,0},{2,1},{3,2},{4,7},{5,4},{6,5},{7,6},{8,11},{9,8},{10,9... | collective-permute-start | bytes 688136 | tf_op jit(solution)/shard_map/ppermute | solution.py:136
  27.1 1.8 %collective-permute-start.1 = (bf16[32,3584]{1,0:T(8,128)(2,1)S(1)}, bf16[32,3584]{1,0:T(8,128)(2,1)S(1)}, u32[]{:S(2)}, u32[]{:S(2)}) collective-permute-start(bf16[32,3584]{1,0:T(8,128)(2,1)S(1)} %get-tuple-element.24), channel_id=1, source_target_pairs={{0,2},{1,3},{2,0},{3,1},{4,6},{5,7},{6,4},{7,5},{8,10},{9,11},{10,... | collective-permute-start | bytes 688136 | tf_op jit(solution)/shard_map/ppermute | solution.py:136
  28.9 3.7 %collective-permute-done = bf16[32,3584]{1,0:T(8,128)(2,1)S(1)} collective-permute-done((bf16[32,3584]{1,0:T(8,128)(2,1)S(1)}, bf16[32,3584]{1,0:T(8,128)(2,1)S(1)}, u32[]{:S(2)}, u32[]{:S(2)}) %collective-permute-start) | collective-permute-done | bytes 229408 | tf_op jit(solution)/shard_map/ppermute | solution.py:136
  32.6 4.3 %collective-permute-done.2 = bf16[32,3584]{1,0:T(8,128)(2,1)S(1)} collective-permute-done((bf16[32,3584]{1,0:T(8,128)(2,1)S(1)}, bf16[32,3584]{1,0:T(8,128)(2,1)S(1)}, u32[]{:S(2)}, u32[]{:S(2)}) %collective-permute-start.2) | collective-permute-done | bytes 229408 | tf_op jit(solution)/shard_map/ppermute | solution.py:136
  36.9 1.8 %collective-permute-done.1 = bf16[32,3584]{1,0:T(8,128)(2,1)S(1)} collective-permute-done((bf16[32,3584]{1,0:T(8,128)(2,1)S(1)}, bf16[32,3584]{1,0:T(8,128)(2,1)S(1)}, u32[]{:S(2)}, u32[]{:S(2)}) %collective-permute-start.1) | collective-permute-done | bytes 229408 | tf_op jit(solution)/shard_map/ppermute | solution.py:136
  38.7 1.2 fusion.15
  39.9 0.8 fusion.17
  40.8 49.7 %all-gather.2.cloned.1.call-done = bf16[512,3584]{1,0:T(8,128)(2,1)} async-done(((bf16[32,3584]{1,0:T(8,128)(2,1)}), bf16[512,3584]{1,0:T(8,128)(2,1)}) %all-gather.2.cloned.1.call-update) | async-done | bytes 3670032 | tf_op jit(solution)/shard_map/all_gather | solution.py:166
  90.5 0.6 fusion.45
  93.9 0.1 select_reduce_fusion.6
  94.5 0.1 eq.202
  94.8 0.2 fusion.43
  95.2 0.2 convolution_convert_fusion.1
  95.4 1.5 bitcast_select_fusion
  97.0 8.1 %all-to-all-start.1 = ((bf16[128,8,896]{2,1,0:T(8,128)(2,1)}), bf16[128,8,896]{2,1,0:T(8,128)(2,1)S(1)}, u32[]{:S(2)}, u32[]{:S(2)}) async-start(bf16[128,8,896]{2,1,0:T(8,128)(2,1)} %bitcast_select_fusion), calls=%async_computation.1 | async-start | bytes 3670016 | tf_op jit(solution)/shard_map/all_to_all | solution.py:163
  105.1 8.4 %fusion.54 = (f32[512]{0:T(512)S(1)}, f32[512,1000]{0,1:T(8,128)}) fusion(bf16[512,3584]{1,0:T(8,128)(2,1)} %all-gather.2.cloned.1.call-done, bf16[1000,3584]{1,0:T(8,128)(2,1)} %param.25), kind=kOutput, calls=%fused_computation.125 | convolution fusion | flops 3670527488 | bytes 12888064 | tf_op jit(solution)/shard_map/dot_general | solution.py:177
  113.5 8.3 %fusion.55 = (f32[512]{0:T(512)S(1)}, f32[512,1000]{0,1:T(8,128)}) fusion(bf16[512,3584]{1,0:T(8,128)(2,1)} %collective-permute-done.3, bf16[1000,3584]{1,0:T(8,128)(2,1)} %param.25), kind=kOutput, calls=%fused_computation.126 | convolution fusion | flops 3670527488 | bytes 12888064 | tf_op jit(solution)/shard_map/dot_general | solution.py:177
  122.0 2.8 %exponential_reduce_fusion.1 = (f32[512]{0:T(512)S(1)}, f32[512]{0:T(512)S(1)}, f32[512]{0:T(512)S(1)}, f32[512]{0:T(512)S(1)}) fusion(f32[512,1000]{0,1:T(8,128)} %get-tuple-element.32, f32[512]{0:T(512)S(1)} %get-tuple-element.31, s32[512]{0:T(512)S(1)} %eq.216, s32[1000]{0:T(1024)S(1)} %iota_add_fusion, f32[512,1000]{0,1:T(8,128)} %get-tuple-element.34, ...), kind=kLoop, calls=%fused_computation.8 | loop fusion | flops 5117952 | bytes 4116384 | tf_op jit(solution)/shard_map/reduce_sum | solution.py:47
  125.3 0.5 select_reduce_fusion
  125.8 0.2 copy.39
  126.0 0.1 copy.53
  126.1 1.1 reshape.340
  127.2 5.0 %all-to-all-done.1 = bf16[128,8,896]{2,1,0:T(8,128)(2,1)S(1)} async-done(((bf16[128,8,896]{2,1,0:T(8,128)(2,1)}), bf16[128,8,896]{2,1,0:T(8,128)(2,1)S(1)}, u32[]{:S(2)}, u32[]{:S(2)}) %all-to-all-start.1) | async-done | bytes 1835040 | tf_op jit(solution)/shard_map/all_to_all | solution.py:163
  132.2 4.6 %all-to-all-start = ((f32[128,1,192]{2,1,0:T(1,128)}), f32[128,1,192]{2,1,0:T(1,128)S(1)}, u32[]{:S(2)}, u32[]{:S(2)}) async-start(f32[128,1,192]{2,1,0:T(1,128)} %reshape.340), calls=%async_computation | async-start | bytes 262144 | tf_op jit(solution)/shard_map/all_to_all | solution.py:224
  136.8 0.4 fusion.6
  137.2 0.6 copy.46
  137.8 8.1 %all-to-all-done = f32[128,1,192]{2,1,0:T(1,128)S(1)} async-done(((f32[128,1,192]{2,1,0:T(1,128)}), f32[128,1,192]{2,1,0:T(1,128)S(1)}, u32[]{:S(2)}, u32[]{:S(2)}) %all-to-all-start) | async-done | bytes 98336 | tf_op jit(solution)/shard_map/all_to_all | solution.py:224
  146.0 0.5 broadcast.351
  146.5 1.0 reduce.10
  147.5 0.3 reshape.341
  147.8 0.2 select_reduce_fusion.4
  148.1 0.6 sub.105
  (64 shorter events, 2.2 us)
Async XLA Ops:
  7.2 10.9 %copy-start = (bf16[2,64,896]{2,1,0:T(8,128)(2,1)S(1)}, bf16[2,64,896]{2,1,0:T(8,128)(2,1)}, u32[]{:S(2)}) copy-start(bf16[2,64,896]{2,1,0:T(8,128)(2,1)} %param.17) | copy-start | bytes 688132
  7.2 4.9 %copy-start.2 = (bf16[2,64,896]{2,1,0:T(8,128)(2,1)S(1)}, bf16[2,64,896]{2,1,0:T(8,128)(2,1)}, u32[]{:S(2)}) copy-start(bf16[2,64,896]{2,1,0:T(8,128)(2,1)} %param.16) | copy-start | bytes 688132
  7.2 83.3 %all-gather.2.cloned.1.call-start = ((), (), s32[]{:S(2)}) async-start(), calls=%async_computation.2 | async-start | bytes 3899392 | tf_op jit(solution)/shard_map/all_gather | solution.py:166
  12.5 4.2 %copy-start.1 = (bf16[2,1024,896]{2,1,0:T(8,128)(2,1)S(1)}, bf16[2,1024,896]{2,1,0:T(8,128)(2,1)}, u32[]{:S(2)}) copy-start(bf16[2,1024,896]{2,1,0:T(8,128)(2,1)} %param.19) | copy-start | bytes 11010052
  22.7 17.3 %copy-start.4 = (f32[3584]{0:T(1024)S(1)}, f32[3584]{0:T(1024)}, u32[]{:S(2)}) copy-start(f32[3584]{0:T(1024)} %param.24) | copy-start | bytes 43012
  22.7 67.8 %copy-start.6 = (s32[64]{0:T(128)S(1)}, s32[64]{0:T(128)}, u32[]{:S(2)}) copy-start(s32[64]{0:T(128)} %param.27) | copy-start | bytes 772
  22.7 71.4 %copy-start.3 = (s32[64,64]{1,0:T(8,128)S(1)}, s32[64,64]{1,0:T(8,128)}, u32[]{:S(2)}) copy-start(s32[64,64]{1,0:T(8,128)} %param.26) | copy-start | bytes 49156
  22.7 72.5 %copy-start.5 = (s32[2,8,64]{2,1,0:T(8,128)S(1)}, s32[2,8,64]{2,1,0:T(8,128)}, u32[]{:S(2)}) copy-start(s32[2,8,64]{2,1,0:T(8,128)} %param.22) | copy-start | bytes 12292
  22.8 9.8 %collective-permute-start = (bf16[32,3584]{1,0:T(8,128)(2,1)S(1)}, bf16[32,3584]{1,0:T(8,128)(2,1)S(1)}, u32[]{:S(2)}, u32[]{:S(2)}) collective-permute-start(bf16[32,3584]{1,0:T(8,128)(2,1)S(1)} %get-tuple-element.22), channel_id=1, source_target_pairs={{0,1},{1,2},{2,3},{3,0},{4,5},{5,6},{6,7},{7,4},{8,9},{9,10},{10,1... | collective-permute-start | bytes 688136 | tf_op jit(solution)/shard_map/ppermute | solution.py:136
  24.9 12.0 %collective-permute-start.2 = (bf16[32,3584]{1,0:T(8,128)(2,1)S(1)}, bf16[32,3584]{1,0:T(8,128)(2,1)S(1)}, u32[]{:S(2)}, u32[]{:S(2)}) collective-permute-start(bf16[32,3584]{1,0:T(8,128)(2,1)S(1)} %get-tuple-element.23), channel_id=1, source_target_pairs={{0,3},{1,0},{2,1},{3,2},{4,7},{5,4},{6,5},{7,6},{8,11},{9,8},{10,9... | collective-permute-start | bytes 688136 | tf_op jit(solution)/shard_map/ppermute | solution.py:136
  27.1 11.6 %collective-permute-start.1 = (bf16[32,3584]{1,0:T(8,128)(2,1)S(1)}, bf16[32,3584]{1,0:T(8,128)(2,1)S(1)}, u32[]{:S(2)}, u32[]{:S(2)}) collective-permute-start(bf16[32,3584]{1,0:T(8,128)(2,1)S(1)} %get-tuple-element.24), channel_id=1, source_target_pairs={{0,2},{1,3},{2,0},{3,1},{4,6},{5,7},{6,4},{7,5},{8,10},{9,11},{10,... | collective-permute-start | bytes 688136 | tf_op jit(solution)/shard_map/ppermute | solution.py:136
  90.5 23.0 %collective-permute-start.3 = (bf16[512,3584]{1,0:T(8,128)(2,1)}, bf16[512,3584]{1,0:T(8,128)(2,1)}, u32[]{:S(2)}, u32[]{:S(2)}) collective-permute-start(bf16[512,3584]{1,0:T(8,128)(2,1)} %all-gather.2.cloned.1.call-done), channel_id=1, source_target_pairs={{0,4},{4,0},{1,5},{5,1},{2,6},{6,2},{3,7},{7,3},{8,12},{12,8},{9,1... | collective-permute-start | bytes 11010056 | tf_op jit(solution)/shard_map/ppermute | solution.py:167
  97.0 35.2 %all-to-all-start.1 = ((bf16[128,8,896]{2,1,0:T(8,128)(2,1)}), bf16[128,8,896]{2,1,0:T(8,128)(2,1)S(1)}, u32[]{:S(2)}, u32[]{:S(2)}) async-start(bf16[128,8,896]{2,1,0:T(8,128)(2,1)} %bitcast_select_fusion), calls=%async_computation.1 | async-start | bytes 3670016 | tf_op jit(solution)/shard_map/all_to_all | solution.py:163
  132.2 13.8 %all-to-all-start = ((f32[128,1,192]{2,1,0:T(1,128)}), f32[128,1,192]{2,1,0:T(1,128)S(1)}, u32[]{:S(2)}, u32[]{:S(2)}) async-start(f32[128,1,192]{2,1,0:T(1,128)} %reshape.340), calls=%async_computation | async-start | bytes 262144 | tf_op jit(solution)/shard_map/all_to_all | solution.py:224
Sparse Core Ops, SparseCore 0:
  40.9 49.5 all-gather.1

commit v10 on v8

--- a/solution.py
+++ b/solution.py
@@ -146,19 +146,28 @@
         accept_own.astype(jnp.bfloat16), post_rows, preferred_element_type=jnp.float32
     ).astype(jnp.bfloat16)
     n_slots = dealing.shape[0]
-    global_slot = req_id * slots + own_slot
     slot_ids = jnp.arange(n_slots, dtype=jnp.int32)
-    owner = jnp.sum(jnp.where(slot_ids == global_slot, dealing, 0)) // slots
-    dest_req = jnp.arange(n_req * n_tp, dtype=jnp.int32) // n_tp
     picked_parts = picked_rows.reshape(acc_rows, n_tp, dslice).transpose(1, 0, 2)
-    picked_out = jnp.where(
-        (dest_req == owner)[:, None, None],
-        jnp.tile(picked_parts, (n_req, 1, 1)),
-        jnp.zeros((), picked_parts.dtype),
-    )
-    picked_in = lax.all_to_all(
-        picked_out, ("req", "tp"), split_axis=0, concat_axis=0, tiled=True
-    )
+    parts_in = lax.all_to_all(picked_parts, "tp", split_axis=0, concat_axis=0, tiled=True)
+    plane_slot = jnp.arange(n_tp, dtype=jnp.int32) // halves
+    local_slots = jnp.arange(slots, dtype=jnp.int32)
+    compact = jnp.einsum(
+        "lt,tad->lad",
+        (plane_slot[None, :] == local_slots[:, None]).astype(jnp.bfloat16),
+        parts_in,
+        preferred_element_type=jnp.float32,
+    ).astype(jnp.bfloat16)
+    my_slots = req_id * slots + local_slots
+    my_requests = jnp.sum(
+        jnp.where(slot_ids[None, :] == my_slots[:, None], dealing[None, :], 0), axis=1
+    )
+    dest_ids = jnp.arange(n_req, dtype=jnp.int32)
+    compact_out = jnp.where(
+        ((my_requests // slots)[None, :] == dest_ids[:, None])[:, :, None, None],
+        compact[None],
+        jnp.zeros((), compact.dtype),
+    )
+    compact_in = lax.all_to_all(compact_out, "req", split_axis=0, concat_axis=0, tiled=True)
     all_rows = lax.all_gather(normed, "req", axis=0, tiled=True)
     vocab_loc = head_weight.shape[0]
     wanted_rows = lax.dynamic_slice_in_dim(
@@ -175,18 +184,11 @@
     own_serving = jnp.sum(
         jnp.where(dealing[None, :] == own_requests[:, None], slot_ids[None, :], 0), axis=1
     )
-    source_slot = (
-        jnp.arange(n_req * n_tp, dtype=jnp.int32) // n_tp * slots
-        + jnp.arange(n_req * n_tp, dtype=jnp.int32) % n_tp // halves
-    )
-    source_request = jnp.sum(
-        jnp.where(source_slot[:, None] == slot_ids[None, :], dealing[None, :], 0), axis=1
-    )
-    routed = source_request[None, :] == own_requests[:, None]
+    routed = dealing[None, :] == own_requests[:, None]
     accepted_state = jnp.einsum(
         "ks,sad->kad",
         routed.astype(jnp.bfloat16),
-        picked_in,
+        compact_in.reshape(n_slots, acc_rows, dslice),
         preferred_element_type=jnp.float32,
     ).astype(jnp.bfloat16)
     row_max, row_sum, picked = vocab_stats(logits, vocab_ids, wanted_rows, 1)

time: 151 us -> 147 us (0.974)
  waiting for transfers between devices: 66.8 us -> 62.2 us
  between operations: 17.2 us -> 14.6 us
  starting transfers between devices: 23.1 us -> 24.8 us
    all_gather x1, waiting for transfers between devices: 48.8 us -> 23.9 us  [local(): all_rows = lax.all_gather(normed, 'req', axis=0, tiled=True)]
    all_to_all x1 -> x2, waiting for transfers between devices: 0.01 us -> 20.2 us  [the longest x1 14.9 us: local(): lax.all_to_all(compact_out, 'req', split_axis=0, concat_axis=0, tiled=True)]
    all_to_all x1 -> x2, starting transfers between devices: 9.06 us -> 10.8 us  [the longest x1 7.5 us: local(): lax.all_to_all(compact_out, 'req', split_axis=0, concat_axis=0, tiled=True)]
  transfers between devices with their start and end apart: 6 -> 7, of which waited for: 5 -> 7; matrix products, arithmetic and copies ran while one was open for 15% -> 4% of each run, Pallas kernels for 0% -> 0%
where the time goes in v10:
time: 147 us; the launch traced here: 146 us
  waiting for transfers between devices  62.2 us (42%)
  matrix products  26.8 us (18%)
  starting transfers between devices  24.8 us (17%)
  between operations  14.6 us (10%)
  other arithmetic  11.5 us (8%)
  local copies, waits for them, and re-layouts  5.7 us (4%)
    all_gather x1, waiting for transfers between devices, local(): all_rows = lax.all_gather(normed, 'req', axis=0, tiled=True)  23.9 us
    all_to_all x1, waiting for transfers between devices, local(): lax.all_to_all(compact_out, 'req', split_axis=0, concat_axis=0, tiled=True)  14.9 us
    dot_general x1, matrix products, local(): lax.dot_general(all_rows, head_weight, (((1,), (1,)), ((), ())), preferre...  13.4 us
    ppermute x3, waiting for transfers between devices, local(): lax.ppermute(outbound, 'tp', [(t, (t + shift) % n_tp) for t in range(n_tp)])  9.83 us
    all_to_all x1, waiting for transfers between devices, local(): lax.all_to_all(outgoing, ('req', 'tp'), split_axis=0, concat_axis=0, tile...  8.28 us
    all_to_all x1, starting transfers between devices, local(): lax.all_to_all(outgoing, ('req', 'tp'), split_axis=0, concat_axis=0, tile...  7.87 us
    all_to_all x1, starting transfers between devices, local(): lax.all_to_all(compact_out, 'req', split_axis=0, concat_axis=0, tiled=True)  7.5 us
    ppermute x3, starting transfers between devices, local(): lax.ppermute(outbound, 'tp', [(t, (t + shift) % n_tp) for t in range(n_tp)])  6.08 us
  transfers between devices with their start and end apart: 7, of which 7 were waited for; matrix products, arithmetic and copies ran while one was open for 4% of the time, Pallas kernels for 0%

profile of v10, /device:TPU:0, one launch (start us, length us, event | category | flops | bytes accessed | tf_op | source)
XLA Modules:
  0.0 145.6 jit_solution(14883574268249813601)
XLA Ops:
  7.3 0.8 iota_compare_fusion.8
  8.1 1.0 fusion.24
  9.1 0.2 fusion.54
  9.3 0.9 fusion.25
  10.1 0.2 fusion.53
  10.4 0.2 fusion.55
  10.7 0.2 reshape.280
  11.0 1.1 bitcast_select_fusion
  12.1 0.4 fusion.51
  12.5 3.6 %fusion = (f32[2,256]{1,0:T(2,128)S(1)}, f32[2,256,1024]{2,1,0:T(8,128)S(1)}) fusion(pred[2,1024]{1,0:T(4,128)(4,1)S(1)} %iota_compare_fusion.8, bf16[2,256,896]{2,1,0:T(8,128)(2,1)S(1)} %bitcast_select_fusion, bf16[2,1024,896]{2,1,0:T(8,128)(2,1)} %param.18), kind=kOutput, calls=%fused_computation.7 | convolution fusion | flops 941096448 | bytes 6688768 | tf_op jit(solution)/shard_map/rnd,rkd->rnk/dot_general | solution.py:84
  16.2 0.6 fusion.1
  16.8 1.3 fusion.4
  18.1 0.5 add_divide_fusion
  18.7 3.9 %convolution_convert_fusion = bf16[128,3584]{1,0:T(8,128)(2,1)S(1)} fusion(bf16[128,896]{1,0:T(8,128)(2,1)S(1)} %bitcast.80, bf16[896,3584]{1,0:T(8,128)(2,1)} %param.23), kind=kOutput, calls=%fused_computation | convolution fusion | flops 822542336 | bytes 7569408 | tf_op jit(solution)/shard_map/dot_general | solution.py:125
  22.8 2.1 %collective-permute-start = (bf16[32,3584]{1,0:T(8,128)(2,1)S(1)}, bf16[32,3584]{1,0:T(8,128)(2,1)S(1)}, u32[]{:S(2)}, u32[]{:S(2)}) collective-permute-start(bf16[32,3584]{1,0:T(8,128)(2,1)S(1)} %get-tuple-element.20), channel_id=1, source_target_pairs={{0,1},{1,2},{2,3},{3,0},{4,5},{5,6},{6,7},{7,4},{8,9},{9,10},{10,1... | collective-permute-start | bytes 688136 | tf_op jit(solution)/shard_map/ppermute | solution.py:132
  24.9 2.2 %collective-permute-start.2 = (bf16[32,3584]{1,0:T(8,128)(2,1)S(1)}, bf16[32,3584]{1,0:T(8,128)(2,1)S(1)}, u32[]{:S(2)}, u32[]{:S(2)}) collective-permute-start(bf16[32,3584]{1,0:T(8,128)(2,1)S(1)} %get-tuple-element.21), channel_id=1, source_target_pairs={{0,3},{1,0},{2,1},{3,2},{4,7},{5,4},{6,5},{7,6},{8,11},{9,8},{10,9... | collective-permute-start | bytes 688136 | tf_op jit(solution)/shard_map/ppermute | solution.py:132
  27.1 1.8 %collective-permute-start.1 = (bf16[32,3584]{1,0:T(8,128)(2,1)S(1)}, bf16[32,3584]{1,0:T(8,128)(2,1)S(1)}, u32[]{:S(2)}, u32[]{:S(2)}) collective-permute-start(bf16[32,3584]{1,0:T(8,128)(2,1)S(1)} %get-tuple-element.22), channel_id=1, source_target_pairs={{0,2},{1,3},{2,0},{3,1},{4,6},{5,7},{6,4},{7,5},{8,10},{9,11},{10,... | collective-permute-start | bytes 688136 | tf_op jit(solution)/shard_map/ppermute | solution.py:132
  28.9 3.7 %collective-permute-done = bf16[32,3584]{1,0:T(8,128)(2,1)S(1)} collective-permute-done((bf16[32,3584]{1,0:T(8,128)(2,1)S(1)}, bf16[32,3584]{1,0:T(8,128)(2,1)S(1)}, u32[]{:S(2)}, u32[]{:S(2)}) %collective-permute-start) | collective-permute-done | bytes 229408 | tf_op jit(solution)/shard_map/ppermute | solution.py:132
  32.6 4.3 %collective-permute-done.2 = bf16[32,3584]{1,0:T(8,128)(2,1)S(1)} collective-permute-done((bf16[32,3584]{1,0:T(8,128)(2,1)S(1)}, bf16[32,3584]{1,0:T(8,128)(2,1)S(1)}, u32[]{:S(2)}, u32[]{:S(2)}) %collective-permute-start.2) | collective-permute-done | bytes 229408 | tf_op jit(solution)/shard_map/ppermute | solution.py:132
  36.9 1.8 %collective-permute-done.1 = bf16[32,3584]{1,0:T(8,128)(2,1)S(1)} collective-permute-done((bf16[32,3584]{1,0:T(8,128)(2,1)S(1)}, bf16[32,3584]{1,0:T(8,128)(2,1)S(1)}, u32[]{:S(2)}, u32[]{:S(2)}) %collective-permute-start.1) | collective-permute-done | bytes 229408 | tf_op jit(solution)/shard_map/ppermute | solution.py:132
  38.7 1.2 fusion.10
  40.0 0.9 fusion.12
  41.3 0.2 fusion.40
  41.5 0.8 convolution_convert_fusion.1
  42.4 3.3 %all-to-all-start.1 = ((bf16[4,8,896]{2,1,0:T(8,128)(2,1)}), bf16[4,8,896]{2,1,0:T(8,128)(2,1)S(1)}, u32[]{:S(2)}, u32[]{:S(2)}) async-start(bf16[4,8,896]{2,1,0:T(8,128)(2,1)} %bitcast.21), calls=%async_computation.1 | async-start | bytes 114688 | tf_op jit(solution)/shard_map/all_to_all | solution.py:151
  45.7 0.1 eq.180
  45.9 5.3 %all-to-all-done.1 = bf16[4,8,896]{2,1,0:T(8,128)(2,1)S(1)} async-done(((bf16[4,8,896]{2,1,0:T(8,128)(2,1)}), bf16[4,8,896]{2,1,0:T(8,128)(2,1)S(1)}, u32[]{:S(2)}, u32[]{:S(2)}) %all-to-all-start.1) | async-done | bytes 57376 | tf_op jit(solution)/shard_map/all_to_all | solution.py:151
  51.2 0.2 convolution_convert_fusion.3
  51.4 1.6 %broadcast_select_fusion = bf16[32,2,8,896]{3,1,2,0:T(2,128)(2,1)} fusion(pred[32,2]{1,0:T(8,128)(4,1)S(1)} %iota_compare_fusion.6, bf16[2,8,896]{2,0,1:T(2,128)(2,1)S(1)} %convolution_convert_fusion.3), kind=kLoop, calls=%fused_computation.10 | loop fusion | flops 458752 | bytes 946240 | tf_op jit(solution)/shard_map/jit(_where)/select_n | solution.py:165
  53.0 7.5 %all-to-all-start.2 = ((bf16[32,2,8,896]{3,1,2,0:T(2,128)(2,1)}), bf16[32,2,8,896]{3,1,2,0:T(2,128)(2,1)S(1)}, u32[]{:S(2)}, u32[]{:S(2)}) async-start(bf16[32,2,8,896]{3,1,2,0:T(2,128)(2,1)} %broadcast_select_fusion), calls=%async_computation.2 | async-start | bytes 1835008 | tf_op jit(solution)/shard_map/all_to_all | solution.py:170
  60.7 14.9 %all-to-all-done.2 = bf16[32,2,8,896]{3,1,2,0:T(2,128)(2,1)S(1)} async-done(((bf16[32,2,8,896]{3,1,2,0:T(2,128)(2,1)}), bf16[32,2,8,896]{3,1,2,0:T(2,128)(2,1)S(1)}, u32[]{:S(2)}, u32[]{:S(2)}) %all-to-all-start.2) | async-done | bytes 917536 | tf_op jit(solution)/shard_map/all_to_all | solution.py:170
  75.6 0.6 copy.47
  76.2 0.3 reshape.287
  76.6 23.9 %all-gather.2.cloned.1.call-done = bf16[1024,3584]{1,0:T(8,128)(2,1)} async-done(((bf16[32,3584]{1,0:T(8,128)(2,1)}), bf16[1024,3584]{1,0:T(8,128)(2,1)}) %all-gather.2.cloned.1.call-update) | async-done | bytes 7340048 | tf_op jit(solution)/shard_map/all_gather | solution.py:171
  100.4 13.4 %fusion.52 = (f32[1024]{0:T(1024)S(1)}, f32[1024,1000]{0,1:T(8,128)}) fusion(bf16[1024,3584]{1,0:T(8,128)(2,1)} %all-gather.2.cloned.1.call-done, bf16[1000,3584]{1,0:T(8,128)(2,1)} %param.25), kind=kOutput, calls=%fused_computation.118 | convolution fusion | flops 7341054976 | bytes 18608128 | tf_op jit(solution)/shard_map/dot_general | solution.py:177
  114.0 2.8 %exponential_reduce_fusion = (f32[1024]{0:T(1024)S(1)}, f32[1024]{0:T(1024)S(1)}) fusion(f32[1024,1000]{0,1:T(8,128)} %get-tuple-element.28, f32[1024]{0:T(1024)S(1)} %get-tuple-element.27, s32[1024]{0:T(1024)S(1)} %eq.192, s32[1000]{0:T(1024)S(1)} %iota_add_fusion), kind=kLoop, calls=%fused_computation.3 | loop fusion | flops 5117952 | bytes 4116384 | tf_op jit(solution)/shard_map/reduce_sum | solution.py:47
  117.1 0.5 select_reduce_fusion.1
  117.6 0.2 copy.40
  117.9 1.1 reshape.291
  119.0 7.9 %all-to-all-start = ((f32[128,1,192]{2,1,0:T(1,128)}), f32[128,1,192]{2,1,0:T(1,128)S(1)}, u32[]{:S(2)}, u32[]{:S(2)}) async-start(f32[128,1,192]{2,1,0:T(1,128)} %reshape.291), calls=%async_computation | async-start | bytes 262144 | tf_op jit(solution)/shard_map/all_to_all | solution.py:208
  126.9 0.3 convolution_convert_fusion.2
  127.2 0.6 copy.48
  127.8 8.3 %all-to-all-done = f32[128,1,192]{2,1,0:T(1,128)S(1)} async-done(((f32[128,1,192]{2,1,0:T(1,128)}), f32[128,1,192]{2,1,0:T(1,128)S(1)}, u32[]{:S(2)}, u32[]{:S(2)}) %all-to-all-start) | async-done | bytes 98336 | tf_op jit(solution)/shard_map/all_to_all | solution.py:208
  136.1 0.5 broadcast.290
  136.6 1.0 reduce.2
  137.5 0.3 reshape.292
  137.9 0.2 select_reduce_fusion.3
  138.1 0.6 sub.82
  (56 shorter events, 1.9 us)
Async XLA Ops:
  7.2 10.9 %copy-start = (bf16[2,64,896]{2,1,0:T(8,128)(2,1)S(1)}, bf16[2,64,896]{2,1,0:T(8,128)(2,1)}, u32[]{:S(2)}) copy-start(bf16[2,64,896]{2,1,0:T(8,128)(2,1)} %param.17) | copy-start | bytes 688132
  7.2 4.9 %copy-start.2 = (bf16[2,64,896]{2,1,0:T(8,128)(2,1)S(1)}, bf16[2,64,896]{2,1,0:T(8,128)(2,1)}, u32[]{:S(2)}) copy-start(bf16[2,64,896]{2,1,0:T(8,128)(2,1)} %param.16) | copy-start | bytes 688132
  7.2 93.3 %all-gather.2.cloned.1.call-start = ((), (), s32[]{:S(2)}) async-start(), calls=%async_computation.3 | async-start | bytes 7569408 | tf_op jit(solution)/shard_map/all_gather | solution.py:171
  12.5 4.2 %copy-start.1 = (bf16[2,1024,896]{2,1,0:T(8,128)(2,1)S(1)}, bf16[2,1024,896]{2,1,0:T(8,128)(2,1)}, u32[]{:S(2)}) copy-start(bf16[2,1024,896]{2,1,0:T(8,128)(2,1)} %param.19) | copy-start | bytes 11010052
  22.7 17.3 %copy-start.4 = (f32[3584]{0:T(1024)S(1)}, f32[3584]{0:T(1024)}, u32[]{:S(2)}) copy-start(f32[3584]{0:T(1024)} %param.24) | copy-start | bytes 43012
  22.7 18.2 %copy-start.6 = (s32[64]{0:T(128)S(1)}, s32[64]{0:T(128)}, u32[]{:S(2)}) copy-start(s32[64]{0:T(128)} %param.27) | copy-start | bytes 772
  22.7 18.4 %copy-start.3 = (s32[64,64]{1,0:T(8,128)S(1)}, s32[64,64]{1,0:T(8,128)}, u32[]{:S(2)}) copy-start(s32[64,64]{1,0:T(8,128)} %param.26) | copy-start | bytes 49156
  22.7 18.8 %copy-start.5 = (s32[2,8,64]{2,1,0:T(8,128)S(1)}, s32[2,8,64]{2,1,0:T(8,128)}, u32[]{:S(2)}) copy-start(s32[2,8,64]{2,1,0:T(8,128)} %param.22) | copy-start | bytes 12292
  22.8 9.8 %collective-permute-start = (bf16[32,3584]{1,0:T(8,128)(2,1)S(1)}, bf16[32,3584]{1,0:T(8,128)(2,1)S(1)}, u32[]{:S(2)}, u32[]{:S(2)}) collective-permute-start(bf16[32,3584]{1,0:T(8,128)(2,1)S(1)} %get-tuple-element.20), channel_id=1, source_target_pairs={{0,1},{1,2},{2,3},{3,0},{4,5},{5,6},{6,7},{7,4},{8,9},{9,10},{10,1... | collective-permute-start | bytes 688136 | tf_op jit(solution)/shard_map/ppermute | solution.py:132
  24.9 12.0 %collective-permute-start.2 = (bf16[32,3584]{1,0:T(8,128)(2,1)S(1)}, bf16[32,3584]{1,0:T(8,128)(2,1)S(1)}, u32[]{:S(2)}, u32[]{:S(2)}) collective-permute-start(bf16[32,3584]{1,0:T(8,128)(2,1)S(1)} %get-tuple-element.21), channel_id=1, source_target_pairs={{0,3},{1,0},{2,1},{3,2},{4,7},{5,4},{6,5},{7,6},{8,11},{9,8},{10,9... | collective-permute-start | bytes 688136 | tf_op jit(solution)/shard_map/ppermute | solution.py:132
  27.1 11.6 %collective-permute-start.1 = (bf16[32,3584]{1,0:T(8,128)(2,1)S(1)}, bf16[32,3584]{1,0:T(8,128)(2,1)S(1)}, u32[]{:S(2)}, u32[]{:S(2)}) collective-permute-start(bf16[32,3584]{1,0:T(8,128)(2,1)S(1)} %get-tuple-element.22), channel_id=1, source_target_pairs={{0,2},{1,3},{2,0},{3,1},{4,6},{5,7},{6,4},{7,5},{8,10},{9,11},{10,... | collective-permute-start | bytes 688136 | tf_op jit(solution)/shard_map/ppermute | solution.py:132
  42.4 8.8 %all-to-all-start.1 = ((bf16[4,8,896]{2,1,0:T(8,128)(2,1)}), bf16[4,8,896]{2,1,0:T(8,128)(2,1)S(1)}, u32[]{:S(2)}, u32[]{:S(2)}) async-start(bf16[4,8,896]{2,1,0:T(8,128)(2,1)} %bitcast.21), calls=%async_computation.1 | async-start | bytes 114688 | tf_op jit(solution)/shard_map/all_to_all | solution.py:151
  53.0 22.6 %all-to-all-start.2 = ((bf16[32,2,8,896]{3,1,2,0:T(2,128)(2,1)}), bf16[32,2,8,896]{3,1,2,0:T(2,128)(2,1)S(1)}, u32[]{:S(2)}, u32[]{:S(2)}) async-start(bf16[32,2,8,896]{3,1,2,0:T(2,128)(2,1)} %broadcast_select_fusion), calls=%async_computation.2 | async-start | bytes 1835008 | tf_op jit(solution)/shard_map/all_to_all | solution.py:170
  119.0 17.1 %all-to-all-start = ((f32[128,1,192]{2,1,0:T(1,128)}), f32[128,1,192]{2,1,0:T(1,128)S(1)}, u32[]{:S(2)}, u32[]{:S(2)}) async-start(f32[128,1,192]{2,1,0:T(1,128)} %reshape.291), calls=%async_computation | async-start | bytes 262144 | tf_op jit(solution)/shard_map/all_to_all | solution.py:208
Sparse Core Ops, SparseCore 0:
  41.0 59.4 all-gather.1

commit v11 on v10

--- a/solution.py
+++ b/solution.py
@@ -23,14 +23,20 @@
 def ancestry(parents):
     node_count = parents.shape[-1]
     node_ids = jnp.arange(node_count, dtype=jnp.int32)
-    stride_map = (parents[..., :, None] == node_ids).astype(jnp.float32)
-    reached = jnp.broadcast_to(jnp.eye(node_count, dtype=jnp.float32), stride_map.shape) > 0.5
+    stride_map = (parents[..., :, None] == node_ids).astype(jnp.bfloat16)
+    reached = jnp.broadcast_to(jnp.eye(node_count, dtype=jnp.bool_), stride_map.shape)
     for doubling in range((ACC - 1).bit_length()):
-        further = lax.optimization_barrier(
-            jnp.einsum("rtk,rku->rtu", reached.astype(jnp.float32), stride_map, precision=HIGH)
+        further = jnp.einsum(
+            "rtk,rku->rtu",
+            reached.astype(jnp.bfloat16),
+            stride_map,
+            preferred_element_type=jnp.float32,
         )
         reached = jnp.logical_or(reached, further > 0.5)
-        stride_map = jnp.einsum("rtk,rku->rtu", stride_map, stride_map, precision=HIGH)
+        stride_map = (
+            jnp.einsum("rtk,rku->rtu", stride_map, stride_map, preferred_element_type=jnp.float32)
+            > 0.5
+        ).astype(jnp.bfloat16)
     return reached
 
 
@@ -122,16 +128,21 @@
     acc_rows = accept.shape[1]
     own_slot = tp_id // halves
     node_off = (tp_id % halves) * quarter
-    partial_out = jnp.dot(
-        attention_rows, out_weight, preferred_element_type=jnp.float32
-    ).astype(jnp.bfloat16)
-    blocks = partial_out.reshape(n_tp, quarter, model_width)
-    summed = lax.dynamic_index_in_dim(blocks, tp_id, 0, keepdims=False).astype(jnp.float32)
+    def partial_block(owner_tp):
+        block_rows = lax.dynamic_slice_in_dim(attention_rows, owner_tp * quarter, quarter, 0)
+        return jnp.dot(
+            block_rows, out_weight, preferred_element_type=jnp.float32
+        ).astype(jnp.bfloat16)
+
+    arrived = []
     for shift in range(1, n_tp):
-        outbound = lax.dynamic_index_in_dim(blocks, (tp_id + shift) % n_tp, 0, keepdims=False)
-        summed = summed + lax.ppermute(
-            outbound, "tp", [(t, (t + shift) % n_tp) for t in range(n_tp)]
-        ).astype(jnp.float32)
+        outbound = partial_block((tp_id + shift) % n_tp)
+        arrived.append(
+            lax.ppermute(outbound, "tp", [(t, (t + shift) % n_tp) for t in range(n_tp)])
+        )
+    summed = partial_block(tp_id).astype(jnp.float32)
+    for block in arrived:
+        summed = summed + block.astype(jnp.float32)
     flat_stream = stream.reshape(rows_all, model_width)
     own_stream = lax.dynamic_slice_in_dim(flat_stream, tp_id * quarter, quarter, 0)
     post_rows = (own_stream.astype(jnp.float32) + summed).astype(jnp.bfloat16)

time: 147 us -> 156 us (1.061)
  matrix products: 26.8 us -> 40.1 us
  waiting for transfers between devices: 62.2 us -> 58.2 us
    dot_general x6 -> x9, matrix products: 6.33 us -> 18.6 us  [the longest x4 16.3 us: partial_block(): jnp.dot(block_rows, out_weight, preferred_element_type=jnp.float32)]
    ppermute x3, waiting for transfers between devices: 9.83 us -> 5.78 us  [local(): lax.ppermute(outbound, 'tp', [(t, (t + shift) % n_tp) for t in range(n_tp)])]
  transfers between devices with their start and end apart: 7 -> 7, of which waited for: 7 -> 6; matrix products, arithmetic and copies ran while one was open for 4% -> 9% of each run, Pallas kernels for 0% -> 0%
where the time goes in v11:
time: 156 us; the launch traced here: 154 us
  waiting for transfers between devices  58.2 us (37%)
  matrix products  40.1 us (26%)
  starting transfers between devices  25.7 us (16%)
  between operations  14.5 us (9%)
  other arithmetic  10.3 us (7%)
  local copies, waits for them, and re-layouts  5.63 us (4%)
    all_gather x1, waiting for transfers between devices, local(): all_rows = lax.all_gather(normed, 'req', axis=0, tiled=True)  23.9 us
    dot_general x4, matrix products, partial_block(): jnp.dot(block_rows, out_weight, preferred_element_type=jnp.float32)  16.3 us
    all_to_all x1, waiting for transfers between devices, local(): lax.all_to_all(compact_out, 'req', split_axis=0, concat_axis=0, tiled=True)  14.9 us
    dot_general x1, matrix products, local(): lax.dot_general(all_rows, head_weight, (((1,), (1,)), ((), ())), preferre...  13.4 us
    all_to_all x1, waiting for transfers between devices, local(): lax.all_to_all(outgoing, ('req', 'tp'), split_axis=0, concat_axis=0, tile...  8.28 us
    all_to_all x1, starting transfers between devices, local(): lax.all_to_all(outgoing, ('req', 'tp'), split_axis=0, concat_axis=0, tile...  7.88 us
    all_to_all x1, starting transfers between devices, local(): lax.all_to_all(compact_out, 'req', split_axis=0, concat_axis=0, tiled=True)  7.5 us
    ppermute x3, starting transfers between devices, local(): lax.ppermute(outbound, 'tp', [(t, (t + shift) % n_tp) for t in range(n_tp)])  6.8 us
  transfers between devices with their start and end apart: 7, of which 6 were waited for; matrix products, arithmetic and copies ran while one was open for 9% of the time, Pallas kernels for 0%

profile of v11, /device:TPU:0, one launch (start us, length us, event | category | flops | bytes accessed | tf_op | source)
XLA Modules:
  0.0 154.4 jit_solution(9315320867678889783)
XLA Ops:
  7.3 0.7 iota_compare_fusion.8
  8.0 1.0 fusion.14
  9.0 0.1 fusion.15
  9.2 0.9 fusion.11
  10.3 0.1 fusion.13
  10.6 0.2 reshape.275
  10.8 1.1 bitcast_select_fusion
  11.9 1.4 fusion.66
  13.3 3.6 %fusion.1 = (f32[2,256]{1,0:T(2,128)S(1)}, f32[2,256,1024]{2,1,0:T(8,128)S(1)}) fusion(pred[2,1024]{1,0:T(4,128)(4,1)S(1)} %iota_compare_fusion.8, bf16[2,256,896]{2,1,0:T(8,128)(2,1)S(1)} %bitcast_select_fusion, bf16[2,1024,896]{2,1,0:T(8,128)(2,1)} %param.18), kind=kOutput, calls=%fused_computation.11 | convolution fusion | flops 941096448 | bytes 6688768 | tf_op jit(solution)/shard_map/rnd,rkd->rnk/dot_general | solution.py:90
  16.9 0.6 fusion.2
  17.5 1.3 fusion.16
  18.9 0.5 add_divide_fusion
  19.5 4.0 %convolution_convert_fusion.2 = bf16[32,3584]{1,0:T(8,128)(2,1)S(1)} fusion(bf16[896,3584]{1,0:T(8,128)(2,1)} %param.23, bf16[128,896]{1,0:T(8,128)(2,1)S(1)} %bitcast.73, s32[]{:T(128)S(6)} %select_n.151), kind=kOutput, calls=%fused_computation.2 | convolution fusion | flops 205635584 | bytes 6709252 | tf_op jit(solution)/shard_map/dot_general | solution.py:133
  23.5 2.1 %collective-permute-start = (bf16[32,3584]{1,0:T(8,128)(2,1)S(1)}, bf16[32,3584]{1,0:T(8,128)(2,1)S(1)}, u32[]{:S(2)}, u32[]{:S(2)}) collective-permute-start(bf16[32,3584]{1,0:T(8,128)(2,1)S(1)} %convolution_convert_fusion.2), channel_id=1, source_target_pairs={{0,1},{1,2},{2,3},{3,0},{4,5},{5,6},{6,7},{7,4},{8,9},{9,10},{10,1... | collective-permute-start | bytes 688136 | tf_op jit(solution)/shard_map/ppermute | solution.py:141
  25.6 4.0 %convolution_convert_fusion.1 = bf16[32,3584]{1,0:T(8,128)(2,1)S(1)} fusion(bf16[896,3584]{1,0:T(8,128)(2,1)} %param.23, bf16[128,896]{1,0:T(8,128)(2,1)S(1)} %bitcast.74, s32[]{:T(128)S(6)} %select_n.153), kind=kOutput, calls=%fused_computation.1 | convolution fusion | flops 205635584 | bytes 6709252 | tf_op jit(solution)/shard_map/dot_general | solution.py:133
  29.6 3.6 %collective-permute-start.1 = (bf16[32,3584]{1,0:T(8,128)(2,1)S(1)}, bf16[32,3584]{1,0:T(8,128)(2,1)S(1)}, u32[]{:S(2)}, u32[]{:S(2)}) collective-permute-start(bf16[32,3584]{1,0:T(8,128)(2,1)S(1)} %convolution_convert_fusion.1), channel_id=1, source_target_pairs={{0,2},{1,3},{2,0},{3,1},{4,6},{5,7},{6,4},{7,5},{8,10},{9,11},{10,... | collective-permute-start | bytes 688136 | tf_op jit(solution)/shard_map/ppermute | solution.py:141
  33.3 4.0 %convolution_convert_fusion = bf16[32,3584]{1,0:T(8,128)(2,1)S(1)} fusion(bf16[896,3584]{1,0:T(8,128)(2,1)} %param.23, bf16[128,896]{1,0:T(8,128)(2,1)S(1)} %bitcast.75, s32[]{:T(128)S(6)} %select_n.155), kind=kOutput, calls=%fused_computation | convolution fusion | flops 205635584 | bytes 6709252 | tf_op jit(solution)/shard_map/dot_general | solution.py:133
  37.3 1.1 collective-permute-start.2
  38.4 1.1 collective-permute-done.1
  39.4 4.7 %collective-permute-done.2 = bf16[32,3584]{1,0:T(8,128)(2,1)S(1)} collective-permute-done((bf16[32,3584]{1,0:T(8,128)(2,1)S(1)}, bf16[32,3584]{1,0:T(8,128)(2,1)S(1)}, u32[]{:S(2)}, u32[]{:S(2)}) %collective-permute-start.2) | collective-permute-done | bytes 229408 | tf_op jit(solution)/shard_map/ppermute | solution.py:141
  44.1 4.3 %fusion.22 = (f32[32]{0:T(128)S(1)}, bf16[32,3584]{1,0:T(8,128)(2,1)S(1)}) fusion(bf16[32,3584]{1,0:T(8,128)(2,1)S(1)} %collective-permute-done.2, bf16[32,3584]{1,0:T(8,128)(2,1)S(1)} %collective-permute-done.1, bf16[32,3584]{1,0:T(8,128)(2,1)S(1)} %collective-permute-done, bf16[896,3584]{1,0:T(8,128)(2,1)} %param.23, bf16[128,896]{1,0:T(8,128)(2,1)S(1)} %bitcast.76, ...), kind=kOutput, calls=%fused_computation.46 | convolution fusion | flops 207126496 | bytes 7627904 | tf_op jit(solution)/shard_map/dot_general | solution.py:133
  48.4 0.9 fusion.24
  49.8 0.2 fusion.56
  50.0 0.8 convolution_convert_fusion.4
  50.8 3.5 %all-to-all-start.1 = ((bf16[4,8,896]{2,1,0:T(8,128)(2,1)}), bf16[4,8,896]{2,1,0:T(8,128)(2,1)S(1)}, u32[]{:S(2)}, u32[]{:S(2)}) async-start(bf16[4,8,896]{2,1,0:T(8,128)(2,1)} %bitcast.16), calls=%async_computation.1 | async-start | bytes 114688 | tf_op jit(solution)/shard_map/all_to_all | solution.py:162
  54.4 0.1 eq.180
  54.5 5.3 %all-to-all-done.1 = bf16[4,8,896]{2,1,0:T(8,128)(2,1)S(1)} async-done(((bf16[4,8,896]{2,1,0:T(8,128)(2,1)}), bf16[4,8,896]{2,1,0:T(8,128)(2,1)S(1)}, u32[]{:S(2)}, u32[]{:S(2)}) %all-to-all-start.1) | async-done | bytes 57376 | tf_op jit(solution)/shard_map/all_to_all | solution.py:162
  59.9 0.2 convolution_convert_fusion.6
  60.0 1.6 %broadcast_select_fusion = bf16[32,2,8,896]{3,1,2,0:T(2,128)(2,1)} fusion(pred[32,2]{1,0:T(8,128)(4,1)S(1)} %iota_compare_fusion.6, bf16[2,8,896]{2,0,1:T(2,128)(2,1)S(1)} %convolution_convert_fusion.6), kind=kLoop, calls=%fused_computation.14 | loop fusion | flops 458752 | bytes 946240 | tf_op jit(solution)/shard_map/jit(_where)/select_n | solution.py:176
  61.7 7.5 %all-to-all-start.2 = ((bf16[32,2,8,896]{3,1,2,0:T(2,128)(2,1)}), bf16[32,2,8,896]{3,1,2,0:T(2,128)(2,1)S(1)}, u32[]{:S(2)}, u32[]{:S(2)}) async-start(bf16[32,2,8,896]{3,1,2,0:T(2,128)(2,1)} %broadcast_select_fusion), calls=%async_computation.2 | async-start | bytes 1835008 | tf_op jit(solution)/shard_map/all_to_all | solution.py:181
  69.3 14.9 %all-to-all-done.2 = bf16[32,2,8,896]{3,1,2,0:T(2,128)(2,1)S(1)} async-done(((bf16[32,2,8,896]{3,1,2,0:T(2,128)(2,1)}), bf16[32,2,8,896]{3,1,2,0:T(2,128)(2,1)S(1)}, u32[]{:S(2)}, u32[]{:S(2)}) %all-to-all-start.2) | async-done | bytes 917536 | tf_op jit(solution)/shard_map/all_to_all | solution.py:181
  84.3 0.6 copy.47
  84.9 0.3 reshape.281
  85.3 23.9 %all-gather.2.cloned.1.call-done = bf16[1024,3584]{1,0:T(8,128)(2,1)} async-done(((bf16[32,3584]{1,0:T(8,128)(2,1)}), bf16[1024,3584]{1,0:T(8,128)(2,1)}) %all-gather.2.cloned.1.call-update) | async-done | bytes 7340048 | tf_op jit(solution)/shard_map/all_gather | solution.py:182
  109.2 13.4 %fusion.67 = (f32[1024]{0:T(1024)S(1)}, f32[1024,1000]{0,1:T(8,128)}) fusion(bf16[1024,3584]{1,0:T(8,128)(2,1)} %all-gather.2.cloned.1.call-done, bf16[1000,3584]{1,0:T(8,128)(2,1)} %param.25), kind=kOutput, calls=%fused_computation.136 | convolution fusion | flops 7341054976 | bytes 18608128 | tf_op jit(solution)/shard_map/dot_general | solution.py:188
  122.7 2.8 %exponential_reduce_fusion = (f32[1024]{0:T(1024)S(1)}, f32[1024]{0:T(1024)S(1)}) fusion(f32[1024,1000]{0,1:T(8,128)} %get-tuple-element.25, f32[1024]{0:T(1024)S(1)} %get-tuple-element.24, s32[1024]{0:T(1024)S(1)} %eq.192, s32[1000]{0:T(1024)S(1)} %iota_add_fusion), kind=kLoop, calls=%fused_computation.7 | loop fusion | flops 5117952 | bytes 4116384 | tf_op jit(solution)/shard_map/reduce_sum | solution.py:53
  125.8 0.5 select_reduce_fusion.1
  126.3 0.2 copy.40
  126.6 1.1 reshape.284
  127.7 7.9 %all-to-all-start = ((f32[128,1,192]{2,1,0:T(1,128)}), f32[128,1,192]{2,1,0:T(1,128)S(1)}, u32[]{:S(2)}, u32[]{:S(2)}) async-start(f32[128,1,192]{2,1,0:T(1,128)} %reshape.284), calls=%async_computation | async-start | bytes 262144 | tf_op jit(solution)/shard_map/all_to_all | solution.py:219
  135.6 0.3 convolution_convert_fusion.5
  135.9 0.6 copy.48
  136.5 8.3 %all-to-all-done = f32[128,1,192]{2,1,0:T(1,128)S(1)} async-done(((f32[128,1,192]{2,1,0:T(1,128)}), f32[128,1,192]{2,1,0:T(1,128)S(1)}, u32[]{:S(2)}, u32[]{:S(2)}) %all-to-all-start) | async-done | bytes 98336 | tf_op jit(solution)/shard_map/all_to_all | solution.py:219
  144.8 0.5 broadcast.289
  145.3 1.0 reduce.6
  146.3 0.3 reshape.285
  146.6 0.2 select_reduce_fusion.3
  146.9 0.6 sub.82
  (55 shorter events, 2.0 us)
Async XLA Ops:
  7.2 11.7 %copy-start = (bf16[2,64,896]{2,1,0:T(8,128)(2,1)S(1)}, bf16[2,64,896]{2,1,0:T(8,128)(2,1)}, u32[]{:S(2)}) copy-start(bf16[2,64,896]{2,1,0:T(8,128)(2,1)} %param.17) | copy-start | bytes 688132
  7.2 102.0 %all-gather.2.cloned.1.call-start = ((), (), s32[]{:S(2)}) async-start(), calls=%async_computation.3 | async-start | bytes 7569408 | tf_op jit(solution)/shard_map/all_gather | solution.py:182
  13.3 4.2 %copy-start.1 = (bf16[2,1024,896]{2,1,0:T(8,128)(2,1)S(1)}, bf16[2,1024,896]{2,1,0:T(8,128)(2,1)}, u32[]{:S(2)}) copy-start(bf16[2,1024,896]{2,1,0:T(8,128)(2,1)} %param.19) | copy-start | bytes 11010052
  23.5 14.8 %collective-permute-start = (bf16[32,3584]{1,0:T(8,128)(2,1)S(1)}, bf16[32,3584]{1,0:T(8,128)(2,1)S(1)}, u32[]{:S(2)}, u32[]{:S(2)}) collective-permute-start(bf16[32,3584]{1,0:T(8,128)(2,1)S(1)} %convolution_convert_fusion.2), channel_id=1, source_target_pairs={{0,1},{1,2},{2,3},{3,0},{4,5},{5,6},{6,7},{7,4},{8,9},{9,10},{10,1... | collective-permute-start | bytes 688136 | tf_op jit(solution)/shard_map/ppermute | solution.py:141
  29.6 9.8 %collective-permute-start.1 = (bf16[32,3584]{1,0:T(8,128)(2,1)S(1)}, bf16[32,3584]{1,0:T(8,128)(2,1)S(1)}, u32[]{:S(2)}, u32[]{:S(2)}) collective-permute-start(bf16[32,3584]{1,0:T(8,128)(2,1)S(1)} %convolution_convert_fusion.1), channel_id=1, source_target_pairs={{0,2},{1,3},{2,0},{3,1},{4,6},{5,7},{6,4},{7,5},{8,10},{9,11},{10,... | collective-permute-start | bytes 688136 | tf_op jit(solution)/shard_map/ppermute | solution.py:141
  37.3 6.8 %collective-permute-start.2 = (bf16[32,3584]{1,0:T(8,128)(2,1)S(1)}, bf16[32,3584]{1,0:T(8,128)(2,1)S(1)}, u32[]{:S(2)}, u32[]{:S(2)}) collective-permute-start(bf16[32,3584]{1,0:T(8,128)(2,1)S(1)} %convolution_convert_fusion), channel_id=1, source_target_pairs={{0,3},{1,0},{2,1},{3,2},{4,7},{5,4},{6,5},{7,6},{8,11},{9,8},{10,9... | collective-permute-start | bytes 688136 | tf_op jit(solution)/shard_map/ppermute | solution.py:141
  44.1 4.3 %copy-start.3 = (f32[3584]{0:T(1024)S(1)}, f32[3584]{0:T(1024)}, u32[]{:S(2)}) copy-start(f32[3584]{0:T(1024)} %param.24) | copy-start | bytes 43012
  44.1 5.2 %copy-start.5 = (s32[64]{0:T(128)S(1)}, s32[64]{0:T(128)}, u32[]{:S(2)}) copy-start(s32[64]{0:T(128)} %param.27) | copy-start | bytes 772
  44.1 5.5 %copy-start.2 = (s32[64,64]{1,0:T(8,128)S(1)}, s32[64,64]{1,0:T(8,128)}, u32[]{:S(2)}) copy-start(s32[64,64]{1,0:T(8,128)} %param.26) | copy-start | bytes 49156
  44.1 5.8 %copy-start.4 = (s32[2,8,64]{2,1,0:T(8,128)S(1)}, s32[2,8,64]{2,1,0:T(8,128)}, u32[]{:S(2)}) copy-start(s32[2,8,64]{2,1,0:T(8,128)} %param.22) | copy-start | bytes 12292
  50.8 9.1 %all-to-all-start.1 = ((bf16[4,8,896]{2,1,0:T(8,128)(2,1)}), bf16[4,8,896]{2,1,0:T(8,128)(2,1)S(1)}, u32[]{:S(2)}, u32[]{:S(2)}) async-start(bf16[4,8,896]{2,1,0:T(8,128)(2,1)} %bitcast.16), calls=%async_computation.1 | async-start | bytes 114688 | tf_op jit(solution)/shard_map/all_to_all | solution.py:162
  61.7 22.6 %all-to-all-start.2 = ((bf16[32,2,8,896]{3,1,2,0:T(2,128)(2,1)}), bf16[32,2,8,896]{3,1,2,0:T(2,128)(2,1)S(1)}, u32[]{:S(2)}, u32[]{:S(2)}) async-start(bf16[32,2,8,896]{3,1,2,0:T(2,128)(2,1)} %broadcast_select_fusion), calls=%async_computation.2 | async-start | bytes 1835008 | tf_op jit(solution)/shard_map/all_to_all | solution.py:181
  127.7 17.1 %all-to-all-start = ((f32[128,1,192]{2,1,0:T(1,128)}), f32[128,1,192]{2,1,0:T(1,128)S(1)}, u32[]{:S(2)}, u32[]{:S(2)}) async-start(f32[128,1,192]{2,1,0:T(1,128)} %reshape.284), calls=%async_computation | async-start | bytes 262144 | tf_op jit(solution)/shard_map/all_to_all | solution.py:219
Sparse Core Ops, SparseCore 0:
  49.4 59.6 all-gather.1

commit v12 on v10

--- a/solution.py
+++ b/solution.py
@@ -167,7 +167,13 @@
         compact[None],
         jnp.zeros((), compact.dtype),
     )
-    compact_in = lax.all_to_all(compact_out, "req", split_axis=0, concat_axis=0, tiled=True)
+    compact_in = lax.all_to_all(
+        compact_out.reshape(n_req, slots * acc_rows, dslice),
+        "req",
+        split_axis=0,
+        concat_axis=0,
+        tiled=True,
+    )
     all_rows = lax.all_gather(normed, "req", axis=0, tiled=True)
     vocab_loc = head_weight.shape[0]
     wanted_rows = lax.dynamic_slice_in_dim(
@@ -206,7 +212,11 @@
         axis=1,
     ).reshape(n_req * n_tp, slots, 3, quarter)
     incoming = lax.all_to_all(
-        outgoing, ("req", "tp"), split_axis=0, concat_axis=0, tiled=True
+        outgoing.reshape(n_req * n_tp, slots * 3 * quarter),
+        ("req", "tp"),
+        split_axis=0,
+        concat_axis=0,
+        tiled=True,
     ).reshape(n_req, n_tp, slots, 3, quarter)
     plane_of = (own_serving % slots)[:, None] * halves + jnp.arange(halves, dtype=jnp.int32)[None, :]
     plane_ids = jnp.arange(n_tp, dtype=jnp.int32)

time: 147 us -> 146 us (level)
    all_gather x1, waiting for transfers between devices: 23.9 us -> 40 us  [local(): all_rows = lax.all_gather(normed, 'req', axis=0, tiled=True)]
    all_to_all x2, waiting for transfers between devices: 23.2 us -> 8.28 us  [the longest x1 8.28 us: local(): lax.all_to_all(outgoing.reshape(n_req * n_tp, slots * 3 * quarter), ('req...]
  transfers between devices with their start and end apart: 7 -> 7, of which waited for: 7 -> 6; matrix products, arithmetic and copies ran while one was open for 4% -> 15% of each run, Pallas kernels for 0% -> 0%
where the time goes in v12:
time: 146 us; the launch traced here: 144 us
  waiting for transfers between devices  63.5 us (43%)
  matrix products  26.9 us (18%)
  starting transfers between devices  24.8 us (17%)
  between operations  14.6 us (10%)
  other arithmetic  10.4 us (7%)
  local copies, waits for them, and re-layouts  4.38 us (3%)
    all_gather x1, waiting for transfers between devices, local(): all_rows = lax.all_gather(normed, 'req', axis=0, tiled=True)  40 us
    dot_general x1, matrix products, local(): lax.dot_general(all_rows, head_weight, (((1,), (1,)), ((), ())), preferre...  13.4 us
    ppermute x3, waiting for transfers between devices, local(): lax.ppermute(outbound, 'tp', [(t, (t + shift) % n_tp) for t in range(n_tp)])  9.83 us
    all_to_all x1, waiting for transfers between devices, local(): lax.all_to_all(outgoing.reshape(n_req * n_tp, slots * 3 * quarter), ('req...  8.28 us
    all_to_all x1, starting transfers between devices, local(): lax.all_to_all(outgoing.reshape(n_req * n_tp, slots * 3 * quarter), ('req...  7.86 us
    all_to_all x1, starting transfers between devices, local(): lax.all_to_all(compact_out.reshape(n_req, slots * acc_rows, dslice), 'req...  7.5 us
    ppermute x3, starting transfers between devices, local(): lax.ppermute(outbound, 'tp', [(t, (t + shift) % n_tp) for t in range(n_tp)])  6.08 us
    all_to_all x1, waiting for transfers between devices, local(): lax.all_to_all(picked_parts, 'tp', split_axis=0, concat_axis=0, tiled=True)  5.37 us
  transfers between devices with their start and end apart: 7, of which 6 were waited for; matrix products, arithmetic and copies ran while one was open for 15% of the time, Pallas kernels for 0%

profile of v12, /device:TPU:0, one launch (start us, length us, event | category | flops | bytes accessed | tf_op | source)
XLA Modules:
  0.0 144.4 jit_solution(15985468088568789331)
XLA Ops:
  7.3 0.8 iota_compare_fusion.7
  8.1 1.0 fusion.25
  9.1 0.2 fusion.55
  9.3 0.9 fusion.26
  10.1 0.2 fusion.54
  10.4 0.2 fusion.56
  10.7 0.2 reshape.285
  11.0 1.1 bitcast_select_fusion
  12.1 0.4 fusion.52
  12.5 3.6 %fusion = (f32[2,256]{1,0:T(2,128)S(1)}, f32[2,256,1024]{2,1,0:T(8,128)S(1)}) fusion(pred[2,1024]{1,0:T(4,128)(4,1)S(1)} %iota_compare_fusion.7, bf16[2,256,896]{2,1,0:T(8,128)(2,1)S(1)} %bitcast_select_fusion, bf16[2,1024,896]{2,1,0:T(8,128)(2,1)} %param.18), kind=kOutput, calls=%fused_computation.7 | convolution fusion | flops 941096448 | bytes 6688768 | tf_op jit(solution)/shard_map/rnd,rkd->rnk/dot_general | solution.py:84
  16.2 0.6 fusion.1
  16.8 1.3 fusion.4
  18.1 0.5 add_divide_fusion
  18.6 0.1 select_reduce_fusion.2
  18.7 3.9 %convolution_convert_fusion = bf16[128,3584]{1,0:T(8,128)(2,1)S(1)} fusion(bf16[128,896]{1,0:T(8,128)(2,1)S(1)} %bitcast.78, bf16[896,3584]{1,0:T(8,128)(2,1)} %param.23), kind=kOutput, calls=%fused_computation | convolution fusion | flops 822542336 | bytes 7569408 | tf_op jit(solution)/shard_map/dot_general | solution.py:125
  22.8 2.1 %collective-permute-start = (bf16[32,3584]{1,0:T(8,128)(2,1)S(1)}, bf16[32,3584]{1,0:T(8,128)(2,1)S(1)}, u32[]{:S(2)}, u32[]{:S(2)}) collective-permute-start(bf16[32,3584]{1,0:T(8,128)(2,1)S(1)} %get-tuple-element.18), channel_id=1, source_target_pairs={{0,1},{1,2},{2,3},{3,0},{4,5},{5,6},{6,7},{7,4},{8,9},{9,10},{10,1... | collective-permute-start | bytes 688136 | tf_op jit(solution)/shard_map/ppermute | solution.py:132
  24.9 2.2 %collective-permute-start.2 = (bf16[32,3584]{1,0:T(8,128)(2,1)S(1)}, bf16[32,3584]{1,0:T(8,128)(2,1)S(1)}, u32[]{:S(2)}, u32[]{:S(2)}) collective-permute-start(bf16[32,3584]{1,0:T(8,128)(2,1)S(1)} %get-tuple-element.19), channel_id=1, source_target_pairs={{0,3},{1,0},{2,1},{3,2},{4,7},{5,4},{6,5},{7,6},{8,11},{9,8},{10,9... | collective-permute-start | bytes 688136 | tf_op jit(solution)/shard_map/ppermute | solution.py:132
  27.1 1.8 %collective-permute-start.1 = (bf16[32,3584]{1,0:T(8,128)(2,1)S(1)}, bf16[32,3584]{1,0:T(8,128)(2,1)S(1)}, u32[]{:S(2)}, u32[]{:S(2)}) collective-permute-start(bf16[32,3584]{1,0:T(8,128)(2,1)S(1)} %get-tuple-element.20), channel_id=1, source_target_pairs={{0,2},{1,3},{2,0},{3,1},{4,6},{5,7},{6,4},{7,5},{8,10},{9,11},{10,... | collective-permute-start | bytes 688136 | tf_op jit(solution)/shard_map/ppermute | solution.py:132
  28.9 3.7 %collective-permute-done = bf16[32,3584]{1,0:T(8,128)(2,1)S(1)} collective-permute-done((bf16[32,3584]{1,0:T(8,128)(2,1)S(1)}, bf16[32,3584]{1,0:T(8,128)(2,1)S(1)}, u32[]{:S(2)}, u32[]{:S(2)}) %collective-permute-start) | collective-permute-done | bytes 229408 | tf_op jit(solution)/shard_map/ppermute | solution.py:132
  32.6 4.3 %collective-permute-done.2 = bf16[32,3584]{1,0:T(8,128)(2,1)S(1)} collective-permute-done((bf16[32,3584]{1,0:T(8,128)(2,1)S(1)}, bf16[32,3584]{1,0:T(8,128)(2,1)S(1)}, u32[]{:S(2)}, u32[]{:S(2)}) %collective-permute-start.2) | collective-permute-done | bytes 229408 | tf_op jit(solution)/shard_map/ppermute | solution.py:132
  36.9 1.8 %collective-permute-done.1 = bf16[32,3584]{1,0:T(8,128)(2,1)S(1)} collective-permute-done((bf16[32,3584]{1,0:T(8,128)(2,1)S(1)}, bf16[32,3584]{1,0:T(8,128)(2,1)S(1)}, u32[]{:S(2)}, u32[]{:S(2)}) %collective-permute-start.1) | collective-permute-done | bytes 229408 | tf_op jit(solution)/shard_map/ppermute | solution.py:132
  38.7 1.2 fusion.11
  40.0 0.8 fusion.13
  40.8 0.1 select_reduce_fusion.4
  40.9 0.1 reduce_sum.121
  41.2 0.1 eq.180
  41.4 0.2 fusion.41
  41.9 0.8 convolution_convert_fusion.1
  42.7 3.3 %all-to-all-start.1 = ((bf16[4,8,896]{2,1,0:T(8,128)(2,1)}), bf16[4,8,896]{2,1,0:T(8,128)(2,1)S(1)}, u32[]{:S(2)}, u32[]{:S(2)}) async-start(bf16[4,8,896]{2,1,0:T(8,128)(2,1)} %bitcast.20), calls=%async_computation.1 | async-start | bytes 114688 | tf_op jit(solution)/shard_map/all_to_all | solution.py:151
  46.2 5.4 %all-to-all-done.1 = bf16[4,8,896]{2,1,0:T(8,128)(2,1)S(1)} async-done(((bf16[4,8,896]{2,1,0:T(8,128)(2,1)}), bf16[4,8,896]{2,1,0:T(8,128)(2,1)S(1)}, u32[]{:S(2)}, u32[]{:S(2)}) %all-to-all-start.1) | async-done | bytes 57376 | tf_op jit(solution)/shard_map/all_to_all | solution.py:151
  51.6 0.2 convolution_convert_fusion.3
  51.7 1.1 broadcast_select_fusion
  52.9 7.5 %all-to-all-start.2 = ((bf16[32,16,896]{2,1,0:T(8,128)(2,1)}), bf16[32,16,896]{2,1,0:T(8,128)(2,1)S(1)}, u32[]{:S(2)}, u32[]{:S(2)}) async-start(bf16[32,16,896]{2,1,0:T(8,128)(2,1)} %broadcast_select_fusion), calls=%async_computation.2 | async-start | bytes 1835008 | tf_op jit(solution)/shard_map/all_to_all | solution.py:170
  60.4 40.0 %all-gather.2.cloned.1.call-done = bf16[1024,3584]{1,0:T(8,128)(2,1)} async-done(((bf16[32,3584]{1,0:T(8,128)(2,1)}), bf16[1024,3584]{1,0:T(8,128)(2,1)}) %all-gather.2.cloned.1.call-update) | async-done | bytes 7340048 | tf_op jit(solution)/shard_map/all_gather | solution.py:177
  100.3 13.4 %fusion.53 = (f32[1024]{0:T(1024)S(1)}, f32[1024,1000]{0,1:T(8,128)}) fusion(bf16[1024,3584]{1,0:T(8,128)(2,1)} %all-gather.2.cloned.1.call-done, bf16[1000,3584]{1,0:T(8,128)(2,1)} %param.25), kind=kOutput, calls=%fused_computation.121 | convolution fusion | flops 7341054976 | bytes 18608128 | tf_op jit(solution)/shard_map/dot_general | solution.py:183
  113.9 2.8 %exponential_reduce_fusion = (f32[1024]{0:T(1024)S(1)}, f32[1024]{0:T(1024)S(1)}) fusion(f32[1024,1000]{0,1:T(8,128)} %get-tuple-element.26, f32[1024]{0:T(1024)S(1)} %get-tuple-element.25, s32[1024]{0:T(1024)S(1)} %eq.192, s32[1000]{0:T(1024)S(1)} %iota_add_fusion), kind=kLoop, calls=%fused_computation.3 | loop fusion | flops 5117952 | bytes 4116384 | tf_op jit(solution)/shard_map/reduce_sum | solution.py:47
  117.0 0.5 select_reduce_fusion.1
  117.5 0.2 copy.38
  117.7 1.0 all_to_all.16
  118.8 7.9 %all-to-all-start = ((f32[128,1,192]{2,1,0:T(1,128)}), f32[128,1,192]{2,1,0:T(1,128)S(1)}, u32[]{:S(2)}, u32[]{:S(2)}) async-start(f32[128,1,192]{2,1,0:T(1,128)} %all_to_all.16), calls=%async_computation | async-start | bytes 262144 | tf_op jit(solution)/shard_map/all_to_all | solution.py:214
  126.7 0.3 convolution_convert_fusion.2
  127.0 0.6 copy.47
  127.6 8.3 %all-to-all-done = f32[128,1,192]{2,1,0:T(1,128)S(1)} async-done(((f32[128,1,192]{2,1,0:T(1,128)}), f32[128,1,192]{2,1,0:T(1,128)S(1)}, u32[]{:S(2)}, u32[]{:S(2)}) %all-to-all-start) | async-done | bytes 98336 | tf_op jit(solution)/shard_map/all_to_all | solution.py:214
  135.8 0.3 reduce.2
  136.2 0.3 reshape.289
  136.5 0.2 copy.40
  136.7 0.1 select_reduce_fusion.3
  137.0 0.6 sub.82
  (53 shorter events, 1.5 us)
Async XLA Ops:
  7.2 10.9 %copy-start = (bf16[2,64,896]{2,1,0:T(8,128)(2,1)S(1)}, bf16[2,64,896]{2,1,0:T(8,128)(2,1)}, u32[]{:S(2)}) copy-start(bf16[2,64,896]{2,1,0:T(8,128)(2,1)} %param.17) | copy-start | bytes 688132
  7.2 4.9 %copy-start.2 = (bf16[2,64,896]{2,1,0:T(8,128)(2,1)S(1)}, bf16[2,64,896]{2,1,0:T(8,128)(2,1)}, u32[]{:S(2)}) copy-start(bf16[2,64,896]{2,1,0:T(8,128)(2,1)} %param.16) | copy-start | bytes 688132
  7.2 93.1 %all-gather.2.cloned.1.call-start = ((), (), s32[]{:S(2)}) async-start(), calls=%async_computation.3 | async-start | bytes 7569408 | tf_op jit(solution)/shard_map/all_gather | solution.py:177
  12.5 4.2 %copy-start.1 = (bf16[2,1024,896]{2,1,0:T(8,128)(2,1)S(1)}, bf16[2,1024,896]{2,1,0:T(8,128)(2,1)}, u32[]{:S(2)}) copy-start(bf16[2,1024,896]{2,1,0:T(8,128)(2,1)} %param.19) | copy-start | bytes 11010052
  22.7 17.3 %copy-start.4 = (f32[3584]{0:T(1024)S(1)}, f32[3584]{0:T(1024)}, u32[]{:S(2)}) copy-start(f32[3584]{0:T(1024)} %param.24) | copy-start | bytes 43012
  22.7 18.1 %copy-start.6 = (s32[64]{0:T(128)S(1)}, s32[64]{0:T(128)}, u32[]{:S(2)}) copy-start(s32[64]{0:T(128)} %param.27) | copy-start | bytes 772
  22.7 18.3 %copy-start.3 = (s32[64,64]{1,0:T(8,128)S(1)}, s32[64,64]{1,0:T(8,128)}, u32[]{:S(2)}) copy-start(s32[64,64]{1,0:T(8,128)} %param.26) | copy-start | bytes 49156
  22.7 19.2 %copy-start.5 = (s32[2,8,64]{2,1,0:T(8,128)S(1)}, s32[2,8,64]{2,1,0:T(8,128)}, u32[]{:S(2)}) copy-start(s32[2,8,64]{2,1,0:T(8,128)} %param.22) | copy-start | bytes 12292
  22.8 9.8 %collective-permute-start = (bf16[32,3584]{1,0:T(8,128)(2,1)S(1)}, bf16[32,3584]{1,0:T(8,128)(2,1)S(1)}, u32[]{:S(2)}, u32[]{:S(2)}) collective-permute-start(bf16[32,3584]{1,0:T(8,128)(2,1)S(1)} %get-tuple-element.18), channel_id=1, source_target_pairs={{0,1},{1,2},{2,3},{3,0},{4,5},{5,6},{6,7},{7,4},{8,9},{9,10},{10,1... | collective-permute-start | bytes 688136 | tf_op jit(solution)/shard_map/ppermute | solution.py:132
  24.9 12.0 %collective-permute-start.2 = (bf16[32,3584]{1,0:T(8,128)(2,1)S(1)}, bf16[32,3584]{1,0:T(8,128)(2,1)S(1)}, u32[]{:S(2)}, u32[]{:S(2)}) collective-permute-start(bf16[32,3584]{1,0:T(8,128)(2,1)S(1)} %get-tuple-element.19), channel_id=1, source_target_pairs={{0,3},{1,0},{2,1},{3,2},{4,7},{5,4},{6,5},{7,6},{8,11},{9,8},{10,9... | collective-permute-start | bytes 688136 | tf_op jit(solution)/shard_map/ppermute | solution.py:132
  27.1 11.6 %collective-permute-start.1 = (bf16[32,3584]{1,0:T(8,128)(2,1)S(1)}, bf16[32,3584]{1,0:T(8,128)(2,1)S(1)}, u32[]{:S(2)}, u32[]{:S(2)}) collective-permute-start(bf16[32,3584]{1,0:T(8,128)(2,1)S(1)} %get-tuple-element.20), channel_id=1, source_target_pairs={{0,2},{1,3},{2,0},{3,1},{4,6},{5,7},{6,4},{7,5},{8,10},{9,11},{10,... | collective-permute-start | bytes 688136 | tf_op jit(solution)/shard_map/ppermute | solution.py:132
  42.7 8.8 %all-to-all-start.1 = ((bf16[4,8,896]{2,1,0:T(8,128)(2,1)}), bf16[4,8,896]{2,1,0:T(8,128)(2,1)S(1)}, u32[]{:S(2)}, u32[]{:S(2)}) async-start(bf16[4,8,896]{2,1,0:T(8,128)(2,1)} %bitcast.20), calls=%async_computation.1 | async-start | bytes 114688 | tf_op jit(solution)/shard_map/all_to_all | solution.py:151
  52.9 65.9 %all-to-all-start.2 = ((bf16[32,16,896]{2,1,0:T(8,128)(2,1)}), bf16[32,16,896]{2,1,0:T(8,128)(2,1)S(1)}, u32[]{:S(2)}, u32[]{:S(2)}) async-start(bf16[32,16,896]{2,1,0:T(8,128)(2,1)} %broadcast_select_fusion), calls=%async_computation.2 | async-start | bytes 1835008 | tf_op jit(solution)/shard_map/all_to_all | solution.py:170
  118.8 17.1 %all-to-all-start = ((f32[128,1,192]{2,1,0:T(1,128)}), f32[128,1,192]{2,1,0:T(1,128)S(1)}, u32[]{:S(2)}, u32[]{:S(2)}) async-start(f32[128,1,192]{2,1,0:T(1,128)} %all_to_all.16), calls=%async_computation | async-start | bytes 262144 | tf_op jit(solution)/shard_map/all_to_all | solution.py:214
Sparse Core Ops, SparseCore 0:
  40.9 59.3 all-gather.1

commit v13 on v12

--- a/solution.py
+++ b/solution.py
@@ -211,13 +211,14 @@
         ),
         axis=1,
     ).reshape(n_req * n_tp, slots, 3, quarter)
+    chunk = slots * 3 * quarter
+    tile = 8 * 128
+    padded = jnp.pad(
+        outgoing.reshape(n_req * n_tp, chunk), ((0, 0), (0, -chunk % tile))
+    ).reshape(n_req * n_tp, -1, 128)
     incoming = lax.all_to_all(
-        outgoing.reshape(n_req * n_tp, slots * 3 * quarter),
-        ("req", "tp"),
-        split_axis=0,
-        concat_axis=0,
-        tiled=True,
-    ).reshape(n_req, n_tp, slots, 3, quarter)
+        padded, ("req", "tp"), split_axis=0, concat_axis=0, tiled=True
+    ).reshape(n_req * n_tp, -1)[:, :chunk].reshape(n_req, n_tp, slots, 3, quarter)
     plane_of = (own_serving % slots)[:, None] * halves + jnp.arange(halves, dtype=jnp.int32)[None, :]
     plane_ids = jnp.arange(n_tp, dtype=jnp.int32)
     chosen = jnp.sum(

time: 146 us -> 149 us (1.021)
  waiting for transfers between devices: 63.5 us -> 66.8 us
    all_to_all x1, waiting for transfers between devices: 8.28 us -> 12.1 us  [local(): lax.all_to_all(padded, ('req', 'tp'), split_axis=0, concat_axis=0, tiled=...]
where the time goes in v13:
time: 149 us; the launch traced here: 148 us
  waiting for transfers between devices  66.8 us (45%)
  matrix products  26.9 us (18%)
  starting transfers between devices  24.8 us (17%)
  between operations  14.6 us (10%)
  other arithmetic  10.1 us (7%)
  local copies, waits for them, and re-layouts  4.66 us (3%)
    all_gather x1, waiting for transfers between devices, local(): all_rows = lax.all_gather(normed, 'req', axis=0, tiled=True)  39.4 us
    dot_general x1, matrix products, local(): lax.dot_general(all_rows, head_weight, (((1,), (1,)), ((), ())), preferre...  13.4 us
    all_to_all x1, waiting for transfers between devices, local(): lax.all_to_all(padded, ('req', 'tp'), split_axis=0, concat_axis=0, tiled=...  12.1 us
    ppermute x3, waiting for transfers between devices, local(): lax.ppermute(outbound, 'tp', [(t, (t + shift) % n_tp) for t in range(n_tp)])  9.83 us
    all_to_all x1, starting transfers between devices, local(): lax.all_to_all(padded, ('req', 'tp'), split_axis=0, concat_axis=0, tiled=...  7.88 us
    all_to_all x1, starting transfers between devices, local(): lax.all_to_all(compact_out.reshape(n_req, slots * acc_rows, dslice), 'req...  7.5 us
    ppermute x3, starting transfers between devices, local(): lax.ppermute(outbound, 'tp', [(t, (t + shift) % n_tp) for t in range(n_tp)])  6.08 us
    all_to_all x1, waiting for transfers between devices, local(): lax.all_to_all(picked_parts, 'tp', split_axis=0, concat_axis=0, tiled=True)  5.37 us
  transfers between devices with their start and end apart: 7, of which 6 were waited for; matrix products, arithmetic and copies ran while one was open for 15% of the time, Pallas kernels for 0%

profile of v13, /device:TPU:0, one launch (start us, length us, event | category | flops | bytes accessed | tf_op | source)
XLA Modules:
  0.0 147.7 jit_solution(9821919203908073376)
XLA Ops:
  7.3 0.8 iota_compare_fusion.7
  8.1 1.0 fusion.25
  9.1 0.2 fusion.55
  9.3 0.9 fusion.26
  10.1 0.2 fusion.54
  10.4 0.2 fusion.56
  10.7 0.2 reshape.287
  11.0 1.1 bitcast_select_fusion
  12.1 0.4 fusion.52
  12.5 3.6 %fusion = (f32[2,256]{1,0:T(2,128)S(1)}, f32[2,256,1024]{2,1,0:T(8,128)S(1)}) fusion(pred[2,1024]{1,0:T(4,128)(4,1)S(1)} %iota_compare_fusion.7, bf16[2,256,896]{2,1,0:T(8,128)(2,1)S(1)} %bitcast_select_fusion, bf16[2,1024,896]{2,1,0:T(8,128)(2,1)} %param.18), kind=kOutput, calls=%fused_computation.7 | convolution fusion | flops 941096448 | bytes 6688768 | tf_op jit(solution)/shard_map/rnd,rkd->rnk/dot_general | solution.py:84
  16.2 0.6 fusion.1
  16.8 1.3 fusion.4
  18.1 0.5 add_divide_fusion
  18.6 0.1 select_reduce_fusion.2
  18.7 3.9 %convolution_convert_fusion = bf16[128,3584]{1,0:T(8,128)(2,1)S(1)} fusion(bf16[128,896]{1,0:T(8,128)(2,1)S(1)} %bitcast.86, bf16[896,3584]{1,0:T(8,128)(2,1)} %param.23), kind=kOutput, calls=%fused_computation | convolution fusion | flops 822542336 | bytes 7569408 | tf_op jit(solution)/shard_map/dot_general | solution.py:125
  22.8 2.1 %collective-permute-start = (bf16[32,3584]{1,0:T(8,128)(2,1)S(1)}, bf16[32,3584]{1,0:T(8,128)(2,1)S(1)}, u32[]{:S(2)}, u32[]{:S(2)}) collective-permute-start(bf16[32,3584]{1,0:T(8,128)(2,1)S(1)} %get-tuple-element.18), channel_id=1, source_target_pairs={{0,1},{1,2},{2,3},{3,0},{4,5},{5,6},{6,7},{7,4},{8,9},{9,10},{10,1... | collective-permute-start | bytes 688136 | tf_op jit(solution)/shard_map/ppermute | solution.py:132
  24.9 2.2 %collective-permute-start.2 = (bf16[32,3584]{1,0:T(8,128)(2,1)S(1)}, bf16[32,3584]{1,0:T(8,128)(2,1)S(1)}, u32[]{:S(2)}, u32[]{:S(2)}) collective-permute-start(bf16[32,3584]{1,0:T(8,128)(2,1)S(1)} %get-tuple-element.19), channel_id=1, source_target_pairs={{0,3},{1,0},{2,1},{3,2},{4,7},{5,4},{6,5},{7,6},{8,11},{9,8},{10,9... | collective-permute-start | bytes 688136 | tf_op jit(solution)/shard_map/ppermute | solution.py:132
  27.1 1.8 %collective-permute-start.1 = (bf16[32,3584]{1,0:T(8,128)(2,1)S(1)}, bf16[32,3584]{1,0:T(8,128)(2,1)S(1)}, u32[]{:S(2)}, u32[]{:S(2)}) collective-permute-start(bf16[32,3584]{1,0:T(8,128)(2,1)S(1)} %get-tuple-element.20), channel_id=1, source_target_pairs={{0,2},{1,3},{2,0},{3,1},{4,6},{5,7},{6,4},{7,5},{8,10},{9,11},{10,... | collective-permute-start | bytes 688136 | tf_op jit(solution)/shard_map/ppermute | solution.py:132
  28.9 3.7 %collective-permute-done = bf16[32,3584]{1,0:T(8,128)(2,1)S(1)} collective-permute-done((bf16[32,3584]{1,0:T(8,128)(2,1)S(1)}, bf16[32,3584]{1,0:T(8,128)(2,1)S(1)}, u32[]{:S(2)}, u32[]{:S(2)}) %collective-permute-start) | collective-permute-done | bytes 229408 | tf_op jit(solution)/shard_map/ppermute | solution.py:132
  32.6 4.3 %collective-permute-done.2 = bf16[32,3584]{1,0:T(8,128)(2,1)S(1)} collective-permute-done((bf16[32,3584]{1,0:T(8,128)(2,1)S(1)}, bf16[32,3584]{1,0:T(8,128)(2,1)S(1)}, u32[]{:S(2)}, u32[]{:S(2)}) %collective-permute-start.2) | collective-permute-done | bytes 229408 | tf_op jit(solution)/shard_map/ppermute | solution.py:132
  36.9 1.8 %collective-permute-done.1 = bf16[32,3584]{1,0:T(8,128)(2,1)S(1)} collective-permute-done((bf16[32,3584]{1,0:T(8,128)(2,1)S(1)}, bf16[32,3584]{1,0:T(8,128)(2,1)S(1)}, u32[]{:S(2)}, u32[]{:S(2)}) %collective-permute-start.1) | collective-permute-done | bytes 229408 | tf_op jit(solution)/shard_map/ppermute | solution.py:132
  38.7 1.2 fusion.11
  40.0 0.8 fusion.13
  40.8 0.1 select_reduce_fusion.4
  40.9 0.1 reduce_sum.121
  41.2 0.1 eq.180
  41.4 0.2 fusion.41
  41.7 0.8 convolution_convert_fusion.1
  42.6 3.3 %all-to-all-start.1 = ((bf16[4,8,896]{2,1,0:T(8,128)(2,1)}), bf16[4,8,896]{2,1,0:T(8,128)(2,1)S(1)}, u32[]{:S(2)}, u32[]{:S(2)}) async-start(bf16[4,8,896]{2,1,0:T(8,128)(2,1)} %bitcast.20), calls=%async_computation.1 | async-start | bytes 114688 | tf_op jit(solution)/shard_map/all_to_all | solution.py:151
  46.0 5.4 %all-to-all-done.1 = bf16[4,8,896]{2,1,0:T(8,128)(2,1)S(1)} async-done(((bf16[4,8,896]{2,1,0:T(8,128)(2,1)}), bf16[4,8,896]{2,1,0:T(8,128)(2,1)S(1)}, u32[]{:S(2)}, u32[]{:S(2)}) %all-to-all-start.1) | async-done | bytes 57376 | tf_op jit(solution)/shard_map/all_to_all | solution.py:151
  51.4 0.2 convolution_convert_fusion.3
  51.6 1.1 broadcast_select_fusion
  52.7 7.5 %all-to-all-start.2 = ((bf16[32,16,896]{2,1,0:T(8,128)(2,1)}), bf16[32,16,896]{2,1,0:T(8,128)(2,1)S(1)}, u32[]{:S(2)}, u32[]{:S(2)}) async-start(bf16[32,16,896]{2,1,0:T(8,128)(2,1)} %broadcast_select_fusion), calls=%async_computation.2 | async-start | bytes 1835008 | tf_op jit(solution)/shard_map/all_to_all | solution.py:170
  60.2 39.4 %all-gather.2.cloned.1.call-done = bf16[1024,3584]{1,0:T(8,128)(2,1)} async-done(((bf16[32,3584]{1,0:T(8,128)(2,1)}), bf16[1024,3584]{1,0:T(8,128)(2,1)}) %all-gather.2.cloned.1.call-update) | async-done | bytes 7340048 | tf_op jit(solution)/shard_map/all_gather | solution.py:177
  99.7 13.4 %fusion.53 = (f32[1024]{0:T(1024)S(1)}, f32[1024,1000]{0,1:T(8,128)}) fusion(bf16[1024,3584]{1,0:T(8,128)(2,1)} %all-gather.2.cloned.1.call-done, bf16[1000,3584]{1,0:T(8,128)(2,1)} %param.25), kind=kOutput, calls=%fused_computation.123 | convolution fusion | flops 7341054976 | bytes 18608128 | tf_op jit(solution)/shard_map/dot_general | solution.py:183
  113.2 2.8 %exponential_reduce_fusion = (f32[1024]{0:T(1024)S(1)}, f32[1024]{0:T(1024)S(1)}) fusion(f32[1024,1000]{0,1:T(8,128)} %get-tuple-element.26, f32[1024]{0:T(1024)S(1)} %get-tuple-element.25, s32[1024]{0:T(1024)S(1)} %eq.192, s32[1000]{0:T(1024)S(1)} %iota_add_fusion), kind=kLoop, calls=%fused_computation.3 | loop fusion | flops 5117952 | bytes 4116384 | tf_op jit(solution)/shard_map/reduce_sum | solution.py:47
  116.3 0.5 select_reduce_fusion.1
  116.8 0.2 copy.37
  117.1 0.3 reshape_reshape.3
  117.4 0.9 copy.47
  118.3 7.9 %all-to-all-start = ((f32[128,8,128]{2,1,0:T(8,128)}), f32[128,8,128]{2,1,0:T(8,128)S(1)}, u32[]{:S(2)}, u32[]{:S(2)}) async-start(f32[128,8,128]{2,1,0:T(8,128)} %bitcast.30), calls=%async_computation | async-start | bytes 1048576 | tf_op jit(solution)/shard_map/all_to_all | solution.py:219
  126.3 0.3 convolution_convert_fusion.2
  126.6 0.6 copy.45
  127.2 12.1 %all-to-all-done = f32[128,8,128]{2,1,0:T(8,128)S(1)} async-done(((f32[128,8,128]{2,1,0:T(8,128)}), f32[128,8,128]{2,1,0:T(8,128)S(1)}, u32[]{:S(2)}, u32[]{:S(2)}) %all-to-all-start) | async-done | bytes 524320 | tf_op jit(solution)/shard_map/all_to_all | solution.py:219
  139.5 0.3 reshape.293
  139.8 0.2 copy.38
  140.0 0.1 select_reduce_fusion.3
  140.3 0.6 sub.82
  (56 shorter events, 1.7 us)
Async XLA Ops:
  7.2 10.9 %copy-start = (bf16[2,64,896]{2,1,0:T(8,128)(2,1)S(1)}, bf16[2,64,896]{2,1,0:T(8,128)(2,1)}, u32[]{:S(2)}) copy-start(bf16[2,64,896]{2,1,0:T(8,128)(2,1)} %param.17) | copy-start | bytes 688132
  7.2 4.9 %copy-start.2 = (bf16[2,64,896]{2,1,0:T(8,128)(2,1)S(1)}, bf16[2,64,896]{2,1,0:T(8,128)(2,1)}, u32[]{:S(2)}) copy-start(bf16[2,64,896]{2,1,0:T(8,128)(2,1)} %param.16) | copy-start | bytes 688132
  7.2 92.5 %all-gather.2.cloned.1.call-start = ((), (), s32[]{:S(2)}) async-start(), calls=%async_computation.3 | async-start | bytes 7569408 | tf_op jit(solution)/shard_map/all_gather | solution.py:177
  12.5 4.2 %copy-start.1 = (bf16[2,1024,896]{2,1,0:T(8,128)(2,1)S(1)}, bf16[2,1024,896]{2,1,0:T(8,128)(2,1)}, u32[]{:S(2)}) copy-start(bf16[2,1024,896]{2,1,0:T(8,128)(2,1)} %param.19) | copy-start | bytes 11010052
  22.7 17.3 %copy-start.4 = (f32[3584]{0:T(1024)S(1)}, f32[3584]{0:T(1024)}, u32[]{:S(2)}) copy-start(f32[3584]{0:T(1024)} %param.24) | copy-start | bytes 43012
  22.7 18.1 %copy-start.6 = (s32[64]{0:T(128)S(1)}, s32[64]{0:T(128)}, u32[]{:S(2)}) copy-start(s32[64]{0:T(128)} %param.27) | copy-start | bytes 772
  22.7 18.3 %copy-start.3 = (s32[64,64]{1,0:T(8,128)S(1)}, s32[64,64]{1,0:T(8,128)}, u32[]{:S(2)}) copy-start(s32[64,64]{1,0:T(8,128)} %param.26) | copy-start | bytes 49156
  22.7 19.0 %copy-start.5 = (s32[2,8,64]{2,1,0:T(8,128)S(1)}, s32[2,8,64]{2,1,0:T(8,128)}, u32[]{:S(2)}) copy-start(s32[2,8,64]{2,1,0:T(8,128)} %param.22) | copy-start | bytes 12292
  22.8 9.8 %collective-permute-start = (bf16[32,3584]{1,0:T(8,128)(2,1)S(1)}, bf16[32,3584]{1,0:T(8,128)(2,1)S(1)}, u32[]{:S(2)}, u32[]{:S(2)}) collective-permute-start(bf16[32,3584]{1,0:T(8,128)(2,1)S(1)} %get-tuple-element.18), channel_id=1, source_target_pairs={{0,1},{1,2},{2,3},{3,0},{4,5},{5,6},{6,7},{7,4},{8,9},{9,10},{10,1... | collective-permute-start | bytes 688136 | tf_op jit(solution)/shard_map/ppermute | solution.py:132
  24.9 12.0 %collective-permute-start.2 = (bf16[32,3584]{1,0:T(8,128)(2,1)S(1)}, bf16[32,3584]{1,0:T(8,128)(2,1)S(1)}, u32[]{:S(2)}, u32[]{:S(2)}) collective-permute-start(bf16[32,3584]{1,0:T(8,128)(2,1)S(1)} %get-tuple-element.19), channel_id=1, source_target_pairs={{0,3},{1,0},{2,1},{3,2},{4,7},{5,4},{6,5},{7,6},{8,11},{9,8},{10,9... | collective-permute-start | bytes 688136 | tf_op jit(solution)/shard_map/ppermute | solution.py:132
  27.1 11.6 %collective-permute-start.1 = (bf16[32,3584]{1,0:T(8,128)(2,1)S(1)}, bf16[32,3584]{1,0:T(8,128)(2,1)S(1)}, u32[]{:S(2)}, u32[]{:S(2)}) collective-permute-start(bf16[32,3584]{1,0:T(8,128)(2,1)S(1)} %get-tuple-element.20), channel_id=1, source_target_pairs={{0,2},{1,3},{2,0},{3,1},{4,6},{5,7},{6,4},{7,5},{8,10},{9,11},{10,... | collective-permute-start | bytes 688136 | tf_op jit(solution)/shard_map/ppermute | solution.py:132
  42.6 8.8 %all-to-all-start.1 = ((bf16[4,8,896]{2,1,0:T(8,128)(2,1)}), bf16[4,8,896]{2,1,0:T(8,128)(2,1)S(1)}, u32[]{:S(2)}, u32[]{:S(2)}) async-start(bf16[4,8,896]{2,1,0:T(8,128)(2,1)} %bitcast.20), calls=%async_computation.1 | async-start | bytes 114688 | tf_op jit(solution)/shard_map/all_to_all | solution.py:151
  52.7 65.6 %all-to-all-start.2 = ((bf16[32,16,896]{2,1,0:T(8,128)(2,1)}), bf16[32,16,896]{2,1,0:T(8,128)(2,1)S(1)}, u32[]{:S(2)}, u32[]{:S(2)}) async-start(bf16[32,16,896]{2,1,0:T(8,128)(2,1)} %broadcast_select_fusion), calls=%async_computation.2 | async-start | bytes 1835008 | tf_op jit(solution)/shard_map/all_to_all | solution.py:170
  118.3 21.1 %all-to-all-start = ((f32[128,8,128]{2,1,0:T(8,128)}), f32[128,8,128]{2,1,0:T(8,128)S(1)}, u32[]{:S(2)}, u32[]{:S(2)}) async-start(f32[128,8,128]{2,1,0:T(8,128)} %bitcast.30), calls=%async_computation | async-start | bytes 1048576 | tf_op jit(solution)/shard_map/all_to_all | solution.py:219
Sparse Core Ops, SparseCore 0:
  40.9 58.6 all-gather.1

commit v14 on v12

--- a/solution.py
+++ b/solution.py
@@ -180,9 +180,16 @@
         candidate.reshape(n_req, rows_all), tp_id * quarter, quarter, 1
     ).reshape(-1)
     vocab_ids = req_id * vocab_loc + jnp.arange(vocab_loc, dtype=jnp.int32)
-    logits = lax.dot_general(
-        all_rows, head_weight, (((1,), (1,)), ((), ())), preferred_element_type=jnp.float32
-    )
+    split_at = (vocab_loc // 2) // 16 * 16
+    part_stats = []
+    for lo, hi in ((0, split_at), (split_at, vocab_loc)):
+        part_logits = lax.dot_general(
+            all_rows,
+            head_weight[lo:hi],
+            (((1,), (1,)), ((), ())),
+            preferred_element_type=jnp.float32,
+        )
+        part_stats.append(vocab_stats(part_logits, vocab_ids[lo:hi], wanted_rows, 1))
     serving_all = jnp.sum(
         jnp.where(dealing[None, :] == slot_ids[:, None], slot_ids[None, :], 0), axis=1
     )
@@ -197,7 +204,7 @@
         compact_in.reshape(n_slots, acc_rows, dslice),
         preferred_element_type=jnp.float32,
     ).astype(jnp.bfloat16)
-    row_max, row_sum, picked = vocab_stats(logits, vocab_ids, wanted_rows, 1)
+    row_max, row_sum, picked = combine_stats(part_stats[0], part_stats[1])
     local_stats = jnp.stack([row_max, row_sum, picked]).reshape(3, n_req, quarter)
     local_stats = local_stats.transpose(1, 0, 2)
     dest_blocks = (serving_all // slots).reshape(n_req, 1, slots)

time: 146 us -> 143 us (0.979)
  matrix products: 26.9 us -> 23.9 us
  local copies, waits for them, and re-layouts: 4.38 us -> 6.27 us
  other arithmetic: 10.4 us -> 8.59 us
    dot_general x1, matrix products: 3.95 us -> 1.13 us  [local(): jnp.dot(attention_rows, out_weight, preferred_element_type=jnp.float32)]
    ppermute x3, waiting for transfers between devices: 9.83 us -> 12 us  [local(): lax.ppermute(outbound, 'tp', [(t, (t + shift) % n_tp) for t in range(n_tp)])]
    all_gather x1, waiting for transfers between devices: 40 us -> 38.1 us  [local(): all_rows = lax.all_gather(normed, 'req', axis=0, tiled=True)]
    reduce_sum x1 -> x2, other arithmetic: 2.84 us -> 0.99 us  [vocab_stats(): jnp.sum(jnp.exp(logits - jnp.expand_dims(row_max, along)), axis=along)]
    unnamed x15 -> x21, local copies, waits for them, and re-layouts: 0.66 us -> 2.3 us
    dot_general x1 -> x2, matrix products: 13.4 us -> 13.3 us  [local(): lax.dot_general(all_rows, head_weight[lo:hi], (((1,), (1,)), ((), ())), p...]
  transfers between devices with their start and end apart: 7 -> 7, of which waited for: 6 -> 6; matrix products, arithmetic and copies ran while one was open for 15% -> 14% of each run, Pallas kernels for 0% -> 0%
where the time goes in v14:
time: 143 us; the launch traced here: 141 us
  waiting for transfers between devices  63.6 us (44%)
  starting transfers between devices  24.1 us (17%)
  matrix products  23.9 us (17%)
  between operations  14.6 us (10%)
  other arithmetic  8.59 us (6%)
  local copies, waits for them, and re-layouts  6.27 us (4%)
    all_gather x1, waiting for transfers between devices, local(): all_rows = lax.all_gather(normed, 'req', axis=0, tiled=True)  38.1 us
    dot_general x2, matrix products, local(): lax.dot_general(all_rows, head_weight[lo:hi], (((1,), (1,)), ((), ())), p...  13.3 us
    ppermute x3, waiting for transfers between devices, local(): lax.ppermute(outbound, 'tp', [(t, (t + shift) % n_tp) for t in range(n_tp)])  12 us
    all_to_all x1, waiting for transfers between devices, local(): lax.all_to_all(outgoing.reshape(n_req * n_tp, slots * 3 * quarter), ('req...  8.28 us
    all_to_all x1, starting transfers between devices, local(): lax.all_to_all(outgoing.reshape(n_req * n_tp, slots * 3 * quarter), ('req...  7.87 us
    all_to_all x1, starting transfers between devices, local(): lax.all_to_all(compact_out.reshape(n_req, slots * acc_rows, dslice), 'req...  7.47 us
    ppermute x3, starting transfers between devices, local(): lax.ppermute(outbound, 'tp', [(t, (t + shift) % n_tp) for t in range(n_tp)])  5.48 us
    all_to_all x1, waiting for transfers between devices, local(): lax.all_to_all(picked_parts, 'tp', split_axis=0, concat_axis=0, tiled=True)  5.29 us
  transfers between devices with their start and end apart: 7, of which 6 were waited for; matrix products, arithmetic and copies ran while one was open for 14% of the time, Pallas kernels for 0%

profile of v14, /device:TPU:0, one launch (start us, length us, event | category | flops | bytes accessed | tf_op | source)
XLA Modules:
  0.0 141.2 jit_solution(14124139915078655105)
XLA Ops:
  7.3 0.7 iota_compare_fusion.7
  8.0 1.0 fusion.29
  9.0 0.9 fusion.30
  9.9 0.2 fusion.60
  10.1 0.2 fusion.59
  10.3 0.2 fusion.61
  10.7 0.2 reshape.379
  10.9 1.1 bitcast_select_fusion
  12.0 3.6 %fusion.4 = (f32[2,256]{1,0:T(2,128)S(1)}, f32[2,256,1024]{2,1,0:T(8,128)S(1)}) fusion(pred[2,1024]{1,0:T(4,128)(4,1)S(1)} %iota_compare_fusion.7, bf16[2,256,896]{2,1,0:T(8,128)(2,1)S(1)} %bitcast_select_fusion, bf16[2,1024,896]{2,1,0:T(8,128)(2,1)} %param.18), kind=kOutput, calls=%fused_computation.13 | convolution fusion | flops 941096448 | bytes 6688768 | tf_op jit(solution)/shard_map/rnd,rkd->rnk/dot_general | solution.py:84
  15.6 0.4 fusion.56
  16.1 0.6 fusion.5
  16.7 1.3 fusion.8
  18.1 0.5 add_divide_fusion
  18.6 0.1 select_reduce_fusion.3
  18.7 1.6 %slice-done.1 = s8[4194304]{0:T(1024)(128)(4,1)S(1)} async-done(((s8[6422528]{0:T(1024)(128)(4,1)}), s8[4194304]{0:T(1024)(128)(4,1)S(1)}, s32[]{:S(2)}) %slice-start.1) | async-done | bytes 4194328
  20.3 1.1 convolution_convert_fusion
  21.6 4.2 %collective-permute-start.2 = (bf16[32,3584]{1,0:T(8,128)(2,1)S(1)}, bf16[32,3584]{1,0:T(8,128)(2,1)S(1)}, u32[]{:S(2)}, u32[]{:S(2)}) collective-permute-start(bf16[32,3584]{1,0:T(8,128)(2,1)S(1)} %get-tuple-element.23), channel_id=1, source_target_pairs={{0,3},{1,0},{2,1},{3,2},{4,7},{5,4},{6,5},{7,6},{8,11},{9,8},{10,9... | collective-permute-start | bytes 688136 | tf_op jit(solution)/shard_map/ppermute | solution.py:132
  25.8 1.3 collective-permute-start
  27.1 8.5 %collective-permute-done.2 = bf16[32,3584]{1,0:T(8,128)(2,1)S(1)} collective-permute-done((bf16[32,3584]{1,0:T(8,128)(2,1)S(1)}, bf16[32,3584]{1,0:T(8,128)(2,1)S(1)}, u32[]{:S(2)}, u32[]{:S(2)}) %collective-permute-start.2) | collective-permute-done | bytes 229408 | tf_op jit(solution)/shard_map/ppermute | solution.py:132
  35.6 0.2 collective-permute-done.1
  35.8 3.2 %collective-permute-done = bf16[32,3584]{1,0:T(8,128)(2,1)S(1)} collective-permute-done((bf16[32,3584]{1,0:T(8,128)(2,1)S(1)}, bf16[32,3584]{1,0:T(8,128)(2,1)S(1)}, u32[]{:S(2)}, u32[]{:S(2)}) %collective-permute-start) | collective-permute-done | bytes 229408 | tf_op jit(solution)/shard_map/ppermute | solution.py:132
  39.0 1.2 fusion.15
  40.3 0.9 fusion.17
  41.5 0.1 eq.193
  41.8 0.2 fusion.45
  42.3 0.8 convolution_convert_fusion.1
  43.1 3.3 %all-to-all-start.1 = ((bf16[4,8,896]{2,1,0:T(8,128)(2,1)}), bf16[4,8,896]{2,1,0:T(8,128)(2,1)S(1)}, u32[]{:S(2)}, u32[]{:S(2)}) async-start(bf16[4,8,896]{2,1,0:T(8,128)(2,1)} %bitcast.20), calls=%async_computation.1 | async-start | bytes 114688 | tf_op jit(solution)/shard_map/all_to_all | solution.py:151
  46.6 5.3 %all-to-all-done.1 = bf16[4,8,896]{2,1,0:T(8,128)(2,1)S(1)} async-done(((bf16[4,8,896]{2,1,0:T(8,128)(2,1)}), bf16[4,8,896]{2,1,0:T(8,128)(2,1)S(1)}, u32[]{:S(2)}, u32[]{:S(2)}) %all-to-all-start.1) | async-done | bytes 57376 | tf_op jit(solution)/shard_map/all_to_all | solution.py:151
  51.9 0.2 convolution_convert_fusion.3
  52.1 1.1 broadcast_select_fusion
  53.2 7.5 %all-to-all-start.2 = ((bf16[32,16,896]{2,1,0:T(8,128)(2,1)}), bf16[32,16,896]{2,1,0:T(8,128)(2,1)S(1)}, u32[]{:S(2)}, u32[]{:S(2)}) async-start(bf16[32,16,896]{2,1,0:T(8,128)(2,1)} %broadcast_select_fusion), calls=%async_computation.2 | async-start | bytes 1835008 | tf_op jit(solution)/shard_map/all_to_all | solution.py:170
  60.7 38.1 %all-gather.2.cloned.1.call-done = bf16[1024,3584]{1,0:T(8,128)(2,1)} async-done(((bf16[32,3584]{1,0:T(8,128)(2,1)}), bf16[1024,3584]{1,0:T(8,128)(2,1)}) %all-gather.2.cloned.1.call-update) | async-done | bytes 7340048 | tf_op jit(solution)/shard_map/all_gather | solution.py:177
  98.8 7.4 %fusion.57 = (f32[1024]{0:T(1024)S(1)}, f32[1024,496]{0,1:T(8,128)S(1)}) fusion(bf16[1024,3584]{1,0:T(8,128)(2,1)} %all-gather.2.cloned.1.call-done, bf16[1000,3584]{1,0:T(8,128)(2,1)} %param.25), kind=kOutput, calls=%fused_computation.128 | convolution fusion | flops 3641162752 | bytes 12931072 | tf_op jit(solution)/shard_map/dot_general | solution.py:186
  106.2 6.0 %fusion.58 = (f32[1024]{0:T(1024)S(1)}, f32[1024,504]{0,1:T(8,128)S(1)}) fusion(bf16[1024,3584]{1,0:T(8,128)(2,1)S(1)} %copy-done.7, bf16[1000,3584]{1,0:T(8,128)(2,1)} %param.25), kind=kOutput, calls=%fused_computation.129 | convolution fusion | flops 3699891200 | bytes 13021184 | tf_op jit(solution)/shard_map/dot_general | solution.py:186
  112.2 0.5 exponential_reduce_fusion.1
  112.8 0.5 exponential_reduce_fusion
  113.7 0.5 select_reduce_fusion
  114.2 0.2 copy.38
  114.5 1.0 all_to_all.16
  115.5 7.9 %all-to-all-start = ((f32[128,1,192]{2,1,0:T(1,128)}), f32[128,1,192]{2,1,0:T(1,128)S(1)}, u32[]{:S(2)}, u32[]{:S(2)}) async-start(f32[128,1,192]{2,1,0:T(1,128)} %all_to_all.16), calls=%async_computation | async-start | bytes 262144 | tf_op jit(solution)/shard_map/all_to_all | solution.py:221
  123.4 0.3 convolution_convert_fusion.2
  123.7 0.6 copy.47
  124.3 8.3 %all-to-all-done = f32[128,1,192]{2,1,0:T(1,128)S(1)} async-done(((f32[128,1,192]{2,1,0:T(1,128)}), f32[128,1,192]{2,1,0:T(1,128)S(1)}, u32[]{:S(2)}, u32[]{:S(2)}) %all-to-all-start) | async-done | bytes 98336 | tf_op jit(solution)/shard_map/all_to_all | solution.py:221
  132.6 0.3 reduce.2
  132.9 0.3 reshape.383
  133.2 0.2 copy.40
  133.5 0.1 select_reduce_fusion.4
  133.7 0.6 sub.116
  (68 shorter events, 2.0 us)
Async XLA Ops:
  7.2 10.9 %copy-start = (bf16[2,64,896]{2,1,0:T(8,128)(2,1)S(1)}, bf16[2,64,896]{2,1,0:T(8,128)(2,1)}, u32[]{:S(2)}) copy-start(bf16[2,64,896]{2,1,0:T(8,128)(2,1)} %param.17) | copy-start | bytes 688132
  7.2 91.6 %all-gather.2.cloned.1.call-start = ((), (), s32[]{:S(2)}) async-start(), calls=%async_computation.3 | async-start | bytes 7569408 | tf_op jit(solution)/shard_map/all_gather | solution.py:177
  12.0 3.6 %copy-start.2 = (bf16[2,64,896]{2,1,0:T(8,128)(2,1)S(1)}, bf16[2,64,896]{2,1,0:T(8,128)(2,1)}, u32[]{:S(2)}) copy-start(bf16[2,64,896]{2,1,0:T(8,128)(2,1)} %param.16) | copy-start | bytes 688132
  12.0 4.6 %copy-start.1 = (bf16[2,1024,896]{2,1,0:T(8,128)(2,1)S(1)}, bf16[2,1024,896]{2,1,0:T(8,128)(2,1)}, u32[]{:S(2)}) copy-start(bf16[2,1024,896]{2,1,0:T(8,128)(2,1)} %param.19) | copy-start | bytes 11010052
  16.7 2.0 %slice-start = ((s8[6422528]{0:T(1024)(128)(4,1)}), s8[2228224]{0:T(1024)(128)(4,1)S(1)}, s32[]{:S(2)}) async-start(s8[6422528]{0:T(1024)(128)(4,1)} %bitcast.79), calls=%async_computation.4 | async-start | bytes 4456448
  18.1 2.2 %slice-start.1 = ((s8[6422528]{0:T(1024)(128)(4,1)}), s8[4194304]{0:T(1024)(128)(4,1)S(1)}, s32[]{:S(2)}) async-start(s8[6422528]{0:T(1024)(128)(4,1)} %bitcast.79), calls=%async_computation.5 | async-start | bytes 8388608
  21.5 18.8 %copy-start.4 = (f32[3584]{0:T(1024)S(1)}, f32[3584]{0:T(1024)}, u32[]{:S(2)}) copy-start(f32[3584]{0:T(1024)} %param.24) | copy-start | bytes 43012
  21.5 19.7 %copy-start.3 = (s32[64,64]{1,0:T(8,128)S(1)}, s32[64,64]{1,0:T(8,128)}, u32[]{:S(2)}) copy-start(s32[64,64]{1,0:T(8,128)} %param.26) | copy-start | bytes 49156
  21.5 19.8 %copy-start.6 = (s32[64]{0:T(128)S(1)}, s32[64]{0:T(128)}, u32[]{:S(2)}) copy-start(s32[64]{0:T(128)} %param.27) | copy-start | bytes 772
  21.5 20.8 %copy-start.5 = (s32[2,8,64]{2,1,0:T(8,128)S(1)}, s32[2,8,64]{2,1,0:T(8,128)}, u32[]{:S(2)}) copy-start(s32[2,8,64]{2,1,0:T(8,128)} %param.22) | copy-start | bytes 12292
  21.6 14.0 %collective-permute-start.2 = (bf16[32,3584]{1,0:T(8,128)(2,1)S(1)}, bf16[32,3584]{1,0:T(8,128)(2,1)S(1)}, u32[]{:S(2)}, u32[]{:S(2)}) collective-permute-start(bf16[32,3584]{1,0:T(8,128)(2,1)S(1)} %get-tuple-element.23), channel_id=1, source_target_pairs={{0,3},{1,0},{2,1},{3,2},{4,7},{5,4},{6,5},{7,6},{8,11},{9,8},{10,9... | collective-permute-start | bytes 688136 | tf_op jit(solution)/shard_map/ppermute | solution.py:132
  25.8 10.0 %collective-permute-start.1 = (bf16[32,3584]{1,0:T(8,128)(2,1)S(1)}, bf16[32,3584]{1,0:T(8,128)(2,1)S(1)}, u32[]{:S(2)}, u32[]{:S(2)}) collective-permute-start(bf16[32,3584]{1,0:T(8,128)(2,1)S(1)} %get-tuple-element.24), channel_id=1, source_target_pairs={{0,2},{1,3},{2,0},{3,1},{4,6},{5,7},{6,4},{7,5},{8,10},{9,11},{10,... | collective-permute-start | bytes 688136 | tf_op jit(solution)/shard_map/ppermute | solution.py:132
  25.8 13.2 %collective-permute-start = (bf16[32,3584]{1,0:T(8,128)(2,1)S(1)}, bf16[32,3584]{1,0:T(8,128)(2,1)S(1)}, u32[]{:S(2)}, u32[]{:S(2)}) collective-permute-start(bf16[32,3584]{1,0:T(8,128)(2,1)S(1)} %get-tuple-element.22), channel_id=1, source_target_pairs={{0,1},{1,2},{2,3},{3,0},{4,5},{5,6},{6,7},{7,4},{8,9},{9,10},{10,1... | collective-permute-start | bytes 688136 | tf_op jit(solution)/shard_map/ppermute | solution.py:132
  43.1 8.8 %all-to-all-start.1 = ((bf16[4,8,896]{2,1,0:T(8,128)(2,1)}), bf16[4,8,896]{2,1,0:T(8,128)(2,1)S(1)}, u32[]{:S(2)}, u32[]{:S(2)}) async-start(bf16[4,8,896]{2,1,0:T(8,128)(2,1)} %bitcast.20), calls=%async_computation.1 | async-start | bytes 114688 | tf_op jit(solution)/shard_map/all_to_all | solution.py:151
  53.2 62.3 %all-to-all-start.2 = ((bf16[32,16,896]{2,1,0:T(8,128)(2,1)}), bf16[32,16,896]{2,1,0:T(8,128)(2,1)S(1)}, u32[]{:S(2)}, u32[]{:S(2)}) async-start(bf16[32,16,896]{2,1,0:T(8,128)(2,1)} %broadcast_select_fusion), calls=%async_computation.2 | async-start | bytes 1835008 | tf_op jit(solution)/shard_map/all_to_all | solution.py:170
  98.8 7.4 %copy-start.7 = (bf16[1024,3584]{1,0:T(8,128)(2,1)S(1)}, bf16[1024,3584]{1,0:T(8,128)(2,1)}, u32[]{:S(2)}) copy-start(bf16[1024,3584]{1,0:T(8,128)(2,1)} %all-gather.2.cloned.1.call-done) | copy-start | bytes 22020100
  115.5 17.1 %all-to-all-start = ((f32[128,1,192]{2,1,0:T(1,128)}), f32[128,1,192]{2,1,0:T(1,128)S(1)}, u32[]{:S(2)}, u32[]{:S(2)}) async-start(f32[128,1,192]{2,1,0:T(1,128)} %all_to_all.16), calls=%async_computation | async-start | bytes 262144 | tf_op jit(solution)/shard_map/all_to_all | solution.py:221
Sparse Core Ops, SparseCore 0:
  41.3 57.4 all-gather.1

commit v15 on v14

--- a/solution.py
+++ b/solution.py
@@ -180,9 +180,9 @@
         candidate.reshape(n_req, rows_all), tp_id * quarter, quarter, 1
     ).reshape(-1)
     vocab_ids = req_id * vocab_loc + jnp.arange(vocab_loc, dtype=jnp.int32)
-    split_at = (vocab_loc // 2) // 16 * 16
+    bounds = [min(vocab_loc, k * 256) for k in range(-(-vocab_loc // 256))] + [vocab_loc]
     part_stats = []
-    for lo, hi in ((0, split_at), (split_at, vocab_loc)):
+    for lo, hi in zip(bounds[:-1], bounds[1:]):
         part_logits = lax.dot_general(
             all_rows,
             head_weight[lo:hi],
@@ -204,7 +204,9 @@
         compact_in.reshape(n_slots, acc_rows, dslice),
         preferred_element_type=jnp.float32,
     ).astype(jnp.bfloat16)
-    row_max, row_sum, picked = combine_stats(part_stats[0], part_stats[1])
+    row_max, row_sum, picked = part_stats[0]
+    for more in part_stats[1:]:
+        row_max, row_sum, picked = combine_stats((row_max, row_sum, picked), more)
     local_stats = jnp.stack([row_max, row_sum, picked]).reshape(3, n_req, quarter)
     local_stats = local_stats.transpose(1, 0, 2)
     dest_blocks = (serving_all // slots).reshape(n_req, 1, slots)

time: 143 us -> 156 us (1.091)
  matrix products: 23.9 us -> 37.1 us
    dot_general x2 -> x4, matrix products: 13.3 us -> 23.6 us  [local(): lax.dot_general(all_rows, head_weight[lo:hi], (((1,), (1,)), ((), ())), p...]
    dot_general x1, matrix products: 1.13 us -> 3.99 us  [local(): jnp.dot(attention_rows, out_weight, preferred_element_type=jnp.float32)]
    ppermute x3, waiting for transfers between devices: 12 us -> 9.83 us  [local(): lax.ppermute(outbound, 'tp', [(t, (t + shift) % n_tp) for t in range(n_tp)])]
    all_gather x1, waiting for transfers between devices: 38.1 us -> 40 us  [local(): all_rows = lax.all_gather(normed, 'req', axis=0, tiled=True)]
    unnamed x21 -> x15, local copies, waits for them, and re-layouts: 2.3 us -> 0.66 us
  transfers between devices with their start and end apart: 7 -> 7, of which waited for: 6 -> 6; matrix products, arithmetic and copies ran while one was open for 14% -> 20% of each run, Pallas kernels for 0% -> 0%
where the time goes in v15:
time: 156 us; the launch traced here: 155 us
  waiting for transfers between devices  63.5 us (41%)
  matrix products  37.1 us (24%)
  starting transfers between devices  24.8 us (16%)
  between operations  14.6 us (9%)
  other arithmetic  9.91 us (6%)
  local copies, waits for them, and re-layouts  4.81 us (3%)
    all_gather x1, waiting for transfers between devices, local(): all_rows = lax.all_gather(normed, 'req', axis=0, tiled=True)  40 us
    dot_general x4, matrix products, local(): lax.dot_general(all_rows, head_weight[lo:hi], (((1,), (1,)), ((), ())), p...  23.6 us
    ppermute x3, waiting for transfers between devices, local(): lax.ppermute(outbound, 'tp', [(t, (t + shift) % n_tp) for t in range(n_tp)])  9.83 us
    all_to_all x1, waiting for transfers between devices, local(): lax.all_to_all(outgoing.reshape(n_req * n_tp, slots * 3 * quarter), ('req...  8.28 us
    all_to_all x1, starting transfers between devices, local(): lax.all_to_all(outgoing.reshape(n_req * n_tp, slots * 3 * quarter), ('req...  7.87 us
    all_to_all x1, starting transfers between devices, local(): lax.all_to_all(compact_out.reshape(n_req, slots * acc_rows, dslice), 'req...  7.49 us
    ppermute x3, starting transfers between devices, local(): lax.ppermute(outbound, 'tp', [(t, (t + shift) % n_tp) for t in range(n_tp)])  6.08 us
    all_to_all x1, waiting for transfers between devices, local(): lax.all_to_all(picked_parts, 'tp', split_axis=0, concat_axis=0, tiled=True)  5.36 us
  transfers between devices with their start and end apart: 7, of which 6 were waited for; matrix products, arithmetic and copies ran while one was open for 20% of the time, Pallas kernels for 0%

profile of v15, /device:TPU:0, one launch (start us, length us, event | category | flops | bytes accessed | tf_op | source)
XLA Modules:
  0.0 154.6 jit_solution(5515791811783284403)
XLA Ops:
  7.3 0.8 iota_compare_fusion.7
  8.1 1.0 fusion.33
  9.1 0.2 fusion.68
  9.3 0.9 fusion.34
  10.1 0.2 fusion.67
  10.4 0.2 fusion.69
  10.7 0.2 reshape.509
  11.0 1.1 bitcast_select_fusion
  12.1 0.4 fusion.62
  12.5 3.6 %fusion = (f32[2,256]{1,0:T(2,128)S(1)}, f32[2,256,1024]{2,1,0:T(8,128)S(1)}) fusion(pred[2,1024]{1,0:T(4,128)(4,1)S(1)} %iota_compare_fusion.7, bf16[2,256,896]{2,1,0:T(8,128)(2,1)S(1)} %bitcast_select_fusion, bf16[2,1024,896]{2,1,0:T(8,128)(2,1)} %param.18), kind=kOutput, calls=%fused_computation.5 | convolution fusion | flops 941096448 | bytes 6688768 | tf_op jit(solution)/shard_map/rnd,rkd->rnk/dot_general | solution.py:84
  16.1 0.6 fusion.9
  16.7 1.3 fusion.12
  18.1 0.5 add_divide_fusion
  18.7 4.0 %convolution_convert_fusion = bf16[128,3584]{1,0:T(8,128)(2,1)S(1)} fusion(bf16[128,896]{1,0:T(8,128)(2,1)S(1)} %bitcast.80, bf16[896,3584]{1,0:T(8,128)(2,1)} %param.23), kind=kOutput, calls=%fused_computation | convolution fusion | flops 822542336 | bytes 7569408 | tf_op jit(solution)/shard_map/dot_general | solution.py:125
  22.8 2.1 %collective-permute-start = (bf16[32,3584]{1,0:T(8,128)(2,1)S(1)}, bf16[32,3584]{1,0:T(8,128)(2,1)S(1)}, u32[]{:S(2)}, u32[]{:S(2)}) collective-permute-start(bf16[32,3584]{1,0:T(8,128)(2,1)S(1)} %get-tuple-element.30), channel_id=1, source_target_pairs={{0,1},{1,2},{2,3},{3,0},{4,5},{5,6},{6,7},{7,4},{8,9},{9,10},{10,1... | collective-permute-start | bytes 688136 | tf_op jit(solution)/shard_map/ppermute | solution.py:132
  24.9 2.2 %collective-permute-start.2 = (bf16[32,3584]{1,0:T(8,128)(2,1)S(1)}, bf16[32,3584]{1,0:T(8,128)(2,1)S(1)}, u32[]{:S(2)}, u32[]{:S(2)}) collective-permute-start(bf16[32,3584]{1,0:T(8,128)(2,1)S(1)} %get-tuple-element.31), channel_id=1, source_target_pairs={{0,3},{1,0},{2,1},{3,2},{4,7},{5,4},{6,5},{7,6},{8,11},{9,8},{10,9... | collective-permute-start | bytes 688136 | tf_op jit(solution)/shard_map/ppermute | solution.py:132
  27.1 1.8 %collective-permute-start.1 = (bf16[32,3584]{1,0:T(8,128)(2,1)S(1)}, bf16[32,3584]{1,0:T(8,128)(2,1)S(1)}, u32[]{:S(2)}, u32[]{:S(2)}) collective-permute-start(bf16[32,3584]{1,0:T(8,128)(2,1)S(1)} %get-tuple-element.32), channel_id=1, source_target_pairs={{0,2},{1,3},{2,0},{3,1},{4,6},{5,7},{6,4},{7,5},{8,10},{9,11},{10,... | collective-permute-start | bytes 688136 | tf_op jit(solution)/shard_map/ppermute | solution.py:132
  28.9 3.7 %collective-permute-done = bf16[32,3584]{1,0:T(8,128)(2,1)S(1)} collective-permute-done((bf16[32,3584]{1,0:T(8,128)(2,1)S(1)}, bf16[32,3584]{1,0:T(8,128)(2,1)S(1)}, u32[]{:S(2)}, u32[]{:S(2)}) %collective-permute-start) | collective-permute-done | bytes 229408 | tf_op jit(solution)/shard_map/ppermute | solution.py:132
  32.6 4.3 %collective-permute-done.2 = bf16[32,3584]{1,0:T(8,128)(2,1)S(1)} collective-permute-done((bf16[32,3584]{1,0:T(8,128)(2,1)S(1)}, bf16[32,3584]{1,0:T(8,128)(2,1)S(1)}, u32[]{:S(2)}, u32[]{:S(2)}) %collective-permute-start.2) | collective-permute-done | bytes 229408 | tf_op jit(solution)/shard_map/ppermute | solution.py:132
  36.9 1.8 %collective-permute-done.1 = bf16[32,3584]{1,0:T(8,128)(2,1)S(1)} collective-permute-done((bf16[32,3584]{1,0:T(8,128)(2,1)S(1)}, bf16[32,3584]{1,0:T(8,128)(2,1)S(1)}, u32[]{:S(2)}, u32[]{:S(2)}) %collective-permute-start.1) | collective-permute-done | bytes 229408 | tf_op jit(solution)/shard_map/ppermute | solution.py:132
  38.7 1.2 fusion.19
  40.0 0.8 fusion.21
  41.5 0.2 fusion.49
  41.9 0.8 convolution_convert_fusion.1
  42.8 3.3 %all-to-all-start.1 = ((bf16[4,8,896]{2,1,0:T(8,128)(2,1)}), bf16[4,8,896]{2,1,0:T(8,128)(2,1)S(1)}, u32[]{:S(2)}, u32[]{:S(2)}) async-start(bf16[4,8,896]{2,1,0:T(8,128)(2,1)} %bitcast.20), calls=%async_computation.1 | async-start | bytes 114688 | tf_op jit(solution)/shard_map/all_to_all | solution.py:151
  46.2 5.4 %all-to-all-done.1 = bf16[4,8,896]{2,1,0:T(8,128)(2,1)S(1)} async-done(((bf16[4,8,896]{2,1,0:T(8,128)(2,1)}), bf16[4,8,896]{2,1,0:T(8,128)(2,1)S(1)}, u32[]{:S(2)}, u32[]{:S(2)}) %all-to-all-start.1) | async-done | bytes 57376 | tf_op jit(solution)/shard_map/all_to_all | solution.py:151
  51.6 0.2 convolution_convert_fusion.3
  51.8 1.2 broadcast_select_fusion
  53.0 7.5 %all-to-all-start.2 = ((bf16[32,16,896]{2,1,0:T(8,128)(2,1)}), bf16[32,16,896]{2,1,0:T(8,128)(2,1)S(1)}, u32[]{:S(2)}, u32[]{:S(2)}) async-start(bf16[32,16,896]{2,1,0:T(8,128)(2,1)} %broadcast_select_fusion), calls=%async_computation.2 | async-start | bytes 1835008 | tf_op jit(solution)/shard_map/all_to_all | solution.py:170
  60.5 40.0 %all-gather.2.cloned.1.call-done = bf16[1024,3584]{1,0:T(8,128)(2,1)} async-done(((bf16[32,3584]{1,0:T(8,128)(2,1)}), bf16[1024,3584]{1,0:T(8,128)(2,1)}) %all-gather.2.cloned.1.call-update) | async-done | bytes 7340048 | tf_op jit(solution)/shard_map/all_gather | solution.py:177
  100.4 5.6 %fusion.63 = (f32[1024]{0:T(1024)S(1)}, f32[1024,232]{0,1:T(8,128)S(1)}) fusion(bf16[1024,3584]{1,0:T(8,128)(2,1)} %all-gather.2.cloned.1.call-done, bf16[1000,3584]{1,0:T(8,128)(2,1)} %param.25), kind=kOutput, calls=%fused_computation.139 | convolution fusion | flops 1703123968 | bytes 9957376 | tf_op jit(solution)/shard_map/dot_general | solution.py:186
  106.1 0.2 exponential_reduce_fusion.3
  106.4 5.7 %fusion.65 = (f32[1024]{0:T(1024)S(1)}, f32[1024,256]{0,1:T(8,128)S(1)}) fusion(bf16[1024,3584]{1,0:T(8,128)(2,1)} %all-gather.2.cloned.1.call-done, bf16[1000,3584]{1,0:T(8,128)(2,1)} %param.25), kind=kOutput, calls=%fused_computation.141 | convolution fusion | flops 1879309312 | bytes 10227712 | tf_op jit(solution)/shard_map/dot_general | solution.py:186
  112.2 5.7 %fusion.66 = (f32[1024]{0:T(1024)S(1)}, f32[1024,256]{0,1:T(8,128)S(1)}) fusion(bf16[1024,3584]{1,0:T(8,128)(2,1)} %all-gather.2.cloned.1.call-done, bf16[1000,3584]{1,0:T(8,128)(2,1)} %param.25), kind=kOutput, calls=%fused_computation.142 | convolution fusion | flops 1879309312 | bytes 10227712 | tf_op jit(solution)/shard_map/dot_general | solution.py:186
  118.0 6.7 %fusion.64 = (f32[1024]{0:T(1024)S(1)}, f32[1024,256]{0,1:T(8,128)}) fusion(bf16[1024,3584]{1,0:T(8,128)(2,1)} %all-gather.2.cloned.1.call-done, bf16[1000,3584]{1,0:T(8,128)(2,1)} %param.25), kind=kOutput, calls=%fused_computation.140 | convolution fusion | flops 1879309312 | bytes 10227712 | tf_op jit(solution)/shard_map/dot_general | solution.py:186
  124.7 2.0 %exponential_reduce_fusion.1 = (f32[1024]{0:T(1024)S(1)}, f32[1024]{0:T(1024)S(1)}, f32[1024]{0:T(1024)S(1)}, f32[1024]{0:T(1024)S(1)}, f32[1024]{0:T(1024)S(1)}, /*index=5*/f32[1024]{0:T(1024)S(1)}) fusion(f32[1024,256]{0,1:T(8,128)} %get-tuple-element.47, f32[1024]{0:T(1024)S(1)} %get-tuple-element.46, s32[1024]{0:T(1024)S(1)} %eq.227, ...), kind=kLoop, calls=%fused_computation.27 | loop fusion | flops 3926016 | bytes 3189760 | tf_op jit(solution)/shard_map/reduce_sum | solution.py:47
  127.1 0.5 select_reduce_fusion
  127.7 0.2 copy.50
  127.9 1.0 all_to_all.16
  129.0 7.9 %all-to-all-start = ((f32[128,1,192]{2,1,0:T(1,128)}), f32[128,1,192]{2,1,0:T(1,128)S(1)}, u32[]{:S(2)}, u32[]{:S(2)}) async-start(f32[128,1,192]{2,1,0:T(1,128)} %all_to_all.16), calls=%async_computation | async-start | bytes 262144 | tf_op jit(solution)/shard_map/all_to_all | solution.py:223
  136.8 0.3 convolution_convert_fusion.2
  137.1 0.6 copy.59
  137.8 8.3 %all-to-all-done = f32[128,1,192]{2,1,0:T(1,128)S(1)} async-done(((f32[128,1,192]{2,1,0:T(1,128)}), f32[128,1,192]{2,1,0:T(1,128)S(1)}, u32[]{:S(2)}, u32[]{:S(2)}) %all-to-all-start) | async-done | bytes 98336 | tf_op jit(solution)/shard_map/all_to_all | solution.py:223
  146.0 0.3 reduce.2
  146.4 0.3 reshape.513
  146.6 0.2 copy.52
  146.9 0.1 select_reduce_fusion.6
  147.1 0.6 sub.184
  (69 shorter events, 2.5 us)
Async XLA Ops:
  7.2 10.9 %copy-start = (bf16[2,64,896]{2,1,0:T(8,128)(2,1)S(1)}, bf16[2,64,896]{2,1,0:T(8,128)(2,1)}, u32[]{:S(2)}) copy-start(bf16[2,64,896]{2,1,0:T(8,128)(2,1)} %param.17) | copy-start | bytes 688132
  7.2 4.9 %copy-start.2 = (bf16[2,64,896]{2,1,0:T(8,128)(2,1)S(1)}, bf16[2,64,896]{2,1,0:T(8,128)(2,1)}, u32[]{:S(2)}) copy-start(bf16[2,64,896]{2,1,0:T(8,128)(2,1)} %param.16) | copy-start | bytes 688132
  7.2 93.2 %all-gather.2.cloned.1.call-start = ((), (), s32[]{:S(2)}) async-start(), calls=%async_computation.3 | async-start | bytes 7569408 | tf_op jit(solution)/shard_map/all_gather | solution.py:177
  12.5 4.2 %copy-start.1 = (bf16[2,1024,896]{2,1,0:T(8,128)(2,1)S(1)}, bf16[2,1024,896]{2,1,0:T(8,128)(2,1)}, u32[]{:S(2)}) copy-start(bf16[2,1024,896]{2,1,0:T(8,128)(2,1)} %param.19) | copy-start | bytes 11010052
  22.7 17.3 %copy-start.4 = (f32[3584]{0:T(1024)S(1)}, f32[3584]{0:T(1024)}, u32[]{:S(2)}) copy-start(f32[3584]{0:T(1024)} %param.24) | copy-start | bytes 43012
  22.7 18.1 %copy-start.6 = (s32[64]{0:T(128)S(1)}, s32[64]{0:T(128)}, u32[]{:S(2)}) copy-start(s32[64]{0:T(128)} %param.27) | copy-start | bytes 772
  22.7 18.3 %copy-start.3 = (s32[64,64]{1,0:T(8,128)S(1)}, s32[64,64]{1,0:T(8,128)}, u32[]{:S(2)}) copy-start(s32[64,64]{1,0:T(8,128)} %param.26) | copy-start | bytes 49156
  22.7 19.2 %copy-start.5 = (s32[2,8,64]{2,1,0:T(8,128)S(1)}, s32[2,8,64]{2,1,0:T(8,128)}, u32[]{:S(2)}) copy-start(s32[2,8,64]{2,1,0:T(8,128)} %param.22) | copy-start | bytes 12292
  22.8 9.8 %collective-permute-start = (bf16[32,3584]{1,0:T(8,128)(2,1)S(1)}, bf16[32,3584]{1,0:T(8,128)(2,1)S(1)}, u32[]{:S(2)}, u32[]{:S(2)}) collective-permute-start(bf16[32,3584]{1,0:T(8,128)(2,1)S(1)} %get-tuple-element.30), channel_id=1, source_target_pairs={{0,1},{1,2},{2,3},{3,0},{4,5},{5,6},{6,7},{7,4},{8,9},{9,10},{10,1... | collective-permute-start | bytes 688136 | tf_op jit(solution)/shard_map/ppermute | solution.py:132
  24.9 12.0 %collective-permute-start.2 = (bf16[32,3584]{1,0:T(8,128)(2,1)S(1)}, bf16[32,3584]{1,0:T(8,128)(2,1)S(1)}, u32[]{:S(2)}, u32[]{:S(2)}) collective-permute-start(bf16[32,3584]{1,0:T(8,128)(2,1)S(1)} %get-tuple-element.31), channel_id=1, source_target_pairs={{0,3},{1,0},{2,1},{3,2},{4,7},{5,4},{6,5},{7,6},{8,11},{9,8},{10,9... | collective-permute-start | bytes 688136 | tf_op jit(solution)/shard_map/ppermute | solution.py:132
  27.1 11.6 %collective-permute-start.1 = (bf16[32,3584]{1,0:T(8,128)(2,1)S(1)}, bf16[32,3584]{1,0:T(8,128)(2,1)S(1)}, u32[]{:S(2)}, u32[]{:S(2)}) collective-permute-start(bf16[32,3584]{1,0:T(8,128)(2,1)S(1)} %get-tuple-element.32), channel_id=1, source_target_pairs={{0,2},{1,3},{2,0},{3,1},{4,6},{5,7},{6,4},{7,5},{8,10},{9,11},{10,... | collective-permute-start | bytes 688136 | tf_op jit(solution)/shard_map/ppermute | solution.py:132
  42.8 8.8 %all-to-all-start.1 = ((bf16[4,8,896]{2,1,0:T(8,128)(2,1)}), bf16[4,8,896]{2,1,0:T(8,128)(2,1)S(1)}, u32[]{:S(2)}, u32[]{:S(2)}) async-start(bf16[4,8,896]{2,1,0:T(8,128)(2,1)} %bitcast.20), calls=%async_computation.1 | async-start | bytes 114688 | tf_op jit(solution)/shard_map/all_to_all | solution.py:151
  53.0 76.0 %all-to-all-start.2 = ((bf16[32,16,896]{2,1,0:T(8,128)(2,1)}), bf16[32,16,896]{2,1,0:T(8,128)(2,1)S(1)}, u32[]{:S(2)}, u32[]{:S(2)}) async-start(bf16[32,16,896]{2,1,0:T(8,128)(2,1)} %broadcast_select_fusion), calls=%async_computation.2 | async-start | bytes 1835008 | tf_op jit(solution)/shard_map/all_to_all | solution.py:170
  129.0 17.1 %all-to-all-start = ((f32[128,1,192]{2,1,0:T(1,128)}), f32[128,1,192]{2,1,0:T(1,128)S(1)}, u32[]{:S(2)}, u32[]{:S(2)}) async-start(f32[128,1,192]{2,1,0:T(1,128)} %all_to_all.16), calls=%async_computation | async-start | bytes 262144 | tf_op jit(solution)/shard_map/all_to_all | solution.py:223
Sparse Core Ops, SparseCore 0:
  40.9 59.4 all-gather.1
